TPU v7x, 512 devices: a whole 4x4x16 slice. The times are simulated.
512 devices in a mesh: expert: 8 (over y, core), mp: 64 (over x, z).
Axes of the slice: x: 4, y: 4, z: 16, core: 2. Of those that a mesh axis runs over, the one named last changes fastest.
Arguments:
- context: bfloat16 [4096, 2048], P('expert', 'mp'), may hold values from -6 to 6
- out_proj: bfloat16 [2048, 2048], P('mp'), may hold values from -1 to 1, as said below
- routes: int32 [4096, 2], P('expert'), may hold values from 0 to 7, all different within a row; in each aligned block of 512 rows (0 to 511, 512 to 1023, ...) at most 256 rows name the same one
- router_logits: float32 [4096, 2], P('expert'), may hold values from -8 to 8
- w_gate: bfloat16 [45056, 2048], P('mp', 'expert'), may hold values from -0.125 to 0.125
- w_up: bfloat16 [45056, 2048], P('mp', 'expert'), may hold values from -0.125 to 0.125
- w_down: bfloat16 [45056, 2048], P('mp', 'expert'), may hold values from -0.078125 to 0.078125
- norm_gain: float32 [2048], P('mp'), may hold values from 0.25 to 1.75
- request_order: int32 [4096], P('expert'), may hold values from 0 to 4095, each once
Outputs:
- restored: bfloat16 [4096, 2048], P('expert', 'mp')
Inputs may be any that keep to these rules, and one draw needn't show every extreme that they name: `routes`: each row names 2 different experts. Within each aligned block of 512 rows no expert is named by more than 256 rows, and in some blocks one expert is named by exactly 256 rows. `request_order`: A permutation of the 4096 token rows. `out_proj`: entries of the order of one over the square root of 2048.
All inputs are finite; a program needn't handle non-finite values.
Results may differ from a plain program's by a relative error of at most 0.0056.
Values may be sent and summed in bfloat16 or wider, within the bound.
No kernel may reach another device: no remote copies, remote signals or barrier semaphores. Data moves between devices by JAX's collectives and lax.ppermute only.
A program may use at most 64 MiB of HBM per device.

v0:
```python
import jax
import jax.numpy as jnp
from jax import lax
from jax.sharding import PartitionSpec as P

EXPERTS = 8
CAP = 256


epsilon = 1e-06


def slot_targets(routes, capacity, experts):
    flat_routes = routes.reshape(-1)
    onehot = (flat_routes[:, None] == jnp.arange(experts, dtype=jnp.int32)[None, :]).astype(
        jnp.int32
    )
    earlier = jnp.cumsum(onehot, axis=0) - onehot
    slot_index = jnp.sum(earlier * onehot, axis=1)
    return flat_routes * capacity + slot_index


def shards(
    context, out_proj, routes, router_logits, w_gate, w_up, w_down, norm_gain, request_order
):
    tok_rows = context.shape[0]
    feat_local = context.shape[1]
    model_width = out_proj.shape[1]
    mp_count = lax.axis_size("mp")
    copies = mp_count // EXPERTS
    capacity = CAP
    top_k = routes.shape[1]
    attended = jnp.einsum(
        "td,cd->tc",
        lax.all_gather(context, "mp", axis=1, tiled=True),
        out_proj,
        preferred_element_type=jnp.float32,
    ).astype(jnp.bfloat16)
    destination = slot_targets(routes, capacity, EXPERTS)
    source_rows = jnp.repeat(jnp.arange(tok_rows, dtype=jnp.int32), top_k)
    slotted = (
        jnp.zeros((EXPERTS * capacity, feat_local), jnp.bfloat16)
        .at[destination]
        .set(attended[source_rows])
    )
    slotted = jnp.repeat(slotted.reshape(EXPERTS, capacity, feat_local), copies, axis=0)
    outgoing = slotted.transpose(1, 0, 2).reshape(capacity, mp_count * feat_local)
    inbox_rows = lax.all_to_all(outgoing, "mp", split_axis=1, concat_axis=1, tiled=True)
    gate_next = jnp.einsum(
        "rd,hd->rh",
        inbox_rows,
        lax.all_gather(w_gate, "expert", axis=1, tiled=True),
        preferred_element_type=jnp.float32,
    )
    up_next = jnp.einsum(
        "rd,hd->rh",
        inbox_rows,
        lax.all_gather(w_up, "expert", axis=1, tiled=True),
        preferred_element_type=jnp.float32,
    )
    activated = (jax.nn.silu(gate_next) * up_next).astype(jnp.bfloat16)
    partial_value = jnp.dot(
        activated,
        lax.all_gather(w_down, "expert", axis=1, tiled=True),
        preferred_element_type=jnp.float32,
    )
    returned = lax.all_to_all(partial_value, "mp", split_axis=1, concat_axis=0, tiled=True)
    expert_out = jnp.sum(returned.reshape(EXPERTS, copies, capacity, feat_local), axis=1).reshape(
        EXPERTS * capacity, feat_local
    )
    picked = expert_out[destination].reshape(tok_rows, top_k, feat_local)
    weights = 1.0 / (1.0 + jnp.exp(router_logits[:, ::-1] - router_logits))
    branch = jnp.sum(picked * weights[:, :, None], axis=1)
    combined = attended.astype(jnp.float32) + branch
    squares = lax.psum(jnp.sum(combined * combined, axis=1), "mp")
    normed = (
        combined * norm_gain[None, :] * lax.rsqrt(squares / model_width + epsilon)[:, None]
    ).astype(jnp.bfloat16)
    everyone = lax.all_gather(normed, "expert", axis=0, tiled=True)
    return everyone[request_order]


def solution(mesh):
    placed = (
        P("expert", "mp"),
        P("mp", None),
        P("expert", None),
        P("expert", None),
        P("mp", "expert"),
        P("mp", "expert"),
        P("mp", "expert"),
        P("mp"),
        P("expert"),
    )
    return jax.shard_map(
        shards, mesh=mesh, in_specs=placed, out_specs=P("expert", "mp"), check_vma=False
    )
```

profile of v0, /device:TPU:1, one launch (start us, length us, event | category | flops | bytes accessed | tf_op | source)
XLA Modules:
  0.0 565.7 jit_solution(14208333560372502879)
XLA Ops:
  6.5 0.0 copy-start
  6.5 0.7 all-gather.5.cloned.1.call-update
  7.3 0.0 all-gather.7.cloned.1.call-start
  7.3 0.7 all-gather.7.cloned.1.call-update
  8.0 0.0 all-gather.11.cloned.1.call-start
  8.1 0.7 all-gather.11.cloned.1.call-update
  8.7 0.0 all-gather.9.cloned.1.call-start
  8.8 0.5 all-gather.9.cloned.1.call-update
  9.3 0.8 copy.42
  10.2 0.2 eq.29
  10.3 0.2 eq.25
  10.5 0.7 broadcast_multiply_fusion
  11.2 2.3 reduce-window.6
  13.5 0.3 slice_reduce_fusion
  13.7 0.2 reduce-window.9
  13.9 0.1 add_bitcast_fusion
  14.0 0.2 copy.41
  14.1 0.2 mul.55
  14.4 0.2 reshape.104
  14.6 133.1 %all-gather.5.cloned.1.call-done = bf16[512,2048]{0,1:T(8,128)(2,1)} async-done(((bf16[512,32]{0,1:T(8,128)(2,1)}), bf16[512,2048]{0,1:T(8,128)(2,1)}) %all-gather.5.cloned.1.call-update) | async-done | bytes 2097168 | tf_op jit(solution)/shard_map/all_gather | solution.py:35
  147.7 2.0 convolution_convert_fusion
  149.7 0.1 copy.44
  149.9 6.4 %scatter_custom_fusion = bf16[2048,32]{1,0:T(8,128)(2,1)S(1)} fusion(s32[1024]{0:T(1024)S(1)} %bitcast.48, bf16[512,32]{1,0:T(8,128)(2,1)S(1)} %copy.44, s32[1024]{0:T(1024)S(1)} %broadcast_clamp_fusion.1, bf16[]{:T(256)} %constant.10.clone.1), kind=kCustom, calls=%fused_computation.16 | custom fusion | bytes 131074 | tf_op jit(solution)/shard_map/scatter | solution.py:44
  156.3 0.2 copy.46
  156.5 1.2 broadcast_in_dim.10
  157.7 8.8 %all-to-all-start = ((bf16[256,64,32]{0,2,1:T(8,128)(2,1)}), bf16[256,64,32]{0,2,1:T(8,128)(2,1)S(1)}, u32[]{:S(2)}, u32[]{:S(2)}) async-start(bf16[256,64,32]{0,2,1:T(8,128)(2,1)} %bitcast.6), calls=%async_computation | async-start | bytes 2097152 | tf_op jit(solution)/shard_map/all_to_all | solution.py:48
  166.5 26.9 %all-gather.7.cloned.1.call-done = bf16[704,2048]{1,0:T(8,128)(2,1)} async-done(((bf16[704,256]{1,0:T(8,128)(2,1)}), bf16[704,2048]{1,0:T(8,128)(2,1)}) %all-gather.7.cloned.1.call-update) | async-done | bytes 2883600 | tf_op jit(solution)/shard_map/all_gather | solution.py:52
  193.4 12.3 %all-to-all-done = bf16[256,64,32]{0,2,1:T(8,128)(2,1)S(1)} async-done(((bf16[256,64,32]{0,2,1:T(8,128)(2,1)}), bf16[256,64,32]{0,2,1:T(8,128)(2,1)S(1)}, u32[]{:S(2)}, u32[]{:S(2)}) %all-to-all-start) | async-done | bytes 1048608 | tf_op jit(solution)/shard_map/all_to_all | solution.py:48
  205.6 2.7 fusion.16
  208.4 26.4 %all-gather.11.cloned.1.call-done = bf16[704,2048]{1,0:T(8,128)(2,1)} async-done(((bf16[704,256]{1,0:T(8,128)(2,1)}), bf16[704,2048]{1,0:T(8,128)(2,1)}) %all-gather.11.cloned.1.call-update) | async-done | bytes 2883600 | tf_op jit(solution)/shard_map/all_gather | solution.py:64
  234.8 41.3 %all-gather.9.cloned.1.call-done = bf16[704,2048]{1,0:T(8,128)(2,1)} async-done(((bf16[704,256]{1,0:T(8,128)(2,1)}), bf16[704,2048]{1,0:T(8,128)(2,1)}) %all-gather.9.cloned.1.call-update) | async-done | bytes 2883600 | tf_op jit(solution)/shard_map/all_gather | solution.py:58
  276.1 7.2 %fusion.1 = f32[256,2048]{0,1:T(8,128)} fusion(bf16[704,2048]{1,0:T(8,128)(2,1)} %all-gather.11.cloned.1.call-done, bf16[704,2048]{1,0:T(8,128)(2,1)} %all-gather.9.cloned.1.call-done, bf16[256,2048]{0,1:T(8,128)(2,1)S(1)} %bitcast.46, f32[256,704]{0,1:T(8,128)S(1)} %fusion.16), kind=kOutput, calls=%fused_computation.8 | convolution fusion | flops 1477476352 | bytes 9633792 | tf_op jit(solution)/shard_map/dot_general | solution.py:62
  283.4 15.6 %all-to-all-start.1 = ((f32[256,64,32]{0,2,1:T(8,128)}), f32[256,64,32]{0,2,1:T(8,128)S(1)}, u32[]{:S(2)}, u32[]{:S(2)}) async-start(f32[256,64,32]{0,2,1:T(8,128)} %bitcast.43), calls=%async_computation.1 | async-start | bytes 4194304 | tf_op jit(solution)/shard_map/all_to_all | solution.py:67
  299.0 0.1 rev.3
  299.2 0.1 copy.49
  299.4 91.4 %all-to-all-done.1 = f32[256,64,32]{0,2,1:T(8,128)S(1)} async-done(((f32[256,64,32]{0,2,1:T(8,128)}), f32[256,64,32]{0,2,1:T(8,128)S(1)}, u32[]{:S(2)}, u32[]{:S(2)}) %all-to-all-start.1) | async-done | bytes 2097184 | tf_op jit(solution)/shard_map/all_to_all | solution.py:67
  390.8 0.2 bitcast_reduce_fusion
  390.9 0.3 copy.48
  391.3 0.0 copy-start.3
  391.3 2.8 gather_fusion
  394.1 2.8 multiply_reduce_fusion
  396.9 0.1 copy.50
  397.1 118.5 %psum.7 = f32[512]{0:T(512)S(1)} all-reduce(f32[512]{0:T(512)S(1)} %multiply_reduce_fusion.1), channel_id=1, replica_groups=mesh['expert'=8,'mp'=64] {'mp'}, use_global_device_ids=true, to_apply=%region_7.8 | all-reduce | flops 512 | bytes 4096 | tf_op jit(solution)/shard_map/psum | solution.py:75
  515.6 0.1 multiply_convert_fusion
  515.6 41.0 %all_gather.19 = bf16[4096,32]{0,1:T(8,128)(2,1)S(1)} all-gather(bf16[512,32]{0,1:T(8,128)(2,1)S(1)} %multiply_convert_fusion), channel_id=1, replica_groups=mesh['expert'=8,'mp'=64] {'expert'}, dimensions={0}, use_global_device_ids=true | all-gather | bytes 294912 | tf_op jit(solution)/shard_map/all_gather | solution.py:79
  556.6 0.5 copy.51
  557.1 1.3 gather_fusion.1
  558.4 0.7 copy.52
  (19 shorter events, 0.2 us)
Async XLA Ops:
  6.5 141.2 %copy-start = (bf16[32,2048]{1,0:T(8,128)(2,1)S(1)}, bf16[32,2048]{1,0:T(8,128)(2,1)}, u32[]{:S(2)}) copy-start(bf16[32,2048]{1,0:T(8,128)(2,1)} %param.10) | copy-start | bytes 393220
  6.5 141.2 %all-gather.5.cloned.1.call-start = ((), (), s32[]{:S(2)}) async-start(), calls=%async_computation.2 | async-start | bytes 2129920 | tf_op jit(solution)/shard_map/all_gather | solution.py:35
  7.3 186.1 %all-gather.7.cloned.1.call-start = ((), (), s32[]{:S(2)}) async-start(), calls=%async_computation.3 | async-start | bytes 3244032 | tf_op jit(solution)/shard_map/all_gather | solution.py:52
  8.0 226.8 %all-gather.11.cloned.1.call-start = ((), (), s32[]{:S(2)}) async-start(), calls=%async_computation.5 | async-start | bytes 3244032 | tf_op jit(solution)/shard_map/all_gather | solution.py:64
  8.7 267.4 %all-gather.9.cloned.1.call-start = ((), (), s32[]{:S(2)}) async-start(), calls=%async_computation.4 | async-start | bytes 3244032 | tf_op jit(solution)/shard_map/all_gather | solution.py:58
  157.7 48.0 %all-to-all-start = ((bf16[256,64,32]{0,2,1:T(8,128)(2,1)}), bf16[256,64,32]{0,2,1:T(8,128)(2,1)S(1)}, u32[]{:S(2)}, u32[]{:S(2)}) async-start(bf16[256,64,32]{0,2,1:T(8,128)(2,1)} %bitcast.6), calls=%async_computation | async-start | bytes 2097152 | tf_op jit(solution)/shard_map/all_to_all | solution.py:48
  283.4 15.7 %copy-start.1 = (f32[512,2]{0,1:T(2,128)S(1)}, f32[512,2]{0,1:T(2,128)}, u32[]{:S(2)}) copy-start(f32[512,2]{0,1:T(2,128)} %param.12) | copy-start | bytes 12292
  283.4 16.0 %copy-start.2 = (s32[512]{0:T(512)S(1)}, s32[512]{0:T(512)}, u32[]{:S(2)}) copy-start(s32[512]{0:T(512)} %param.17) | copy-start | bytes 6148
  283.4 107.4 %all-to-all-start.1 = ((f32[256,64,32]{0,2,1:T(8,128)}), f32[256,64,32]{0,2,1:T(8,128)S(1)}, u32[]{:S(2)}, u32[]{:S(2)}) async-start(f32[256,64,32]{0,2,1:T(8,128)} %bitcast.43), calls=%async_computation.1 | async-start | bytes 4194304 | tf_op jit(solution)/shard_map/all_to_all | solution.py:67
  391.3 124.3 %copy-start.3 = (f32[32]{0:T(128)S(1)}, f32[32]{0:T(128)}, u32[]{:S(2)}) copy-start(f32[32]{0:T(128)} %param.16) | copy-start | bytes 388
Sparse Core Ops, SparseCore 0:
  10.3 137.3 all-gather.4
  149.8 43.5 all-gather.6
  195.5 39.2 all-gather.10
  236.8 39.2 all-gather.8
where the time goes:
time: 566 us
  waiting for transfers between devices  334 us (59%)
  blocking collectives  159 us (28%)
  starting transfers between devices  24.5 us (4%)
  local copies, waits for them, and re-layouts  16 us (3%)
  between operations  13.4 us (2%)
  matrix products  12 us (2%)
  other arithmetic  6.35 us (1%)
    all_gather x1, waiting for transfers between devices, shards(): lax.all_gather(context, 'mp', axis=1, tiled=True)  133 us
    psum x1, blocking collectives, shards(): squares = lax.psum(jnp.sum(combined * combined, axis=1), 'mp')  118 us
    all_to_all x1, waiting for transfers between devices, shards(): lax.all_to_all(partial_value, 'mp', split_axis=1, concat_axis=0, tiled=True)  91.4 us
    all_gather x1, waiting for transfers between devices, shards(): lax.all_gather(w_up, 'expert', axis=1, tiled=True)  41.3 us
    all_gather x1, blocking collectives, shards(): everyone = lax.all_gather(normed, 'expert', axis=0, tiled=True)  41 us
    all_gather x1, waiting for transfers between devices, shards(): lax.all_gather(w_gate, 'expert', axis=1, tiled=True)  26.9 us
    all_gather x1, waiting for transfers between devices, shards(): lax.all_gather(w_down, 'expert', axis=1, tiled=True)  26.4 us
    all_to_all x1, starting transfers between devices, shards(): lax.all_to_all(partial_value, 'mp', split_axis=1, concat_axis=0, tiled=True)  15.6 us
  transfers between devices with their start and end apart: 6, of which 6 were waited for; matrix products, arithmetic and copies ran while one was open for 3% of the time, Pallas kernels for 0%

commit v1 on v0

v1 whole, which is shorter than its diff:
```python
import jax
import jax.numpy as jnp
from jax import lax
from jax.sharding import Mesh, PartitionSpec as P

EXPERTS = 8
CAP = 256


epsilon = 1e-06


def slot_targets(routes, capacity, experts):
    flat_routes = routes.reshape(-1)
    onehot = (flat_routes[:, None] == jnp.arange(experts, dtype=jnp.int32)[None, :]).astype(
        jnp.int32
    )
    earlier = jnp.cumsum(onehot, axis=0) - onehot
    slot_index = jnp.sum(earlier * onehot, axis=1)
    return flat_routes * capacity + slot_index


def shards(
    context, out_proj, routes, router_logits, w_gate, w_up, w_down, norm_gain, request_order
):
    tok_rows = context.shape[0]
    feat_local = context.shape[1]
    model_width = out_proj.shape[1]
    mp_count = lax.axis_size(MP)
    copies = mp_count // EXPERTS
    capacity = CAP
    top_k = routes.shape[1]
    gathered = lax.all_gather(
        lax.all_gather(context, "mz", axis=1, tiled=True), "mx", axis=1, tiled=True
    )
    attended = jnp.einsum(
        "td,cd->tc",
        gathered,
        out_proj,
        preferred_element_type=jnp.float32,
    ).astype(jnp.bfloat16)
    destination = slot_targets(routes, capacity, EXPERTS)
    source_rows = jnp.repeat(jnp.arange(tok_rows, dtype=jnp.int32), top_k)
    slotted = (
        jnp.zeros((EXPERTS * capacity, feat_local), jnp.bfloat16)
        .at[destination]
        .set(attended[source_rows])
    )
    slotted = jnp.repeat(slotted.reshape(EXPERTS, capacity, feat_local), copies, axis=0)
    outgoing = slotted.transpose(1, 0, 2).reshape(capacity, mp_count * feat_local)
    inbox_rows = lax.all_to_all(outgoing, MP, split_axis=1, concat_axis=1, tiled=True)
    gate_next = jnp.einsum(
        "rd,hd->rh",
        inbox_rows,
        lax.all_gather(w_gate, EX, axis=1, tiled=True),
        preferred_element_type=jnp.float32,
    )
    up_next = jnp.einsum(
        "rd,hd->rh",
        inbox_rows,
        lax.all_gather(w_up, EX, axis=1, tiled=True),
        preferred_element_type=jnp.float32,
    )
    activated = (jax.nn.silu(gate_next) * up_next).astype(jnp.bfloat16)
    partial_value = jnp.dot(
        activated,
        lax.all_gather(w_down, EX, axis=1, tiled=True),
        preferred_element_type=jnp.float32,
    )
    returned = lax.all_to_all(
        partial_value.astype(jnp.bfloat16), MP, split_axis=1, concat_axis=0, tiled=True
    )
    expert_out = jnp.sum(
        returned.reshape(EXPERTS, copies, capacity, feat_local).astype(jnp.float32), axis=1
    ).reshape(
        EXPERTS * capacity, feat_local
    )
    picked = expert_out[destination].reshape(tok_rows, top_k, feat_local)
    weights = 1.0 / (1.0 + jnp.exp(router_logits[:, ::-1] - router_logits))
    branch = jnp.sum(picked * weights[:, :, None], axis=1)
    combined = attended.astype(jnp.float32) + branch
    squares = lax.psum(lax.psum(jnp.sum(combined * combined, axis=1), "mz"), "mx")
    normed = (
        combined * norm_gain[None, :] * lax.rsqrt(squares / model_width + epsilon)[:, None]
    ).astype(jnp.bfloat16)
    everyone = lax.all_gather(normed, EX, axis=0, tiled=True)
    return everyone[request_order]


EX = ("ey", "ec")
MP = ("mx", "mz")


def split_mesh(mesh):
    devices = mesh.devices
    n_exp, n_mp = devices.shape
    row = devices[0].reshape(-1)
    try:
        z_count = len({d.coords[2] for d in row})
    except (AttributeError, IndexError, TypeError):
        z_count = n_mp
    return Mesh(
        devices.reshape(1, n_exp, n_mp // z_count, z_count), ("ey", "ec", "mx", "mz")
    )


def solution(mesh):
    fine = split_mesh(mesh)
    placed = (
        P(EX, MP),
        P(MP, None),
        P(EX, None),
        P(EX, None),
        P(MP, EX),
        P(MP, EX),
        P(MP, EX),
        P(MP),
        P(EX),
    )
    return jax.shard_map(
        shards, mesh=fine, in_specs=placed, out_specs=P(EX, MP), check_vma=False
    )
```

time: 566 us -> 352 us (0.62)
  waiting for transfers between devices: 334 us -> 184 us
  blocking collectives: 159 us -> 90.6 us
    all_gather x4, waiting for transfers between devices: 228 us -> 98 us  [the longest x1 41.3 us: shards(): lax.all_gather(w_up, EX, axis=1, tiled=True)]
    psum x1 -> x2, blocking collectives: 118 us -> 32.8 us  [the longest x1 23.3 us: shards(): lax.psum(jnp.sum(combined * combined, axis=1), 'mz')]
    all_to_all x2, waiting for transfers between devices: 104 us -> 83.8 us  [the longest x1 50.3 us: shards(): lax.all_to_all(partial_value.astype(jnp.bfloat16), MP, split_axis=1, conc...]
    all_gather x1 -> x2, blocking collectives: 41 us -> 57.8 us  [the longest x1 35 us: shards(): lax.all_gather(context, 'mz', axis=1, tiled=True)]
  transfers between devices with their start and end apart: 6 -> 6, of which waited for: 6 -> 6; matrix products, arithmetic and copies ran while one was open for 3% -> 5% of each run, Pallas kernels for 0% -> 0%
where the time goes in v1:
time: 352 us; the launch traced here: 351 us
  waiting for transfers between devices  184 us (52%)
  blocking collectives  90.6 us (26%)
  starting transfers between devices  29.7 us (8%)
  local copies, waits for them, and re-layouts  17.3 us (5%)
  between operations  13.4 us (4%)
  matrix products  10.9 us (3%)
  other arithmetic  5.68 us (2%)
    all_to_all x1, waiting for transfers between devices, shards(): lax.all_to_all(partial_value.astype(jnp.bfloat16), MP, split_axis=1, conc...  50.3 us
    all_gather x1, waiting for transfers between devices, shards(): lax.all_gather(w_up, EX, axis=1, tiled=True)  41.3 us
    all_gather x1, blocking collectives, shards(): lax.all_gather(context, 'mz', axis=1, tiled=True)  35 us
    all_gather x1, waiting for transfers between devices, shards(): lax.all_gather(lax.all_gather(context, 'mz', axis=1, tiled=True), 'mx', a...  34.9 us
    all_to_all x1, waiting for transfers between devices, shards(): lax.all_to_all(outgoing, MP, split_axis=1, concat_axis=1, tiled=True)  33.5 us
    psum x1, blocking collectives, shards(): lax.psum(jnp.sum(combined * combined, axis=1), 'mz')  23.3 us
    all_gather x1, blocking collectives, shards(): everyone = lax.all_gather(normed, EX, axis=0, tiled=True)  22.8 us
    all_gather x1, waiting for transfers between devices, shards(): lax.all_gather(w_gate, EX, axis=1, tiled=True)  16.8 us
  transfers between devices with their start and end apart: 6, of which 6 were waited for; matrix products, arithmetic and copies ran while one was open for 5% of the time, Pallas kernels for 0%

profile of v1, /device:TPU:1, one launch (start us, length us, event | category | flops | bytes accessed | tf_op | source)
XLA Modules:
  0.0 351.4 jit_solution(4756676370487490608)
XLA Ops:
  6.5 35.0 %all_gather.18 = bf16[512,512]{0,1:T(8,128)(2,1)} all-gather(bf16[512,32]{0,1:T(8,128)(2,1)} %param.9), channel_id=1, replica_groups=mesh['ey'=1,'ec'=8,'mx'=4,'mz'=16] {'mz'}, dimensions={1}, use_global_device_ids=true | all-gather | bytes 557056 | tf_op jit(solution)/shard_map/all_gather | solution.py:34
  41.5 0.0 all-gather.5.cloned.1.call-update
  41.5 0.0 all-gather.7.cloned.1.call-start
  41.6 0.7 all-gather.7.cloned.1.call-update
  42.3 0.0 all-gather.11.cloned.1.call-start
  42.3 0.7 all-gather.11.cloned.1.call-update
  43.0 0.0 all-gather.9.cloned.1.call-start
  43.1 0.5 all-gather.9.cloned.1.call-update
  43.6 0.8 copy.42
  44.4 0.2 eq.29
  44.6 0.2 eq.25
  44.8 2.3 reduce-window.6
  47.1 0.3 slice_reduce_fusion
  47.4 0.2 reduce-window.9
  47.5 0.1 add_bitcast_fusion
  47.6 0.2 copy.41
  47.8 0.2 mul.55
  48.0 0.2 reshape.104
  48.2 34.9 %all-gather.5.cloned.1.call-done = bf16[512,2048]{0,1:T(8,128)(2,1)} async-done(((bf16[512,512]{0,1:T(8,128)(2,1)}), bf16[512,2048]{0,1:T(8,128)(2,1)}) %all-gather.5.cloned.1.call-update) | async-done | bytes 2097168 | tf_op jit(solution)/shard_map/all_gather | solution.py:33
  83.1 2.0 convolution_convert_fusion.1
  85.1 0.1 copy.44
  85.3 6.4 %scatter_custom_fusion = bf16[2048,32]{1,0:T(8,128)(2,1)S(1)} fusion(s32[1024]{0:T(1024)S(1)} %bitcast.47, bf16[512,32]{1,0:T(8,128)(2,1)S(1)} %copy.44, s32[1024]{0:T(1024)S(1)} %broadcast_clamp_fusion.1, bf16[]{:T(256)} %constant.10.clone.1), kind=kCustom, calls=%fused_computation.11 | custom fusion | bytes 131074 | tf_op jit(solution)/shard_map/scatter | solution.py:47
  91.7 0.2 copy.46
  91.9 1.2 broadcast_in_dim.10
  93.1 14.1 %all-to-all-start = ((bf16[256,64,32]{0,2,1:T(8,128)(2,1)}), bf16[256,64,32]{0,2,1:T(8,128)(2,1)S(1)}, u32[]{:S(2)}, u32[]{:S(2)}) async-start(bf16[256,64,32]{0,2,1:T(8,128)(2,1)} %bitcast.6), calls=%async_computation | async-start | bytes 2097152 | tf_op jit(solution)/shard_map/all_to_all | solution.py:51
  107.2 16.8 %all-gather.7.cloned.1.call-done = bf16[704,2048]{1,0:T(8,128)(2,1)} async-done(((bf16[704,256]{1,0:T(8,128)(2,1)}), bf16[704,2048]{1,0:T(8,128)(2,1)}) %all-gather.7.cloned.1.call-update) | async-done | bytes 2883600 | tf_op jit(solution)/shard_map/all_gather | solution.py:55
  124.0 33.5 %all-to-all-done = bf16[256,64,32]{0,2,1:T(8,128)(2,1)S(1)} async-done(((bf16[256,64,32]{0,2,1:T(8,128)(2,1)}), bf16[256,64,32]{0,2,1:T(8,128)(2,1)S(1)}, u32[]{:S(2)}, u32[]{:S(2)}) %all-to-all-start) | async-done | bytes 1048608 | tf_op jit(solution)/shard_map/all_to_all | solution.py:51
  157.5 2.9 fusion.10
  160.4 5.0 %all-gather.11.cloned.1.call-done = bf16[704,2048]{1,0:T(8,128)(2,1)} async-done(((bf16[704,256]{1,0:T(8,128)(2,1)}), bf16[704,2048]{1,0:T(8,128)(2,1)}) %all-gather.11.cloned.1.call-update) | async-done | bytes 2883600 | tf_op jit(solution)/shard_map/all_gather | solution.py:67
  165.5 41.3 %all-gather.9.cloned.1.call-done = bf16[704,2048]{1,0:T(8,128)(2,1)} async-done(((bf16[704,256]{1,0:T(8,128)(2,1)}), bf16[704,2048]{1,0:T(8,128)(2,1)}) %all-gather.9.cloned.1.call-update) | async-done | bytes 2883600 | tf_op jit(solution)/shard_map/all_gather | solution.py:61
  206.8 6.0 %convolution_convert_fusion = bf16[256,2048]{1,0:T(8,128)(2,1)S(1)} fusion(bf16[704,2048]{1,0:T(8,128)(2,1)} %all-gather.11.cloned.1.call-done, bf16[704,2048]{1,0:T(8,128)(2,1)} %all-gather.9.cloned.1.call-done, bf16[256,2048]{0,1:T(8,128)(2,1)S(1)} %bitcast.45, f32[256,704]{0,1:T(8,128)S(1)} %fusion.10), kind=kOutput, calls=%fused_computation.4 | convolution fusion | flops 1478000640 | bytes 8585216 | tf_op jit(solution)/shard_map/dot_general | solution.py:65
  212.7 1.3 copy.47
  214.1 15.5 %all-to-all-start.1 = ((bf16[256,64,32]{0,2,1:T(8,128)(2,1)}), bf16[256,64,32]{0,2,1:T(8,128)(2,1)S(1)}, u32[]{:S(2)}, u32[]{:S(2)}) async-start(bf16[256,64,32]{0,2,1:T(8,128)(2,1)} %bitcast.8), calls=%async_computation.1 | async-start | bytes 2097152 | tf_op jit(solution)/shard_map/all_to_all | solution.py:70
  229.6 0.1 rev.3
  229.8 0.1 copy.49
  230.0 50.3 %all-to-all-done.1 = bf16[256,64,32]{0,2,1:T(8,128)(2,1)S(1)} async-done(((bf16[256,64,32]{0,2,1:T(8,128)(2,1)}), bf16[256,64,32]{0,2,1:T(8,128)(2,1)S(1)}, u32[]{:S(2)}, u32[]{:S(2)}) %all-to-all-start.1) | async-done | bytes 1048608 | tf_op jit(solution)/shard_map/all_to_all | solution.py:70
  280.3 0.2 bitcast_reduce_fusion
  280.4 0.3 copy.48
  280.8 2.8 gather_fusion
  283.6 2.8 multiply_reduce_fusion
  286.4 0.1 copy.50
  286.6 23.3 %psum.14 = f32[512]{0:T(512)S(1)} all-reduce(f32[512]{0:T(512)S(1)} %multiply_reduce_fusion.1), channel_id=1, replica_groups=mesh['ey'=1,'ec'=8,'mx'=4,'mz'=16] {'mz'}, use_global_device_ids=true, to_apply=%region_7.8 | all-reduce | flops 512 | bytes 4096 | tf_op jit(solution)/shard_map/psum | solution.py:82
  309.8 9.5 %psum.15 = f32[512]{0:T(512)S(1)} all-reduce(f32[512]{0:T(512)S(1)} %psum.14), channel_id=1, replica_groups=mesh['ey'=1,'ec'=8,'mx'=4,'mz'=16] {'mx'}, use_global_device_ids=true, to_apply=%region_8.9 | all-reduce | flops 512 | bytes 4096 | tf_op jit(solution)/shard_map/psum | solution.py:82
  319.4 0.1 multiply_convert_fusion
  319.4 22.8 %all_gather.23 = bf16[4096,32]{0,1:T(8,128)(2,1)S(1)} all-gather(bf16[512,32]{0,1:T(8,128)(2,1)S(1)} %multiply_convert_fusion), channel_id=1, replica_groups=mesh['ey'=1,'ec'=8,'mx'=4,'mz'=16] {'ey','ec'}, dimensions={0}, use_global_device_ids=true | all-gather | bytes 294912 | tf_op jit(solution)/shard_map/all_gather | solution.py:86
  342.3 0.5 copy.51
  342.8 1.3 gather_fusion.1
  344.1 0.7 copy.52
  (24 shorter events, 0.2 us)
Async XLA Ops:
  6.5 76.6 %copy-start = (bf16[32,2048]{1,0:T(8,128)(2,1)S(1)}, bf16[32,2048]{1,0:T(8,128)(2,1)}, u32[]{:S(2)}) copy-start(bf16[32,2048]{1,0:T(8,128)(2,1)} %param.10) | copy-start | bytes 393220
  6.5 38.2 %copy-start.1 = (s32[512,2]{0,1:T(2,128)S(1)}, s32[512,2]{0,1:T(2,128)}, u32[]{:S(2)}) copy-start(s32[512,2]{0,1:T(2,128)} %param.11) | copy-start | bytes 12292
  6.5 76.6 %all-gather.5.cloned.1.call-start = ((), (), s32[]{:S(2)}) async-start(), calls=%async_computation.2 | async-start | bytes 2621440 | tf_op jit(solution)/shard_map/all_gather | solution.py:33
  41.5 82.5 %all-gather.7.cloned.1.call-start = ((), (), s32[]{:S(2)}) async-start(), calls=%async_computation.3 | async-start | bytes 3244032 | tf_op jit(solution)/shard_map/all_gather | solution.py:55
  42.3 123.2 %all-gather.11.cloned.1.call-start = ((), (), s32[]{:S(2)}) async-start(), calls=%async_computation.5 | async-start | bytes 3244032 | tf_op jit(solution)/shard_map/all_gather | solution.py:67
  43.0 163.7 %all-gather.9.cloned.1.call-start = ((), (), s32[]{:S(2)}) async-start(), calls=%async_computation.4 | async-start | bytes 3244032 | tf_op jit(solution)/shard_map/all_gather | solution.py:61
  93.1 64.4 %all-to-all-start = ((bf16[256,64,32]{0,2,1:T(8,128)(2,1)}), bf16[256,64,32]{0,2,1:T(8,128)(2,1)S(1)}, u32[]{:S(2)}, u32[]{:S(2)}) async-start(bf16[256,64,32]{0,2,1:T(8,128)(2,1)} %bitcast.6), calls=%async_computation | async-start | bytes 2097152 | tf_op jit(solution)/shard_map/all_to_all | solution.py:51
  212.7 16.9 %copy-start.2 = (f32[512,2]{0,1:T(2,128)S(1)}, f32[512,2]{0,1:T(2,128)}, u32[]{:S(2)}) copy-start(f32[512,2]{0,1:T(2,128)} %param.12) | copy-start | bytes 12292
  212.7 17.2 %copy-start.3 = (s32[512]{0:T(512)S(1)}, s32[512]{0:T(512)}, u32[]{:S(2)}) copy-start(s32[512]{0:T(512)} %param.17) | copy-start | bytes 6148
  214.1 66.2 %all-to-all-start.1 = ((bf16[256,64,32]{0,2,1:T(8,128)(2,1)}), bf16[256,64,32]{0,2,1:T(8,128)(2,1)S(1)}, u32[]{:S(2)}, u32[]{:S(2)}) async-start(bf16[256,64,32]{0,2,1:T(8,128)(2,1)} %bitcast.8), calls=%async_computation.1 | async-start | bytes 2097152 | tf_op jit(solution)/shard_map/all_to_all | solution.py:70
  280.8 38.6 %copy-start.4 = (f32[32]{0:T(128)S(1)}, f32[32]{0:T(128)}, u32[]{:S(2)}) copy-start(f32[32]{0:T(128)} %param.16) | copy-start | bytes 388
Sparse Core Ops, SparseCore 0:
  41.7 41.3 all-gather.4
  85.2 38.7 all-gather.6
  126.1 39.2 all-gather.10
  167.4 39.2 all-gather.8

commit v2 on v1

--- a/solution.py
+++ b/solution.py
@@ -49,22 +49,23 @@
     slotted = jnp.repeat(slotted.reshape(EXPERTS, capacity, feat_local), copies, axis=0)
     outgoing = slotted.transpose(1, 0, 2).reshape(capacity, mp_count * feat_local)
     inbox_rows = lax.all_to_all(outgoing, MP, split_axis=1, concat_axis=1, tiled=True)
+    stacked = lax.all_gather(jnp.stack([w_gate, w_up, w_down]), EX, axis=2, tiled=True)
     gate_next = jnp.einsum(
         "rd,hd->rh",
         inbox_rows,
-        lax.all_gather(w_gate, EX, axis=1, tiled=True),
+        stacked[0],
         preferred_element_type=jnp.float32,
     )
     up_next = jnp.einsum(
         "rd,hd->rh",
         inbox_rows,
-        lax.all_gather(w_up, EX, axis=1, tiled=True),
+        stacked[1],
         preferred_element_type=jnp.float32,
     )
     activated = (jax.nn.silu(gate_next) * up_next).astype(jnp.bfloat16)
     partial_value = jnp.dot(
         activated,
-        lax.all_gather(w_down, EX, axis=1, tiled=True),
+        stacked[2],
         preferred_element_type=jnp.float32,
     )
     returned = lax.all_to_all(

time: 352 us -> 299 us (0.85)
  waiting for transfers between devices: 184 us -> 85.2 us
  blocking collectives: 90.6 us -> 155 us
  starting transfers between devices: 29.7 us -> 10.3 us
    all_to_all x0 -> x1, blocking collectives: none -> 64.2 us  [shards(): lax.all_to_all(outgoing, MP, split_axis=1, concat_axis=1, tiled=True)]
    all_gather x3 -> x1, waiting for transfers between devices: 63.2 us -> 0.01 us  [shards(): lax.all_gather(jnp.stack([w_gate, w_up, w_down]), EX, axis=2, tiled=True)]
    all_to_all x1 -> x0, waiting for transfers between devices: 33.5 us -> none  [shards(): lax.all_to_all(outgoing, MP, split_axis=1, concat_axis=1, tiled=True)]
    all_to_all x1 -> x0, starting transfers between devices: 14.1 us -> none  [shards(): lax.all_to_all(outgoing, MP, split_axis=1, concat_axis=1, tiled=True)]
    all_to_all x1, starting transfers between devices: 15.5 us -> 10.3 us  [shards(): lax.all_to_all(partial_value.astype(jnp.bfloat16), MP, split_axis=1, conc...]
  transfers between devices with their start and end apart: 6 -> 3, of which waited for: 6 -> 2; matrix products, arithmetic and copies ran while one was open for 5% -> 5% of each run, Pallas kernels for 0% -> 0%
where the time goes in v2:
time: 299 us
  blocking collectives  155 us (52%)
  waiting for transfers between devices  85.2 us (28%)
  local copies, waits for them, and re-layouts  15.5 us (5%)
  between operations  13.7 us (5%)
  matrix products  10.7 us (4%)
  starting transfers between devices  10.3 us (3%)
  other arithmetic  8 us (3%)
    all_to_all x1, blocking collectives, shards(): lax.all_to_all(outgoing, MP, split_axis=1, concat_axis=1, tiled=True)  64.2 us
    all_to_all x1, waiting for transfers between devices, shards(): lax.all_to_all(partial_value.astype(jnp.bfloat16), MP, split_axis=1, conc...  49.9 us
    all_gather x1, waiting for transfers between devices, shards(): lax.all_gather(lax.all_gather(context, 'mz', axis=1, tiled=True), 'mx', a...  35.2 us
    all_gather x1, blocking collectives, shards(): lax.all_gather(context, 'mz', axis=1, tiled=True)  35 us
    all_gather x1, blocking collectives, shards(): everyone = lax.all_gather(normed, EX, axis=0, tiled=True)  24.4 us
    psum x1, blocking collectives, shards(): lax.psum(jnp.sum(combined * combined, axis=1), 'mz')  23.4 us
    all_to_all x1, starting transfers between devices, shards(): lax.all_to_all(partial_value.astype(jnp.bfloat16), MP, split_axis=1, conc...  10.3 us
    psum x1, blocking collectives, shards(): lax.psum(lax.psum(jnp.sum(combined * combined, axis=1), 'mz'), 'mx')  8.45 us
  transfers between devices with their start and end apart: 3, of which 2 were waited for; matrix products, arithmetic and copies ran while one was open for 5% of the time, Pallas kernels for 0%

profile of v2, /device:TPU:1, one launch (start us, length us, event | category | flops | bytes accessed | tf_op | source)
XLA Modules:
  0.0 298.8 jit_solution(14872229043753311498)
XLA Ops:
  6.5 0.0 copy-start
  6.5 0.0 all-gather.3.cloned.1.call-start
  6.5 35.0 %all_gather.12 = bf16[512,512]{0,1:T(8,128)(2,1)} all-gather(bf16[512,32]{0,1:T(8,128)(2,1)} %param.9), channel_id=1, replica_groups=mesh['ey'=1,'ec'=8,'mx'=4,'mz'=16] {'mz'}, dimensions={1}, use_global_device_ids=true | all-gather | bytes 557056 | tf_op jit(solution)/shard_map/all_gather | solution.py:34
  41.5 0.0 all-gather.3.cloned.1.call-update
  41.5 0.0 all-gather.5.cloned.1.call-start
  41.6 2.3 pad_maximum_fusion
  43.9 0.0 all-gather.5.cloned.1.call-update
  43.9 0.0 copy-done.1
  43.9 0.1 copy.42
  44.1 0.2 eq.29
  44.3 0.2 eq.25
  44.4 2.3 reduce-window.6
  46.7 0.3 slice_reduce_fusion
  47.0 0.2 reduce-window.9
  47.2 0.2 copy.41
  47.3 0.2 mul.55
  47.5 0.2 reshape.104
  47.7 0.1 add_bitcast_fusion
  47.9 35.2 %all-gather.3.cloned.1.call-done = bf16[512,2048]{0,1:T(8,128)(2,1)} async-done(((bf16[512,512]{0,1:T(8,128)(2,1)}), bf16[512,2048]{0,1:T(8,128)(2,1)}) %all-gather.3.cloned.1.call-update) | async-done | bytes 2097168 | tf_op jit(solution)/shard_map/all_gather | solution.py:33
  83.1 0.0 copy-done
  83.1 2.0 convolution_convert_fusion
  85.1 0.1 copy.44
  85.3 6.4 %scatter_custom_fusion = bf16[2048,32]{1,0:T(8,128)(2,1)S(1)} fusion(s32[1024]{0:T(1024)S(1)} %bitcast.68, bf16[512,32]{1,0:T(8,128)(2,1)S(1)} %copy.44, s32[1024]{0:T(1024)S(1)} %broadcast_clamp_fusion.1, bf16[]{:T(256)} %constant.10.clone.1), kind=kCustom, calls=%fused_computation.23 | custom fusion | bytes 131074 | tf_op jit(solution)/shard_map/scatter | solution.py:47
  91.7 0.2 copy.46
  91.9 0.1 broadcast_in_dim.10
  92.0 64.2 %all_to_all.22 = bf16[256,64,32]{0,2,1:T(8,128)(2,1)S(1)} all-to-all(bf16[256,64,32]{0,2,1:T(8,128)(2,1)S(1)} %bitcast.59), channel_id=1, replica_groups=mesh['ey'=1,'ec'=8,'mx'=4,'mz'=16] {'mx','mz'}, dimensions={1} | all-to-all | bytes 2097152 | tf_op jit(solution)/shard_map/all_to_all | solution.py:51
  156.2 2.7 fusion.2
  159.0 6.0 %fusion.3 = bf16[256,2048]{1,0:T(8,128)(2,1)S(1)} fusion(bf16[3,704,2048]{2,1,0:T(8,128)(2,1)} %all-gather.5.cloned.1.call-done, bf16[256,2048]{0,1:T(8,128)(2,1)S(1)} %bitcast.63, f32[256,704]{0,1:T(8,128)S(1)} %fusion.2), kind=kOutput, calls=%fused_computation.10 | convolution fusion | flops 1478000640 | bytes 8585216 | tf_op jit(solution)/shard_map/dot_general | solution.py:66
  164.9 0.0 copy-start.2
  165.0 0.0 copy-start.3
  165.0 1.3 copy.47
  166.3 10.3 %all-to-all-start.1 = ((bf16[256,64,32]{0,2,1:T(8,128)(2,1)}), bf16[256,64,32]{0,2,1:T(8,128)(2,1)S(1)}, u32[]{:S(2)}, u32[]{:S(2)}) async-start(bf16[256,64,32]{0,2,1:T(8,128)(2,1)} %bitcast.14), calls=%async_computation.1 | async-start | bytes 2097152 | tf_op jit(solution)/shard_map/all_to_all | solution.py:71
  176.6 0.1 rev.3
  176.8 0.1 copy.49
  177.0 49.9 %all-to-all-done.1 = bf16[256,64,32]{0,2,1:T(8,128)(2,1)S(1)} async-done(((bf16[256,64,32]{0,2,1:T(8,128)(2,1)}), bf16[256,64,32]{0,2,1:T(8,128)(2,1)S(1)}, u32[]{:S(2)}, u32[]{:S(2)}) %all-to-all-start.1) | async-done | bytes 1048608 | tf_op jit(solution)/shard_map/all_to_all | solution.py:71
  226.9 0.2 bitcast_reduce_fusion
  227.0 0.3 copy.48
  227.4 0.0 copy-start.4
  227.4 2.8 gather_fusion
  230.2 2.8 multiply_reduce_fusion
  233.0 0.1 copy.50
  233.2 23.4 %psum.14 = f32[512]{0:T(512)S(1)} all-reduce(f32[512]{0:T(512)S(1)} %multiply_reduce_fusion.1), channel_id=1, replica_groups=mesh['ey'=1,'ec'=8,'mx'=4,'mz'=16] {'mz'}, use_global_device_ids=true, to_apply=%region_7.8 | all-reduce | flops 512 | bytes 4096 | tf_op jit(solution)/shard_map/psum | solution.py:83
  256.5 8.4 %psum.15 = f32[512]{0:T(512)S(1)} all-reduce(f32[512]{0:T(512)S(1)} %psum.14), channel_id=1, replica_groups=mesh['ey'=1,'ec'=8,'mx'=4,'mz'=16] {'mx'}, use_global_device_ids=true, to_apply=%region_8.9 | all-reduce | flops 512 | bytes 4096 | tf_op jit(solution)/shard_map/psum | solution.py:83
  265.0 0.1 multiply_convert_fusion
  265.1 24.4 %all_gather.15 = bf16[4096,32]{0,1:T(8,128)(2,1)S(1)} all-gather(bf16[512,32]{0,1:T(8,128)(2,1)S(1)} %multiply_convert_fusion), channel_id=1, replica_groups=mesh['ey'=1,'ec'=8,'mx'=4,'mz'=16] {'ey','ec'}, dimensions={0}, use_global_device_ids=true | all-gather | bytes 294912 | tf_op jit(solution)/shard_map/all_gather | solution.py:87
  289.4 0.5 copy.51
  289.9 1.3 gather_fusion.1
  291.3 0.7 copy.52
  (18 shorter events, 0.2 us)
Async XLA Ops:
  6.5 76.6 %copy-start = (bf16[32,2048]{1,0:T(8,128)(2,1)S(1)}, bf16[32,2048]{1,0:T(8,128)(2,1)}, u32[]{:S(2)}) copy-start(bf16[32,2048]{1,0:T(8,128)(2,1)} %param.10) | copy-start | bytes 393220
  6.5 37.4 %copy-start.1 = (s32[512,2]{0,1:T(2,128)S(1)}, s32[512,2]{0,1:T(2,128)}, u32[]{:S(2)}) copy-start(s32[512,2]{0,1:T(2,128)} %param.11) | copy-start | bytes 12292
  6.5 76.6 %all-gather.3.cloned.1.call-start = ((), (), s32[]{:S(2)}) async-start(), calls=%async_computation.2 | async-start | bytes 2621440 | tf_op jit(solution)/shard_map/all_gather | solution.py:33
  41.5 114.7 %all-gather.5.cloned.1.call-start = ((), (), s32[]{:S(2)}) async-start(), calls=%async_computation.3 | async-start | bytes 9732096 | tf_op jit(solution)/shard_map/all_gather | solution.py:52
  164.9 11.7 %copy-start.2 = (f32[512,2]{0,1:T(2,128)S(1)}, f32[512,2]{0,1:T(2,128)}, u32[]{:S(2)}) copy-start(f32[512,2]{0,1:T(2,128)} %param.12) | copy-start | bytes 12292
  165.0 12.0 %copy-start.3 = (s32[512]{0:T(512)S(1)}, s32[512]{0:T(512)}, u32[]{:S(2)}) copy-start(s32[512]{0:T(512)} %param.17) | copy-start | bytes 6148
  166.3 60.6 %all-to-all-start.1 = ((bf16[256,64,32]{0,2,1:T(8,128)(2,1)}), bf16[256,64,32]{0,2,1:T(8,128)(2,1)S(1)}, u32[]{:S(2)}, u32[]{:S(2)}) async-start(bf16[256,64,32]{0,2,1:T(8,128)(2,1)} %bitcast.14), calls=%async_computation.1 | async-start | bytes 2097152 | tf_op jit(solution)/shard_map/all_to_all | solution.py:71
  227.4 37.6 %copy-start.4 = (f32[32]{0:T(128)S(1)}, f32[32]{0:T(128)}, u32[]{:S(2)}) copy-start(f32[32]{0:T(128)} %param.16) | copy-start | bytes 388
Sparse Core Ops, SparseCore 0:
  41.7 41.3 all-gather.2
  85.2 63.2 all-gather.4

commit v3 on v2

--- a/solution.py
+++ b/solution.py
@@ -30,14 +30,17 @@
     copies = mp_count // EXPERTS
     capacity = CAP
     top_k = routes.shape[1]
-    gathered = lax.all_gather(
-        lax.all_gather(context, "mz", axis=1, tiled=True), "mx", axis=1, tiled=True
+    x_count = lax.axis_size("mx")
+    x_at = lax.axis_index("mx")
+    along_z = lax.all_gather(context, "mz", axis=1, tiled=True)
+    z_width = along_z.shape[1]
+    rows_x = lax.all_gather(out_proj, "mx", axis=0, tiled=True)
+    rows_x = lax.dynamic_slice_in_dim(rows_x, x_at * z_width, z_width, axis=1)
+    partial_attended = jnp.einsum(
+        "td,cd->tc", along_z, rows_x, preferred_element_type=jnp.float32
     )
-    attended = jnp.einsum(
-        "td,cd->tc",
-        gathered,
-        out_proj,
-        preferred_element_type=jnp.float32,
+    attended = lax.psum_scatter(
+        partial_attended, "mx", scatter_dimension=1, tiled=True
     ).astype(jnp.bfloat16)
     destination = slot_targets(routes, capacity, EXPERTS)
     source_rows = jnp.repeat(jnp.arange(tok_rows, dtype=jnp.int32), top_k)

time: 299 us -> 298 us (level)
  waiting for transfers between devices: 85.2 us -> 72.5 us
  blocking collectives: 155 us -> 165 us
    all_gather x1 -> x0, waiting for transfers between devices: 35.2 us -> none  [shards(): lax.all_gather(lax.all_gather(context, 'mz', axis=1, tiled=True), 'mx', a...]
    reduce_scatter x0 -> x1, waiting for transfers between devices: none -> 24.5 us  [shards(): lax.psum_scatter(partial_attended, 'mx', scatter_dimension=1, tiled=True)]
    all_gather x1 -> x2, blocking collectives: 35 us -> 44.4 us  [the longest x1 33 us: shards(): along_z = lax.all_gather(context, 'mz', axis=1, tiled=True)]
where the time goes in v3:
time: 298 us
  blocking collectives  165 us (55%)
  waiting for transfers between devices  72.5 us (24%)
  local copies, waits for them, and re-layouts  15.5 us (5%)
  between operations  15.1 us (5%)
  starting transfers between devices  10.9 us (4%)
  matrix products  9.64 us (3%)
  other arithmetic  8.91 us (3%)
    all_to_all x1, blocking collectives, shards(): lax.all_to_all(outgoing, MP, split_axis=1, concat_axis=1, tiled=True)  62 us
    all_to_all x1, waiting for transfers between devices, shards(): lax.all_to_all(partial_value.astype(jnp.bfloat16), MP, split_axis=1, conc...  48 us
    all_gather x1, blocking collectives, shards(): along_z = lax.all_gather(context, 'mz', axis=1, tiled=True)  33 us
    all_gather x1, blocking collectives, shards(): everyone = lax.all_gather(normed, EX, axis=0, tiled=True)  25.2 us
    reduce_scatter x1, waiting for transfers between devices, shards(): lax.psum_scatter(partial_attended, 'mx', scatter_dimension=1, tiled=True)  24.5 us
    psum x1, blocking collectives, shards(): lax.psum(jnp.sum(combined * combined, axis=1), 'mz')  24.4 us
    all_gather x1, blocking collectives, shards(): rows_x = lax.all_gather(out_proj, 'mx', axis=0, tiled=True)  11.4 us
    all_to_all x1, starting transfers between devices, shards(): lax.all_to_all(partial_value.astype(jnp.bfloat16), MP, split_axis=1, conc...  10.9 us
  transfers between devices with their start and end apart: 3, of which 2 were waited for; matrix products, arithmetic and copies ran while one was open for 5% of the time, Pallas kernels for 0%

profile of v3, /device:TPU:1, one launch (start us, length us, event | category | flops | bytes accessed | tf_op | source)
XLA Modules:
  0.0 297.6 jit_solution(8688629110815897243)
XLA Ops:
  7.4 0.0 reduce-scatter.2.cloned.1.call-start
  7.4 11.4 %all_gather.12 = bf16[128,2048]{1,0:T(8,128)(2,1)S(1)} all-gather(bf16[32,2048]{1,0:T(8,128)(2,1)} %param.10), channel_id=1, replica_groups=mesh['ey'=1,'ec'=8,'mx'=4,'mz'=16] {'mx'}, dimensions={0}, use_global_device_ids=true | all-gather | bytes 655360 | tf_op jit(solution)/shard_map/all_gather | solution.py:37
  18.8 33.0 %all_gather.13 = bf16[512,512]{0,1:T(8,128)(2,1)S(1)} all-gather(bf16[512,32]{0,1:T(8,128)(2,1)} %param.9), channel_id=1, replica_groups=mesh['ey'=1,'ec'=8,'mx'=4,'mz'=16] {'mz'}, dimensions={1}, use_global_device_ids=true | all-gather | bytes 557056 | tf_op jit(solution)/shard_map/all_gather | solution.py:35
  51.8 0.9 convolution_bitcast_fusion
  52.7 0.0 reduce-scatter.2.cloned.1.call-update
  52.7 0.0 all-gather.2.cloned.1.call-start
  52.8 2.4 pad_maximum_fusion
  55.2 0.0 all-gather.2.cloned.1.call-update
  55.2 0.0 copy-done.1
  55.2 0.1 copy.42
  55.4 0.2 eq.29
  55.5 0.2 eq.25
  55.7 2.3 reduce-window.6
  58.0 0.3 slice_reduce_fusion
  58.3 0.2 reduce-window.9
  58.4 0.2 copy.41
  58.6 0.2 mul.59
  58.8 0.2 reshape.104
  59.0 0.1 add_bitcast_fusion
  59.1 24.5 %reduce-scatter.2.cloned.1.call-done = f32[512,32]{0,1:T(8,128)} async-done(((f32[512,128]{0,1:T(8,128)}), f32[512,32]{0,1:T(8,128)}) %reduce-scatter.2.cloned.1.call-update) | async-done | bytes 65552 | tf_op jit(solution)/shard_map/reduce_scatter | solution.py:42
  83.7 0.8 convert_element_type.31
  84.5 0.1 copy.44
  84.6 6.4 %scatter_custom_fusion = bf16[2048,32]{1,0:T(8,128)(2,1)S(1)} fusion(s32[1024]{0:T(1024)S(1)} %bitcast.69, bf16[512,32]{1,0:T(8,128)(2,1)S(1)} %copy.44, s32[1024]{0:T(1024)S(1)} %broadcast_clamp_fusion.1, bf16[]{:T(256)} %constant.7.clone.1), kind=kCustom, calls=%fused_computation.23 | custom fusion | bytes 131074 | tf_op jit(solution)/shard_map/scatter | solution.py:50
  91.0 0.2 copy.46
  91.2 0.1 broadcast_in_dim.10
  91.4 62.0 %all_to_all.22 = bf16[256,64,32]{0,2,1:T(8,128)(2,1)S(1)} all-to-all(bf16[256,64,32]{0,2,1:T(8,128)(2,1)S(1)} %bitcast.60), channel_id=1, replica_groups=mesh['ey'=1,'ec'=8,'mx'=4,'mz'=16] {'mx','mz'}, dimensions={1} | all-to-all | bytes 2097152 | tf_op jit(solution)/shard_map/all_to_all | solution.py:54
  153.4 2.7 fusion.2
  156.1 6.0 %fusion.3 = bf16[256,2048]{1,0:T(8,128)(2,1)S(1)} fusion(bf16[3,704,2048]{2,1,0:T(8,128)(2,1)} %all-gather.2.cloned.1.call-done, bf16[256,2048]{0,1:T(8,128)(2,1)S(1)} %bitcast.64, f32[256,704]{0,1:T(8,128)S(1)} %fusion.2), kind=kOutput, calls=%fused_computation.10 | convolution fusion | flops 1478000640 | bytes 8585216 | tf_op jit(solution)/shard_map/dot_general | solution.py:69
  162.1 0.0 copy-start.2
  162.1 0.0 copy-start.3
  162.1 1.3 copy.47
  163.4 10.9 %all-to-all-start.1 = ((bf16[256,64,32]{0,2,1:T(8,128)(2,1)}), bf16[256,64,32]{0,2,1:T(8,128)(2,1)S(1)}, u32[]{:S(2)}, u32[]{:S(2)}) async-start(bf16[256,64,32]{0,2,1:T(8,128)(2,1)} %bitcast.15), calls=%async_computation.2 | async-start | bytes 2097152 | tf_op jit(solution)/shard_map/all_to_all | solution.py:74
  174.3 0.1 rev.3
  174.5 0.1 copy.49
  174.7 48.0 %all-to-all-done.1 = bf16[256,64,32]{0,2,1:T(8,128)(2,1)S(1)} async-done(((bf16[256,64,32]{0,2,1:T(8,128)(2,1)}), bf16[256,64,32]{0,2,1:T(8,128)(2,1)S(1)}, u32[]{:S(2)}, u32[]{:S(2)}) %all-to-all-start.1) | async-done | bytes 1048608 | tf_op jit(solution)/shard_map/all_to_all | solution.py:74
  222.7 0.2 bitcast_reduce_fusion
  222.8 0.3 copy.48
  223.2 0.0 copy-start.4
  223.2 2.8 gather_fusion
  226.0 2.8 multiply_reduce_fusion
  228.8 0.1 copy.50
  229.0 24.4 %psum.14 = f32[512]{0:T(512)S(1)} all-reduce(f32[512]{0:T(512)S(1)} %multiply_reduce_fusion.1), channel_id=1, replica_groups=mesh['ey'=1,'ec'=8,'mx'=4,'mz'=16] {'mz'}, use_global_device_ids=true, to_apply=%region_8.9 | all-reduce | flops 512 | bytes 4096 | tf_op jit(solution)/shard_map/psum | solution.py:86
  253.4 9.0 %psum.15 = f32[512]{0:T(512)S(1)} all-reduce(f32[512]{0:T(512)S(1)} %psum.14), channel_id=1, replica_groups=mesh['ey'=1,'ec'=8,'mx'=4,'mz'=16] {'mx'}, use_global_device_ids=true, to_apply=%region_9.10 | all-reduce | flops 512 | bytes 4096 | tf_op jit(solution)/shard_map/psum | solution.py:86
  262.4 0.1 multiply_convert_fusion
  262.5 25.2 %all_gather.15 = bf16[4096,32]{0,1:T(8,128)(2,1)S(1)} all-gather(bf16[512,32]{0,1:T(8,128)(2,1)S(1)} %multiply_convert_fusion), channel_id=1, replica_groups=mesh['ey'=1,'ec'=8,'mx'=4,'mz'=16] {'ey','ec'}, dimensions={0}, use_global_device_ids=true | all-gather | bytes 294912 | tf_op jit(solution)/shard_map/all_gather | solution.py:90
  287.7 0.5 copy.51
  288.1 1.3 gather_fusion.1
  289.5 0.7 copy.52
  (20 shorter events, 0.2 us)
Async XLA Ops:
  7.4 47.8 %copy-start.1 = (s32[512,2]{0,1:T(2,128)S(1)}, s32[512,2]{0,1:T(2,128)}, u32[]{:S(2)}) copy-start(s32[512,2]{0,1:T(2,128)} %param.11) | copy-start | bytes 12292
  7.4 76.3 %reduce-scatter.2.cloned.1.call-start = ((), (), s32[]{:S(2)}) async-start(), calls=%async_computation.3 | async-start | bytes 327680 | tf_op jit(solution)/shard_map/reduce_scatter | solution.py:42
  52.7 100.6 %all-gather.2.cloned.1.call-start = ((), (), s32[]{:S(2)}) async-start(), calls=%async_computation.4 | async-start | bytes 9732096 | tf_op jit(solution)/shard_map/all_gather | solution.py:55
  162.1 12.2 %copy-start.2 = (f32[512,2]{0,1:T(2,128)S(1)}, f32[512,2]{0,1:T(2,128)}, u32[]{:S(2)}) copy-start(f32[512,2]{0,1:T(2,128)} %param.12) | copy-start | bytes 12292
  162.1 12.5 %copy-start.3 = (s32[512]{0:T(512)S(1)}, s32[512]{0:T(512)}, u32[]{:S(2)}) copy-start(s32[512]{0:T(512)} %param.17) | copy-start | bytes 6148
  163.4 59.2 %all-to-all-start.1 = ((bf16[256,64,32]{0,2,1:T(8,128)(2,1)}), bf16[256,64,32]{0,2,1:T(8,128)(2,1)S(1)}, u32[]{:S(2)}, u32[]{:S(2)}) async-start(bf16[256,64,32]{0,2,1:T(8,128)(2,1)} %bitcast.15), calls=%async_computation.2 | async-start | bytes 2097152 | tf_op jit(solution)/shard_map/all_to_all | solution.py:74
  223.2 5.8 %copy-start = (f32[512,32]{0,1:T(8,128)S(1)}, f32[512,32]{0,1:T(8,128)}, u32[]{:S(2)}) copy-start(f32[512,32]{0,1:T(8,128)} %reduce-scatter.2.cloned.1.call-done) | copy-start | bytes 196612
  223.2 39.2 %copy-start.4 = (f32[32]{0:T(128)S(1)}, f32[32]{0:T(128)}, u32[]{:S(2)}) copy-start(f32[32]{0:T(128)} %param.16) | copy-start | bytes 388
Sparse Core Ops, SparseCore 0:
  52.9 30.7 reduce-scatter.1
Sparse Core Ops, SparseCore 1:
  55.3 67.2 all-gather.1

commit v4 on v3

--- a/solution.py
+++ b/solution.py
@@ -39,8 +39,15 @@
     partial_attended = jnp.einsum(
         "td,cd->tc", along_z, rows_x, preferred_element_type=jnp.float32
     )
-    attended = lax.psum_scatter(
-        partial_attended, "mx", scatter_dimension=1, tiled=True
+    attended = jnp.sum(
+        lax.all_to_all(
+            partial_attended.reshape(tok_rows, x_count, feat_local),
+            "mx",
+            split_axis=1,
+            concat_axis=1,
+            tiled=True,
+        ),
+        axis=1,
     ).astype(jnp.bfloat16)
     destination = slot_targets(routes, capacity, EXPERTS)
     source_rows = jnp.repeat(jnp.arange(tok_rows, dtype=jnp.int32), top_k)
@@ -83,7 +90,10 @@
     weights = 1.0 / (1.0 + jnp.exp(router_logits[:, ::-1] - router_logits))
     branch = jnp.sum(picked * weights[:, :, None], axis=1)
     combined = attended.astype(jnp.float32) + branch
-    squares = lax.psum(lax.psum(jnp.sum(combined * combined, axis=1), "mz"), "mx")
+    squares = jnp.sum(
+        lax.all_gather(jnp.sum(combined * combined, axis=1), "mz", axis=0), axis=0
+    )
+    squares = jnp.sum(lax.all_gather(squares, "mx", axis=0), axis=0)
     normed = (
         combined * norm_gain[None, :] * lax.rsqrt(squares / model_width + epsilon)[:, None]
     ).astype(jnp.bfloat16)

time: 298 us -> 264 us (0.89)
  waiting for transfers between devices: 72.5 us -> 43 us
  blocking collectives: 165 us -> 160 us
    psum x2 -> x0, blocking collectives: 33.4 us -> none  [the longest x1 24.4 us: shards(): lax.psum(jnp.sum(combined * combined, axis=1), 'mz')]
    all_gather x0 -> x2, blocking collectives: none -> 32.5 us  [the longest x1 23.3 us: shards(): lax.all_gather(jnp.sum(combined * combined, axis=1), 'mz', axis=0)]
    reduce_scatter x1 -> x0, waiting for transfers between devices: 24.5 us -> none  [shards(): lax.psum_scatter(partial_attended, 'mx', scatter_dimension=1, tiled=True)]
    all_to_all x1, blocking collectives: 62 us -> 50.9 us  [shards(): lax.all_to_all(outgoing, MP, split_axis=1, concat_axis=1, tiled=True)]
    all_to_all x1, waiting for transfers between devices: 48 us -> 41.4 us  [shards(): lax.all_to_all(partial_value.astype(jnp.bfloat16), MP, split_axis=1, conc...]
    all_gather x1, blocking collectives: 25.2 us -> 31.6 us  [shards(): everyone = lax.all_gather(normed, EX, axis=0, tiled=True)]
    all_to_all x0 -> x1, starting transfers between devices: none -> 3.4 us  [shards(): lax.all_to_all(partial_attended.reshape(tok_rows, x_count, feat_local), '...]
where the time goes in v4:
time: 264 us
  blocking collectives  160 us (61%)
  waiting for transfers between devices  43 us (16%)
  local copies, waits for them, and re-layouts  15.5 us (6%)
  between operations  13.7 us (5%)
  starting transfers between devices  13.3 us (5%)
  matrix products  9.64 us (4%)
  other arithmetic  8.19 us (3%)
    all_to_all x1, blocking collectives, shards(): lax.all_to_all(outgoing, MP, split_axis=1, concat_axis=1, tiled=True)  50.9 us
    all_to_all x1, waiting for transfers between devices, shards(): lax.all_to_all(partial_value.astype(jnp.bfloat16), MP, split_axis=1, conc...  41.4 us
    all_gather x1, blocking collectives, shards(): along_z = lax.all_gather(context, 'mz', axis=1, tiled=True)  34.1 us
    all_gather x1, blocking collectives, shards(): everyone = lax.all_gather(normed, EX, axis=0, tiled=True)  31.6 us
    all_gather x1, blocking collectives, shards(): lax.all_gather(jnp.sum(combined * combined, axis=1), 'mz', axis=0)  23.3 us
    all_gather x1, blocking collectives, shards(): rows_x = lax.all_gather(out_proj, 'mx', axis=0, tiled=True)  11.1 us
    all_to_all x1, starting transfers between devices, shards(): lax.all_to_all(partial_value.astype(jnp.bfloat16), MP, split_axis=1, conc...  9.91 us
    all_gather x1, blocking collectives, shards(): squares = jnp.sum(lax.all_gather(squares, 'mx', axis=0), axis=0)  9.11 us
  transfers between devices with their start and end apart: 3, of which 2 were waited for; matrix products, arithmetic and copies ran while one was open for 5% of the time, Pallas kernels for 0%

profile of v4, /device:TPU:1, one launch (start us, length us, event | category | flops | bytes accessed | tf_op | source)
XLA Modules:
  0.0 263.5 jit_solution(8372045463833635151)
XLA Ops:
  6.5 0.0 all-gather.6.cloned.1.call-start
  6.5 2.4 pad_maximum_fusion
  9.0 0.0 all-gather.6.cloned.1.call-update
  9.0 0.0 copy-done
  9.0 11.1 %all_gather.24 = bf16[128,2048]{1,0:T(8,128)(2,1)S(1)} all-gather(bf16[32,2048]{1,0:T(8,128)(2,1)S(1)} %copy-done), channel_id=1, replica_groups=mesh['ey'=1,'ec'=8,'mx'=4,'mz'=16] {'mx'}, dimensions={0}, use_global_device_ids=true | all-gather | bytes 655360 | tf_op jit(solution)/shard_map/all_gather | solution.py:37
  20.1 0.0 copy-done.1
  20.1 34.1 %all_gather.25 = bf16[512,512]{0,1:T(8,128)(2,1)S(1)} all-gather(bf16[512,32]{0,1:T(8,128)(2,1)S(1)} %copy-done.1), channel_id=1, replica_groups=mesh['ey'=1,'ec'=8,'mx'=4,'mz'=16] {'mz'}, dimensions={1}, use_global_device_ids=true | all-gather | bytes 557056 | tf_op jit(solution)/shard_map/all_gather | solution.py:35
  54.2 0.9 fusion.15
  55.1 3.4 %all-to-all-start = ((f32[512,4,32]{0,2,1:T(8,128)}), f32[512,4,32]{0,2,1:T(8,128)S(1)}, u32[]{:S(2)}, u32[]{:S(2)}) async-start(f32[512,4,32]{0,2,1:T(8,128)} %bitcast.1), calls=%async_computation | async-start | bytes 524288 | tf_op jit(solution)/shard_map/all_to_all | solution.py:43
  58.6 0.0 copy-done.2
  58.6 0.1 copy.55
  58.7 0.2 eq.29
  58.9 0.2 eq.25
  59.1 2.3 reduce-window.6
  61.3 0.3 slice_reduce_fusion
  61.6 0.2 reduce-window.9
  61.8 0.1 copy.54
  62.0 0.2 mul.59
  62.2 0.2 reshape.112
  62.3 0.1 add_bitcast_fusion
  62.5 1.6 all-to-all-done
  64.1 0.1 copy.57
  64.2 6.4 %scatter_custom_fusion = bf16[2048,32]{1,0:T(8,128)(2,1)S(1)} fusion(s32[1024]{0:T(1024)S(1)} %bitcast.72, bf16[512,32]{1,0:T(8,128)(2,1)S(1)} %copy.57, s32[1024]{0:T(1024)S(1)} %broadcast_clamp_fusion.1, bf16[]{:T(256)} %constant.18.clone.1), kind=kCustom, calls=%fused_computation.22 | custom fusion | bytes 131074 | tf_op jit(solution)/shard_map/scatter | solution.py:57
  70.6 0.2 copy.59
  70.8 0.1 broadcast_in_dim.10
  70.9 50.9 %all_to_all.27 = bf16[256,64,32]{0,2,1:T(8,128)(2,1)S(1)} all-to-all(bf16[256,64,32]{0,2,1:T(8,128)(2,1)S(1)} %bitcast.63), channel_id=1, replica_groups=mesh['ey'=1,'ec'=8,'mx'=4,'mz'=16] {'mx','mz'}, dimensions={1} | all-to-all | bytes 2097152 | tf_op jit(solution)/shard_map/all_to_all | solution.py:61
  121.9 2.7 %fusion.2 = f32[256,704]{0,1:T(8,128)S(1)} fusion(bf16[256,2048]{0,1:T(8,128)(2,1)S(1)} %bitcast.66, bf16[3,704,2048]{2,1,0:T(8,128)(2,1)} %all-gather.6.cloned.1.call-done), kind=kOutput, calls=%fused_computation.9 | convolution fusion | flops 738197504 | bytes 4653056 | tf_op jit(solution)/shard_map/rd,hd->rh/dot_general | solution.py:63
  124.6 6.0 %fusion.3 = bf16[256,2048]{1,0:T(8,128)(2,1)S(1)} fusion(bf16[3,704,2048]{2,1,0:T(8,128)(2,1)} %all-gather.6.cloned.1.call-done, bf16[256,2048]{0,1:T(8,128)(2,1)S(1)} %bitcast.67, f32[256,704]{0,1:T(8,128)S(1)} %fusion.2), kind=kOutput, calls=%fused_computation.10 | convolution fusion | flops 1478000640 | bytes 8585216 | tf_op jit(solution)/shard_map/dot_general | solution.py:76
  130.6 0.0 copy-start.3
  130.6 0.0 copy-start.4
  130.6 1.3 copy.60
  131.9 9.9 %all-to-all-start.2 = ((bf16[256,64,32]{0,2,1:T(8,128)(2,1)}), bf16[256,64,32]{0,2,1:T(8,128)(2,1)S(1)}, u32[]{:S(2)}, u32[]{:S(2)}) async-start(bf16[256,64,32]{0,2,1:T(8,128)(2,1)} %bitcast.16), calls=%async_computation.2 | async-start | bytes 2097152 | tf_op jit(solution)/shard_map/all_to_all | solution.py:81
  141.8 0.1 rev.3
  142.0 0.1 copy.62
  142.2 41.4 %all-to-all-done.2 = bf16[256,64,32]{0,2,1:T(8,128)(2,1)S(1)} async-done(((bf16[256,64,32]{0,2,1:T(8,128)(2,1)}), bf16[256,64,32]{0,2,1:T(8,128)(2,1)S(1)}, u32[]{:S(2)}, u32[]{:S(2)}) %all-to-all-start.2) | async-done | bytes 1048608 | tf_op jit(solution)/shard_map/all_to_all | solution.py:81
  183.6 0.2 bitcast_reduce_fusion
  183.8 0.3 copy.61
  184.2 0.0 copy-start.5
  184.2 2.8 %gather_fusion = f32[1024,32]{1,0:T(8,128)S(1)} fusion(f32[2048,32]{1,0:T(8,128)S(1)} %bitcast.62, s32[1024]{0:T(1024)S(1)} %broadcast_clamp_fusion), kind=kCustom, calls=%fused_computation.1 | custom fusion | bytes 266240 | tf_op jit(solution)/shard_map/gather | solution.py:89
  187.0 2.8 %multiply_reduce_fusion = f32[512,32]{1,0:T(8,128)S(1)} fusion(f32[512,2,32]{2,1,0:T(2,128)S(1)} %bitcast.65, f32[512,2]{1,0:T(8,128)S(1)} %copy.62), kind=kLoop, calls=%fused_computation.20 | loop fusion | flops 49152 | bytes 200704 | tf_op jit(solution)/shard_map/reduce_sum | solution.py:91
  189.8 0.1 copy.63
  189.9 23.3 %all-gather.2 = f32[16,1,512]{2,1,0:T(1,128)S(1)} all-gather(f32[1,1,512]{2,1,0:T(1,128)S(1)} %bitcast.77), channel_id=2, replica_groups=mesh['ey'=1,'ec'=8,'mx'=4,'mz'=16] {'mz'}, dimensions={0}, use_global_device_ids=true | all-gather | bytes 34816 | tf_op jit(solution)/shard_map/all_gather | solution.py:94
  213.3 9.1 %all-gather.3 = f32[4,1,512]{2,1,0:T(1,128)S(1)} all-gather(f32[1,1,512]{2,1,0:T(1,128)S(1)} %bitcast.76), channel_id=3, replica_groups=mesh['ey'=1,'ec'=8,'mx'=4,'mz'=16] {'mx'}, dimensions={0}, use_global_device_ids=true | all-gather | bytes 10240 | tf_op jit(solution)/shard_map/all_gather | solution.py:96
  222.5 0.1 multiply_convert_fusion
  222.6 31.6 %all_gather.31 = bf16[4096,32]{0,1:T(8,128)(2,1)S(1)} all-gather(bf16[512,32]{0,1:T(8,128)(2,1)S(1)} %multiply_convert_fusion), channel_id=1, replica_groups=mesh['ey'=1,'ec'=8,'mx'=4,'mz'=16] {'ey','ec'}, dimensions={0}, use_global_device_ids=true | all-gather | bytes 294912 | tf_op jit(solution)/shard_map/all_gather | solution.py:100
  254.1 0.5 copy.64
  254.6 1.3 gather_fusion.1
  256.0 0.7 copy.65
  (23 shorter events, 0.2 us)
Async XLA Ops:
  6.5 2.5 copy-start
  6.5 13.5 %copy-start.1 = (bf16[512,32]{0,1:T(8,128)(2,1)S(1)}, bf16[512,32]{0,1:T(8,128)(2,1)}, u32[]{:S(2)}) copy-start(bf16[512,32]{0,1:T(8,128)(2,1)} %param.9) | copy-start | bytes 98308
  6.5 115.3 %all-gather.6.cloned.1.call-start = ((), (), s32[]{:S(2)}) async-start(), calls=%async_computation.3 | async-start | bytes 9732096 | tf_op jit(solution)/shard_map/all_gather | solution.py:62
  6.5 52.0 %copy-start.2 = (s32[512,2]{0,1:T(2,128)S(1)}, s32[512,2]{0,1:T(2,128)}, u32[]{:S(2)}) copy-start(s32[512,2]{0,1:T(2,128)} %param.11) | copy-start | bytes 12292
  55.1 8.9 %all-to-all-start = ((f32[512,4,32]{0,2,1:T(8,128)}), f32[512,4,32]{0,2,1:T(8,128)S(1)}, u32[]{:S(2)}, u32[]{:S(2)}) async-start(f32[512,4,32]{0,2,1:T(8,128)} %bitcast.1), calls=%async_computation | async-start | bytes 524288 | tf_op jit(solution)/shard_map/all_to_all | solution.py:43
  130.6 11.3 %copy-start.3 = (f32[512,2]{0,1:T(2,128)S(1)}, f32[512,2]{0,1:T(2,128)}, u32[]{:S(2)}) copy-start(f32[512,2]{0,1:T(2,128)} %param.12) | copy-start | bytes 12292
  130.6 11.6 %copy-start.4 = (s32[512]{0:T(512)S(1)}, s32[512]{0:T(512)}, u32[]{:S(2)}) copy-start(s32[512]{0:T(512)} %param.17) | copy-start | bytes 6148
  131.9 51.7 %all-to-all-start.2 = ((bf16[256,64,32]{0,2,1:T(8,128)(2,1)}), bf16[256,64,32]{0,2,1:T(8,128)(2,1)S(1)}, u32[]{:S(2)}, u32[]{:S(2)}) async-start(bf16[256,64,32]{0,2,1:T(8,128)(2,1)} %bitcast.16), calls=%async_computation.2 | async-start | bytes 2097152 | tf_op jit(solution)/shard_map/all_to_all | solution.py:81
  184.2 38.3 %copy-start.5 = (f32[32]{0:T(128)S(1)}, f32[32]{0:T(128)}, u32[]{:S(2)}) copy-start(f32[32]{0:T(128)} %param.16) | copy-start | bytes 388
Sparse Core Ops, SparseCore 0:
  9.5 68.4 all-gather.5

commit v5 on v4

--- a/solution.py
+++ b/solution.py
@@ -32,7 +32,9 @@
     top_k = routes.shape[1]
     x_count = lax.axis_size("mx")
     x_at = lax.axis_index("mx")
-    along_z = lax.all_gather(context, "mz", axis=1, tiled=True)
+    along_z = lax.all_gather(
+        lax.all_gather(context, "mzb", axis=1, tiled=True), "mza", axis=1, tiled=True
+    )
     z_width = along_z.shape[1]
     rows_x = lax.all_gather(out_proj, "mx", axis=0, tiled=True)
     rows_x = lax.dynamic_slice_in_dim(rows_x, x_at * z_width, z_width, axis=1)
@@ -90,9 +92,9 @@
     weights = 1.0 / (1.0 + jnp.exp(router_logits[:, ::-1] - router_logits))
     branch = jnp.sum(picked * weights[:, :, None], axis=1)
     combined = attended.astype(jnp.float32) + branch
-    squares = jnp.sum(
-        lax.all_gather(jnp.sum(combined * combined, axis=1), "mz", axis=0), axis=0
-    )
+    squares = jnp.sum(combined * combined, axis=1)
+    squares = jnp.sum(lax.all_gather(squares, "mzb", axis=0), axis=0)
+    squares = jnp.sum(lax.all_gather(squares, "mza", axis=0), axis=0)
     squares = jnp.sum(lax.all_gather(squares, "mx", axis=0), axis=0)
     normed = (
         combined * norm_gain[None, :] * lax.rsqrt(squares / model_width + epsilon)[:, None]
@@ -102,7 +104,7 @@
 
 
 EX = ("ey", "ec")
-MP = ("mx", "mz")
+MP = ("mx", "mza", "mzb")
 
 
 def split_mesh(mesh):
@@ -113,8 +115,10 @@
         z_count = len({d.coords[2] for d in row})
     except (AttributeError, IndexError, TypeError):
         z_count = n_mp
+    z_low = 4 if z_count % 4 == 0 else 1
     return Mesh(
-        devices.reshape(1, n_exp, n_mp // z_count, z_count), ("ey", "ec", "mx", "mz")
+        devices.reshape(1, n_exp, n_mp // z_count, z_count // z_low, z_low),
+        ("ey", "ec", "mx", "mza", "mzb"),
     )
 
 

time: 264 us -> 276 us (1.045)
  blocking collectives: 160 us -> 170 us
    all_gather x2 -> x4, blocking collectives: 57.5 us -> 68.3 us  [the longest x1 29.7 us: shards(): lax.all_gather(lax.all_gather(context, 'mzb', axis=1, tiled=True), 'mza',...]
  transfers between devices with their start and end apart: 3 -> 3, of which waited for: 2 -> 2; matrix products, arithmetic and copies ran while one was open for 5% -> 4% of each run, Pallas kernels for 0% -> 0%
where the time goes in v5:
time: 276 us
  blocking collectives  170 us (62%)
  waiting for transfers between devices  44.5 us (16%)
  local copies, waits for them, and re-layouts  15.5 us (6%)
  starting transfers between devices  14.8 us (5%)
  between operations  13.7 us (5%)
  matrix products  9.64 us (3%)
  other arithmetic  8.19 us (3%)
    all_to_all x1, blocking collectives, shards(): lax.all_to_all(outgoing, MP, split_axis=1, concat_axis=1, tiled=True)  51.5 us
    all_to_all x1, waiting for transfers between devices, shards(): lax.all_to_all(partial_value.astype(jnp.bfloat16), MP, split_axis=1, conc...  42.9 us
    all_gather x1, blocking collectives, shards(): lax.all_gather(lax.all_gather(context, 'mzb', axis=1, tiled=True), 'mza',...  29.7 us
    all_gather x1, blocking collectives, shards(): everyone = lax.all_gather(normed, EX, axis=0, tiled=True)  29.5 us
    all_gather x1, blocking collectives, shards(): squares = jnp.sum(lax.all_gather(squares, 'mza', axis=0), axis=0)  14.4 us
    all_gather x1, blocking collectives, shards(): lax.all_gather(context, 'mzb', axis=1, tiled=True)  12.8 us
    all_gather x1, blocking collectives, shards(): rows_x = lax.all_gather(out_proj, 'mx', axis=0, tiled=True)  11.8 us
    all_to_all x1, starting transfers between devices, shards(): lax.all_to_all(partial_value.astype(jnp.bfloat16), MP, split_axis=1, conc...  11.4 us
  transfers between devices with their start and end apart: 3, of which 2 were waited for; matrix products, arithmetic and copies ran while one was open for 4% of the time, Pallas kernels for 0%

profile of v5, /device:TPU:1, one launch (start us, length us, event | category | flops | bytes accessed | tf_op | source)
XLA Modules:
  0.0 275.9 jit_solution(13814009746815433132)
XLA Ops:
  6.5 2.4 pad_maximum_fusion
  9.0 0.0 all-gather.8.cloned.1.call-update
  9.0 0.0 copy-done.1
  9.0 12.8 %all_gather.34 = bf16[512,128]{0,1:T(8,128)(2,1)S(1)} all-gather(bf16[512,32]{0,1:T(8,128)(2,1)S(1)} %copy-done.1), channel_id=1, replica_groups=mesh['ey'=1,'ec'=8,'mx'=4,'mza'=4,'mzb'=4] {'mzb'}, dimensions={1}, use_global_device_ids=true | all-gather | bytes 163840 | tf_op jit(solution)/shard_map/all_gather | solution.py:36
  21.8 29.7 %all_gather.35 = bf16[512,512]{0,1:T(8,128)(2,1)S(1)} all-gather(bf16[512,128]{0,1:T(8,128)(2,1)S(1)} %all_gather.34), channel_id=1, replica_groups=mesh['ey'=1,'ec'=8,'mx'=4,'mza'=4,'mzb'=4] {'mza'}, dimensions={1}, use_global_device_ids=true | all-gather | bytes 655360 | tf_op jit(solution)/shard_map/all_gather | solution.py:35
  51.5 11.8 %all_gather.33 = bf16[128,2048]{1,0:T(8,128)(2,1)S(1)} all-gather(bf16[32,2048]{1,0:T(8,128)(2,1)S(1)} %copy-done), channel_id=1, replica_groups=mesh['ey'=1,'ec'=8,'mx'=4,'mza'=4,'mzb'=4] {'mx'}, dimensions={0}, use_global_device_ids=true | all-gather | bytes 655360 | tf_op jit(solution)/shard_map/all_gather | solution.py:39
  63.3 0.9 fusion.15
  64.2 3.4 %all-to-all-start = ((f32[512,4,32]{0,2,1:T(8,128)}), f32[512,4,32]{0,2,1:T(8,128)S(1)}, u32[]{:S(2)}, u32[]{:S(2)}) async-start(f32[512,4,32]{0,2,1:T(8,128)} %bitcast.1), calls=%async_computation | async-start | bytes 524288 | tf_op jit(solution)/shard_map/all_to_all | solution.py:45
  67.6 0.1 copy.55
  67.8 0.2 eq.29
  68.0 0.2 eq.25
  68.1 2.3 reduce-window.6
  70.4 0.3 slice_reduce_fusion
  70.7 0.2 reduce-window.9
  70.9 0.2 copy.54
  71.0 0.2 mul.59
  71.2 0.2 reshape.112
  71.4 0.1 add_bitcast_fusion
  71.6 1.6 all-to-all-done
  73.2 0.1 copy.57
  73.3 6.4 %scatter_custom_fusion = bf16[2048,32]{1,0:T(8,128)(2,1)S(1)} fusion(s32[1024]{0:T(1024)S(1)} %bitcast.73, bf16[512,32]{1,0:T(8,128)(2,1)S(1)} %copy.57, s32[1024]{0:T(1024)S(1)} %broadcast_clamp_fusion.1, bf16[]{:T(256)} %constant.18.clone.1), kind=kCustom, calls=%fused_computation.22 | custom fusion | bytes 131074 | tf_op jit(solution)/shard_map/scatter | solution.py:59
  79.7 0.2 copy.59
  79.9 0.1 broadcast_in_dim.10
  80.0 51.5 %all_to_all.27 = bf16[256,64,32]{0,2,1:T(8,128)(2,1)S(1)} all-to-all(bf16[256,64,32]{0,2,1:T(8,128)(2,1)S(1)} %bitcast.64), channel_id=1, replica_groups=mesh['ey'=1,'ec'=8,'mx'=4,'mza'=4,'mzb'=4] {'mx','mza','mzb'}, dimensions={1} | all-to-all | bytes 2097152 | tf_op jit(solution)/shard_map/all_to_all | solution.py:63
  131.6 2.7 fusion.2
  134.3 6.0 %fusion.3 = bf16[256,2048]{1,0:T(8,128)(2,1)S(1)} fusion(bf16[3,704,2048]{2,1,0:T(8,128)(2,1)} %all-gather.8.cloned.1.call-done, bf16[256,2048]{0,1:T(8,128)(2,1)S(1)} %bitcast.68, f32[256,704]{0,1:T(8,128)S(1)} %fusion.2), kind=kOutput, calls=%fused_computation.10 | convolution fusion | flops 1478000640 | bytes 8585216 | tf_op jit(solution)/shard_map/dot_general | solution.py:78
  140.3 0.0 copy-start.3
  140.3 0.0 copy-start.4
  140.3 1.3 copy.60
  141.6 11.4 %all-to-all-start.2 = ((bf16[256,64,32]{0,2,1:T(8,128)(2,1)}), bf16[256,64,32]{0,2,1:T(8,128)(2,1)S(1)}, u32[]{:S(2)}, u32[]{:S(2)}) async-start(bf16[256,64,32]{0,2,1:T(8,128)(2,1)} %bitcast.16), calls=%async_computation.2 | async-start | bytes 2097152 | tf_op jit(solution)/shard_map/all_to_all | solution.py:83
  153.0 0.1 rev.3
  153.2 0.1 copy.62
  153.3 0.0 copy-done.4
  153.4 42.9 %all-to-all-done.2 = bf16[256,64,32]{0,2,1:T(8,128)(2,1)S(1)} async-done(((bf16[256,64,32]{0,2,1:T(8,128)(2,1)}), bf16[256,64,32]{0,2,1:T(8,128)(2,1)S(1)}, u32[]{:S(2)}, u32[]{:S(2)}) %all-to-all-start.2) | async-done | bytes 1048608 | tf_op jit(solution)/shard_map/all_to_all | solution.py:83
  196.3 0.2 bitcast_reduce_fusion
  196.5 0.3 copy.61
  196.8 0.0 copy-start.5
  196.9 2.8 %gather_fusion = f32[1024,32]{1,0:T(8,128)S(1)} fusion(f32[2048,32]{1,0:T(8,128)S(1)} %bitcast.63, s32[1024]{0:T(1024)S(1)} %broadcast_clamp_fusion), kind=kCustom, calls=%fused_computation.1 | custom fusion | bytes 266240 | tf_op jit(solution)/shard_map/gather | solution.py:91
  199.7 2.8 %multiply_reduce_fusion = f32[512,32]{1,0:T(8,128)S(1)} fusion(f32[512,2,32]{2,1,0:T(2,128)S(1)} %bitcast.66, f32[512,2]{1,0:T(8,128)S(1)} %copy.62), kind=kLoop, calls=%fused_computation.20 | loop fusion | flops 49152 | bytes 200704 | tf_op jit(solution)/shard_map/reduce_sum | solution.py:93
  202.5 0.1 copy.63
  202.6 11.4 %all-gather.3 = f32[4,1,512]{2,1,0:T(1,128)S(1)} all-gather(f32[1,1,512]{2,1,0:T(1,128)S(1)} %bitcast.77), channel_id=2, replica_groups=mesh['ey'=1,'ec'=8,'mx'=4,'mza'=4,'mzb'=4] {'mzb'}, dimensions={0}, use_global_device_ids=true | all-gather | bytes 10240 | tf_op jit(solution)/shard_map/all_gather | solution.py:96
  214.0 14.4 %all-gather.4 = f32[4,1,512]{2,1,0:T(1,128)S(1)} all-gather(f32[1,1,512]{2,1,0:T(1,128)S(1)} %bitcast.78), channel_id=3, replica_groups=mesh['ey'=1,'ec'=8,'mx'=4,'mza'=4,'mzb'=4] {'mza'}, dimensions={0}, use_global_device_ids=true | all-gather | bytes 10240 | tf_op jit(solution)/shard_map/all_gather | solution.py:97
  228.5 8.5 %all-gather.5 = f32[4,1,512]{2,1,0:T(1,128)S(1)} all-gather(f32[1,1,512]{2,1,0:T(1,128)S(1)} %bitcast.79), channel_id=4, replica_groups=mesh['ey'=1,'ec'=8,'mx'=4,'mza'=4,'mzb'=4] {'mx'}, dimensions={0}, use_global_device_ids=true | all-gather | bytes 10240 | tf_op jit(solution)/shard_map/all_gather | solution.py:98
  237.0 0.1 multiply_convert_fusion
  237.1 29.5 %all_gather.43 = bf16[4096,32]{0,1:T(8,128)(2,1)S(1)} all-gather(bf16[512,32]{0,1:T(8,128)(2,1)S(1)} %multiply_convert_fusion), channel_id=1, replica_groups=mesh['ey'=1,'ec'=8,'mx'=4,'mza'=4,'mzb'=4] {'ey','ec'}, dimensions={0}, use_global_device_ids=true | all-gather | bytes 294912 | tf_op jit(solution)/shard_map/all_gather | solution.py:102
  266.5 0.5 copy.64
  267.0 1.3 gather_fusion.1
  268.3 0.7 copy.65
  (26 shorter events, 0.3 us)
Async XLA Ops:
  6.5 2.5 copy-start.1
  6.5 44.9 %copy-start = (bf16[32,2048]{1,0:T(8,128)(2,1)S(1)}, bf16[32,2048]{1,0:T(8,128)(2,1)}, u32[]{:S(2)}) copy-start(bf16[32,2048]{1,0:T(8,128)(2,1)} %param.10) | copy-start | bytes 393220
  6.5 125.0 %all-gather.8.cloned.1.call-start = ((), (), s32[]{:S(2)}) async-start(), calls=%async_computation.3 | async-start | bytes 9732096 | tf_op jit(solution)/shard_map/all_gather | solution.py:64
  6.5 61.1 %copy-start.2 = (s32[512,2]{0,1:T(2,128)S(1)}, s32[512,2]{0,1:T(2,128)}, u32[]{:S(2)}) copy-start(s32[512,2]{0,1:T(2,128)} %param.11) | copy-start | bytes 12292
  64.2 8.9 %all-to-all-start = ((f32[512,4,32]{0,2,1:T(8,128)}), f32[512,4,32]{0,2,1:T(8,128)S(1)}, u32[]{:S(2)}, u32[]{:S(2)}) async-start(f32[512,4,32]{0,2,1:T(8,128)} %bitcast.1), calls=%async_computation | async-start | bytes 524288 | tf_op jit(solution)/shard_map/all_to_all | solution.py:45
  140.3 12.8 %copy-start.3 = (f32[512,2]{0,1:T(2,128)S(1)}, f32[512,2]{0,1:T(2,128)}, u32[]{:S(2)}) copy-start(f32[512,2]{0,1:T(2,128)} %param.12) | copy-start | bytes 12292
  140.3 13.1 %copy-start.4 = (s32[512]{0:T(512)S(1)}, s32[512]{0:T(512)}, u32[]{:S(2)}) copy-start(s32[512]{0:T(512)} %param.17) | copy-start | bytes 6148
  141.6 54.7 %all-to-all-start.2 = ((bf16[256,64,32]{0,2,1:T(8,128)(2,1)}), bf16[256,64,32]{0,2,1:T(8,128)(2,1)S(1)}, u32[]{:S(2)}, u32[]{:S(2)}) async-start(bf16[256,64,32]{0,2,1:T(8,128)(2,1)} %bitcast.16), calls=%async_computation.2 | async-start | bytes 2097152 | tf_op jit(solution)/shard_map/all_to_all | solution.py:83
  196.8 40.1 %copy-start.5 = (f32[32]{0:T(128)S(1)}, f32[32]{0:T(128)}, u32[]{:S(2)}) copy-start(f32[32]{0:T(128)} %param.16) | copy-start | bytes 388
Sparse Core Ops, SparseCore 0:
  9.5 68.4 all-gather.7

commit v6 on v4

--- a/solution.py
+++ b/solution.py
@@ -34,7 +34,13 @@
     x_at = lax.axis_index("mx")
     along_z = lax.all_gather(context, "mz", axis=1, tiled=True)
     z_width = along_z.shape[1]
-    rows_x = lax.all_gather(out_proj, "mx", axis=0, tiled=True)
+    rows_x = lax.all_to_all(
+        jnp.broadcast_to(out_proj[None], (x_count,) + out_proj.shape),
+        "mx",
+        split_axis=0,
+        concat_axis=0,
+        tiled=True,
+    ).reshape(x_count * feat_local, model_width)
     rows_x = lax.dynamic_slice_in_dim(rows_x, x_at * z_width, z_width, axis=1)
     partial_attended = jnp.einsum(
         "td,cd->tc", along_z, rows_x, preferred_element_type=jnp.float32

time: 264 us -> 263 us (level)
  blocking collectives: 160 us -> 146 us
  starting transfers between devices: 13.3 us -> 19.4 us
  waiting for transfers between devices: 43 us -> 48.6 us
    all_gather x1 -> x0, blocking collectives: 11.1 us -> none  [shards(): rows_x = lax.all_gather(out_proj, 'mx', axis=0, tiled=True)]
    all_to_all x0 -> x1, starting transfers between devices: none -> 4.84 us  [shards(): lax.all_to_all(jnp.broadcast_to(out_proj[None], (x_count,) + out_proj.sha...]
    all_to_all x1, waiting for transfers between devices: 1.56 us -> 5.53 us  [shards(): lax.all_to_all(partial_attended.reshape(tok_rows, x_count, feat_local), '...]
  transfers between devices with their start and end apart: 3 -> 4, of which waited for: 2 -> 2; matrix products, arithmetic and copies ran while one was open for 5% -> 5% of each run, Pallas kernels for 0% -> 0%
where the time goes in v6:
time: 263 us; the launch traced here: 262 us
  blocking collectives  146 us (56%)
  waiting for transfers between devices  48.6 us (18%)
  starting transfers between devices  19.4 us (7%)
  local copies, waits for them, and re-layouts  16.4 us (6%)
  between operations  13.7 us (5%)
  matrix products  9.64 us (4%)
  other arithmetic  8.18 us (3%)
    all_to_all x1, blocking collectives, shards(): lax.all_to_all(outgoing, MP, split_axis=1, concat_axis=1, tiled=True)  50 us
    all_to_all x1, waiting for transfers between devices, shards(): lax.all_to_all(partial_value.astype(jnp.bfloat16), MP, split_axis=1, conc...  43 us
    all_gather x1, blocking collectives, shards(): along_z = lax.all_gather(context, 'mz', axis=1, tiled=True)  33.5 us
    all_gather x1, blocking collectives, shards(): everyone = lax.all_gather(normed, EX, axis=0, tiled=True)  32 us
    all_gather x1, blocking collectives, shards(): lax.all_gather(jnp.sum(combined * combined, axis=1), 'mz', axis=0)  21.8 us
    all_to_all x1, starting transfers between devices, shards(): lax.all_to_all(partial_value.astype(jnp.bfloat16), MP, split_axis=1, conc...  10.7 us
    all_gather x1, blocking collectives, shards(): squares = jnp.sum(lax.all_gather(squares, 'mx', axis=0), axis=0)  8.99 us
    scatter x1, local copies, waits for them, and re-layouts, shards(): slotted = jnp.zeros((EXPERTS * capacity, feat_local), jnp.bfloat16).at[de...  6.41 us
  transfers between devices with their start and end apart: 4, of which 2 were waited for; matrix products, arithmetic and copies ran while one was open for 5% of the time, Pallas kernels for 0%

profile of v6, /device:TPU:1, one launch (start us, length us, event | category | flops | bytes accessed | tf_op | source)
XLA Modules:
  0.0 262.2 jit_solution(9592055030657348600)
XLA Ops:
  6.5 2.4 pad_maximum_fusion
  9.0 0.0 all-gather.6.cloned.1.call-update
  9.0 0.0 copy-done
  9.0 0.9 broadcast_in_dim.10
  9.9 4.8 %all-to-all-start = ((bf16[4,32,2048]{2,1,0:T(8,128)(2,1)}), bf16[4,32,2048]{2,1,0:T(8,128)(2,1)S(1)}, u32[]{:S(2)}, u32[]{:S(2)}) async-start(bf16[4,32,2048]{2,1,0:T(8,128)(2,1)} %broadcast_in_dim.10), calls=%async_computation | async-start | bytes 1048576 | tf_op jit(solution)/shard_map/all_to_all | solution.py:37
  14.7 0.0 copy-done.2
  14.7 0.1 copy.55
  14.9 0.2 eq.29
  15.0 0.2 eq.25
  15.2 2.3 reduce-window.6
  17.5 0.3 slice_reduce_fusion
  17.8 0.2 reduce-window.9
  17.9 0.2 copy.54
  18.1 0.2 mul.59
  18.3 0.2 reshape.117
  18.5 0.1 add_bitcast_fusion
  18.6 33.5 %all_gather.21 = bf16[512,512]{0,1:T(8,128)(2,1)S(1)} all-gather(bf16[512,32]{0,1:T(8,128)(2,1)S(1)} %copy-done.1), channel_id=1, replica_groups=mesh['ey'=1,'ec'=8,'mx'=4,'mz'=16] {'mz'}, dimensions={1}, use_global_device_ids=true | all-gather | bytes 557056 | tf_op jit(solution)/shard_map/all_gather | solution.py:35
  52.2 0.0 all-to-all-done
  52.2 0.9 fusion.15
  53.1 3.8 %all-to-all-start.1 = ((f32[512,4,32]{0,2,1:T(8,128)}), f32[512,4,32]{0,2,1:T(8,128)S(1)}, u32[]{:S(2)}, u32[]{:S(2)}) async-start(f32[512,4,32]{0,2,1:T(8,128)} %bitcast.2), calls=%async_computation.1 | async-start | bytes 524288 | tf_op jit(solution)/shard_map/all_to_all | solution.py:49
  56.9 5.5 %all-to-all-done.1 = f32[512,4,32]{0,2,1:T(8,128)S(1)} async-done(((f32[512,4,32]{0,2,1:T(8,128)}), f32[512,4,32]{0,2,1:T(8,128)S(1)}, u32[]{:S(2)}, u32[]{:S(2)}) %all-to-all-start.1) | async-done | bytes 262176 | tf_op jit(solution)/shard_map/all_to_all | solution.py:49
  62.5 0.1 copy.57
  62.6 6.4 %scatter_custom_fusion = bf16[2048,32]{1,0:T(8,128)(2,1)S(1)} fusion(s32[1024]{0:T(1024)S(1)} %bitcast.74, bf16[512,32]{1,0:T(8,128)(2,1)S(1)} %copy.57, s32[1024]{0:T(1024)S(1)} %broadcast_clamp_fusion.1, bf16[]{:T(256)} %constant.18.clone.1), kind=kCustom, calls=%fused_computation.22 | custom fusion | bytes 131074 | tf_op jit(solution)/shard_map/scatter | solution.py:63
  69.0 0.2 copy.59
  69.2 0.1 broadcast_in_dim.13
  69.4 50.0 %all_to_all.32 = bf16[256,64,32]{0,2,1:T(8,128)(2,1)S(1)} all-to-all(bf16[256,64,32]{0,2,1:T(8,128)(2,1)S(1)} %bitcast.64), channel_id=1, replica_groups=mesh['ey'=1,'ec'=8,'mx'=4,'mz'=16] {'mx','mz'}, dimensions={1} | all-to-all | bytes 2097152 | tf_op jit(solution)/shard_map/all_to_all | solution.py:67
  119.4 2.7 %fusion.2 = f32[256,704]{0,1:T(8,128)S(1)} fusion(bf16[256,2048]{0,1:T(8,128)(2,1)S(1)} %bitcast.67, bf16[3,704,2048]{2,1,0:T(8,128)(2,1)} %all-gather.6.cloned.1.call-done), kind=kOutput, calls=%fused_computation.9 | convolution fusion | flops 738197504 | bytes 4653056 | tf_op jit(solution)/shard_map/rd,hd->rh/dot_general | solution.py:69
  122.1 6.0 %fusion.3 = bf16[256,2048]{1,0:T(8,128)(2,1)S(1)} fusion(bf16[3,704,2048]{2,1,0:T(8,128)(2,1)} %all-gather.6.cloned.1.call-done, bf16[256,2048]{0,1:T(8,128)(2,1)S(1)} %bitcast.68, f32[256,704]{0,1:T(8,128)S(1)} %fusion.2), kind=kOutput, calls=%fused_computation.10 | convolution fusion | flops 1478000640 | bytes 8585216 | tf_op jit(solution)/shard_map/dot_general | solution.py:82
  128.1 0.0 copy-start.3
  128.1 0.0 copy-start.4
  128.1 1.3 copy.60
  129.4 10.7 %all-to-all-start.3 = ((bf16[256,64,32]{0,2,1:T(8,128)(2,1)}), bf16[256,64,32]{0,2,1:T(8,128)(2,1)S(1)}, u32[]{:S(2)}, u32[]{:S(2)}) async-start(bf16[256,64,32]{0,2,1:T(8,128)(2,1)} %bitcast.17), calls=%async_computation.3 | async-start | bytes 2097152 | tf_op jit(solution)/shard_map/all_to_all | solution.py:87
  140.2 0.1 rev.3
  140.3 0.1 copy.62
  140.5 43.0 %all-to-all-done.3 = bf16[256,64,32]{0,2,1:T(8,128)(2,1)S(1)} async-done(((bf16[256,64,32]{0,2,1:T(8,128)(2,1)}), bf16[256,64,32]{0,2,1:T(8,128)(2,1)S(1)}, u32[]{:S(2)}, u32[]{:S(2)}) %all-to-all-start.3) | async-done | bytes 1048608 | tf_op jit(solution)/shard_map/all_to_all | solution.py:87
  183.6 0.2 bitcast_reduce_fusion
  183.8 0.3 copy.61
  184.1 0.0 copy-start.5
  184.1 2.8 %gather_fusion = f32[1024,32]{1,0:T(8,128)S(1)} fusion(f32[2048,32]{1,0:T(8,128)S(1)} %bitcast.63, s32[1024]{0:T(1024)S(1)} %broadcast_clamp_fusion), kind=kCustom, calls=%fused_computation.1 | custom fusion | bytes 266240 | tf_op jit(solution)/shard_map/gather | solution.py:95
  186.9 2.8 %multiply_reduce_fusion = f32[512,32]{1,0:T(8,128)S(1)} fusion(f32[512,2,32]{2,1,0:T(2,128)S(1)} %bitcast.66, f32[512,2]{1,0:T(8,128)S(1)} %copy.62), kind=kLoop, calls=%fused_computation.20 | loop fusion | flops 49152 | bytes 200704 | tf_op jit(solution)/shard_map/reduce_sum | solution.py:97
  189.7 0.1 copy.63
  189.9 21.8 %all-gather.2 = f32[16,1,512]{2,1,0:T(1,128)S(1)} all-gather(f32[1,1,512]{2,1,0:T(1,128)S(1)} %bitcast.79), channel_id=2, replica_groups=mesh['ey'=1,'ec'=8,'mx'=4,'mz'=16] {'mz'}, dimensions={0}, use_global_device_ids=true | all-gather | bytes 34816 | tf_op jit(solution)/shard_map/all_gather | solution.py:100
  211.7 9.0 %all-gather.3 = f32[4,1,512]{2,1,0:T(1,128)S(1)} all-gather(f32[1,1,512]{2,1,0:T(1,128)S(1)} %bitcast.78), channel_id=3, replica_groups=mesh['ey'=1,'ec'=8,'mx'=4,'mz'=16] {'mx'}, dimensions={0}, use_global_device_ids=true | all-gather | bytes 10240 | tf_op jit(solution)/shard_map/all_gather | solution.py:102
  220.8 0.1 multiply_convert_fusion
  220.8 32.0 %all_gather.27 = bf16[4096,32]{0,1:T(8,128)(2,1)S(1)} all-gather(bf16[512,32]{0,1:T(8,128)(2,1)S(1)} %multiply_convert_fusion), channel_id=1, replica_groups=mesh['ey'=1,'ec'=8,'mx'=4,'mz'=16] {'ey','ec'}, dimensions={0}, use_global_device_ids=true | all-gather | bytes 294912 | tf_op jit(solution)/shard_map/all_gather | solution.py:106
  252.8 0.5 copy.64
  253.3 1.3 gather_fusion.1
  254.7 0.7 copy.65
  (25 shorter events, 0.2 us)
Async XLA Ops:
  6.5 2.5 copy-start
  6.5 8.2 %copy-start.2 = (s32[512,2]{0,1:T(2,128)S(1)}, s32[512,2]{0,1:T(2,128)}, u32[]{:S(2)}) copy-start(s32[512,2]{0,1:T(2,128)} %param.11) | copy-start | bytes 12292
  6.5 112.8 %all-gather.6.cloned.1.call-start = ((), (), s32[]{:S(2)}) async-start(), calls=%async_computation.4 | async-start | bytes 9732096 | tf_op jit(solution)/shard_map/all_gather | solution.py:68
  9.0 9.7 %copy-start.1 = (bf16[512,32]{0,1:T(8,128)(2,1)S(1)}, bf16[512,32]{0,1:T(8,128)(2,1)}, u32[]{:S(2)}) copy-start(bf16[512,32]{0,1:T(8,128)(2,1)} %param.9) | copy-start | bytes 98308
  9.9 42.3 %all-to-all-start = ((bf16[4,32,2048]{2,1,0:T(8,128)(2,1)}), bf16[4,32,2048]{2,1,0:T(8,128)(2,1)S(1)}, u32[]{:S(2)}, u32[]{:S(2)}) async-start(bf16[4,32,2048]{2,1,0:T(8,128)(2,1)} %broadcast_in_dim.10), calls=%async_computation | async-start | bytes 1048576 | tf_op jit(solution)/shard_map/all_to_all | solution.py:37
  53.1 9.4 %all-to-all-start.1 = ((f32[512,4,32]{0,2,1:T(8,128)}), f32[512,4,32]{0,2,1:T(8,128)S(1)}, u32[]{:S(2)}, u32[]{:S(2)}) async-start(f32[512,4,32]{0,2,1:T(8,128)} %bitcast.2), calls=%async_computation.1 | async-start | bytes 524288 | tf_op jit(solution)/shard_map/all_to_all | solution.py:49
  128.1 12.1 %copy-start.3 = (f32[512,2]{0,1:T(2,128)S(1)}, f32[512,2]{0,1:T(2,128)}, u32[]{:S(2)}) copy-start(f32[512,2]{0,1:T(2,128)} %param.12) | copy-start | bytes 12292
  128.1 12.4 %copy-start.4 = (s32[512]{0:T(512)S(1)}, s32[512]{0:T(512)}, u32[]{:S(2)}) copy-start(s32[512]{0:T(512)} %param.17) | copy-start | bytes 6148
  129.4 54.2 %all-to-all-start.3 = ((bf16[256,64,32]{0,2,1:T(8,128)(2,1)}), bf16[256,64,32]{0,2,1:T(8,128)(2,1)S(1)}, u32[]{:S(2)}, u32[]{:S(2)}) async-start(bf16[256,64,32]{0,2,1:T(8,128)(2,1)} %bitcast.17), calls=%async_computation.3 | async-start | bytes 2097152 | tf_op jit(solution)/shard_map/all_to_all | solution.py:87
  184.1 36.7 %copy-start.5 = (f32[32]{0:T(128)S(1)}, f32[32]{0:T(128)}, u32[]{:S(2)}) copy-start(f32[32]{0:T(128)} %param.16) | copy-start | bytes 388
Sparse Core Ops, SparseCore 0:
  9.5 68.4 all-gather.5

commit v7 on v6

--- a/solution.py
+++ b/solution.py
@@ -32,7 +32,7 @@
     top_k = routes.shape[1]
     x_count = lax.axis_size("mx")
     x_at = lax.axis_index("mx")
-    along_z = lax.all_gather(context, "mz", axis=1, tiled=True)
+    along_z = lax.all_gather(context, MZ, axis=1, tiled=True)
     z_width = along_z.shape[1]
     rows_x = lax.all_to_all(
         jnp.broadcast_to(out_proj[None], (x_count,) + out_proj.shape),
@@ -62,9 +62,18 @@
         .at[destination]
         .set(attended[source_rows])
     )
-    slotted = jnp.repeat(slotted.reshape(EXPERTS, capacity, feat_local), copies, axis=0)
-    outgoing = slotted.transpose(1, 0, 2).reshape(capacity, mp_count * feat_local)
-    inbox_rows = lax.all_to_all(outgoing, MP, split_axis=1, concat_axis=1, tiled=True)
+    one_copy = lax.all_to_all(
+        slotted.reshape(EXPERTS, capacity, feat_local),
+        ("mx", "mzh"),
+        split_axis=0,
+        concat_axis=0,
+        tiled=True,
+    )
+    inbox_rows = (
+        lax.all_gather(one_copy, "mzl", axis=0)
+        .transpose(2, 1, 0, 3)
+        .reshape(capacity, mp_count * feat_local)
+    )
     stacked = lax.all_gather(jnp.stack([w_gate, w_up, w_down]), EX, axis=2, tiled=True)
     gate_next = jnp.einsum(
         "rd,hd->rh",
@@ -97,7 +106,7 @@
     branch = jnp.sum(picked * weights[:, :, None], axis=1)
     combined = attended.astype(jnp.float32) + branch
     squares = jnp.sum(
-        lax.all_gather(jnp.sum(combined * combined, axis=1), "mz", axis=0), axis=0
+        lax.all_gather(jnp.sum(combined * combined, axis=1), MZ, axis=0), axis=0
     )
     squares = jnp.sum(lax.all_gather(squares, "mx", axis=0), axis=0)
     normed = (
@@ -108,7 +117,8 @@
 
 
 EX = ("ey", "ec")
-MP = ("mx", "mz")
+MZ = ("mzh", "mzl")
+MP = ("mx",) + MZ
 
 
 def split_mesh(mesh):
@@ -119,8 +129,10 @@
         z_count = len({d.coords[2] for d in row})
     except (AttributeError, IndexError, TypeError):
         z_count = n_mp
+    group = n_mp // EXPERTS
     return Mesh(
-        devices.reshape(1, n_exp, n_mp // z_count, z_count), ("ey", "ec", "mx", "mz")
+        devices.reshape(1, n_exp, n_mp // z_count, z_count // group, group),
+        ("ey", "ec", "mx", "mzh", "mzl"),
     )
 
 

time: 263 us -> 366 us (1.39)
  waiting for transfers between devices: 48.6 us -> 182 us
  blocking collectives: 146 us -> 108 us
  starting transfers between devices: 19.4 us -> 24.5 us
    all_gather x1, waiting for transfers between devices: 0.01 us -> 64 us  [shards(): lax.all_gather(jnp.stack([w_gate, w_up, w_down]), EX, axis=2, tiled=True)]
    all_gather x0 -> x1, waiting for transfers between devices: none -> 62.6 us  [shards(): lax.all_gather(one_copy, 'mzl', axis=0).transpose(2, 1, 0, 3)]
    all_to_all x1, blocking collectives: 50 us -> 20.9 us  [shards(): lax.all_to_all(slotted.reshape(EXPERTS, capacity, feat_local), ('mx', 'mz...]
    all_gather x1, blocking collectives: 32 us -> 23.2 us  [shards(): everyone = lax.all_gather(normed, EX, axis=0, tiled=True)]
    all_to_all x1, waiting for transfers between devices: 43 us -> 50.3 us  [shards(): lax.all_to_all(partial_value.astype(jnp.bfloat16), MP, split_axis=1, conc...]
    all_to_all x1, starting transfers between devices: 10.7 us -> 15.5 us  [shards(): lax.all_to_all(partial_value.astype(jnp.bfloat16), MP, split_axis=1, conc...]
  transfers between devices with their start and end apart: 4 -> 5, of which waited for: 2 -> 4; matrix products, arithmetic and copies ran while one was open for 5% -> 2% of each run, Pallas kernels for 0% -> 0%
where the time goes in v7:
time: 366 us; the launch traced here: 365 us
  waiting for transfers between devices  182 us (50%)
  blocking collectives  108 us (30%)
  starting transfers between devices  24.5 us (7%)
  local copies, waits for them, and re-layouts  19.2 us (5%)
  between operations  13.7 us (4%)
  matrix products  9.63 us (3%)
  other arithmetic  7.73 us (2%)
    all_gather x1, waiting for transfers between devices, shards(): lax.all_gather(jnp.stack([w_gate, w_up, w_down]), EX, axis=2, tiled=True)  64 us
    all_gather x1, waiting for transfers between devices, shards(): lax.all_gather(one_copy, 'mzl', axis=0).transpose(2, 1, 0, 3)  62.6 us
    all_to_all x1, waiting for transfers between devices, shards(): lax.all_to_all(partial_value.astype(jnp.bfloat16), MP, split_axis=1, conc...  50.3 us
    all_gather x1, blocking collectives, shards(): along_z = lax.all_gather(context, MZ, axis=1, tiled=True)  31.9 us
    all_gather x1, blocking collectives, shards(): everyone = lax.all_gather(normed, EX, axis=0, tiled=True)  23.2 us
    all_gather x1, blocking collectives, shards(): lax.all_gather(jnp.sum(combined * combined, axis=1), MZ, axis=0)  22.4 us
    all_to_all x1, blocking collectives, shards(): lax.all_to_all(slotted.reshape(EXPERTS, capacity, feat_local), ('mx', 'mz...  20.9 us
    all_to_all x1, starting transfers between devices, shards(): lax.all_to_all(partial_value.astype(jnp.bfloat16), MP, split_axis=1, conc...  15.5 us
  transfers between devices with their start and end apart: 5, of which 4 were waited for; matrix products, arithmetic and copies ran while one was open for 2% of the time, Pallas kernels for 0%

profile of v7, /device:TPU:1, one launch (start us, length us, event | category | flops | bytes accessed | tf_op | source)
XLA Modules:
  0.0 365.1 jit_solution(336323215488150138)
XLA Ops:
  6.5 1.7 broadcast_in_dim.8
  8.3 4.8 %all-to-all-start = ((bf16[4,32,2048]{2,1,0:T(8,128)(2,1)}), bf16[4,32,2048]{2,1,0:T(8,128)(2,1)S(1)}, u32[]{:S(2)}, u32[]{:S(2)}) async-start(bf16[4,32,2048]{2,1,0:T(8,128)(2,1)} %broadcast_in_dim.8), calls=%async_computation | async-start | bytes 1048576 | tf_op jit(solution)/shard_map/all_to_all | solution.py:37
  13.1 0.8 copy.77
  14.0 0.2 eq.29
  14.2 0.0 copy-start.2
  14.2 0.2 eq.25
  14.3 0.8 broadcast_multiply_fusion
  15.1 2.3 reduce-window.6
  17.4 0.3 slice_reduce_fusion
  17.7 0.2 reduce-window.9
  17.8 0.1 add_bitcast_fusion
  17.9 0.2 copy.76
  18.1 0.2 mul.59
  18.3 0.2 reshape.113
  18.5 31.9 %all_gather.27 = bf16[512,512]{0,1:T(8,128)(2,1)S(1)} all-gather(bf16[512,32]{0,1:T(8,128)(2,1)S(1)} %copy-done.3), channel_id=1, replica_groups=mesh['ey'=1,'ec'=8,'mx'=4,'mzh'=2,'mzl'=8] {'mzh','mzl'}, dimensions={1}, use_global_device_ids=true | all-gather | bytes 557056 | tf_op jit(solution)/shard_map/all_gather | solution.py:35
  50.5 0.9 fusion.15
  51.4 4.1 %all-to-all-start.1 = ((f32[512,4,32]{0,2,1:T(8,128)}), f32[512,4,32]{0,2,1:T(8,128)S(1)}, u32[]{:S(2)}, u32[]{:S(2)}) async-start(f32[512,4,32]{0,2,1:T(8,128)} %bitcast.2), calls=%async_computation.1 | async-start | bytes 524288 | tf_op jit(solution)/shard_map/all_to_all | solution.py:49
  55.5 5.5 %all-to-all-done.1 = f32[512,4,32]{0,2,1:T(8,128)S(1)} async-done(((f32[512,4,32]{0,2,1:T(8,128)}), f32[512,4,32]{0,2,1:T(8,128)S(1)}, u32[]{:S(2)}, u32[]{:S(2)}) %all-to-all-start.1) | async-done | bytes 262176 | tf_op jit(solution)/shard_map/all_to_all | solution.py:49
  61.0 0.1 copy.79
  61.1 6.4 %scatter_custom_fusion = bf16[2048,32]{1,0:T(8,128)(2,1)S(1)} fusion(s32[1024]{0:T(1024)S(1)} %bitcast.74, bf16[512,32]{1,0:T(8,128)(2,1)S(1)} %copy.79, s32[1024]{0:T(1024)S(1)} %broadcast_clamp_fusion.1, bf16[]{:T(256)} %constant.18.clone.1), kind=kCustom, calls=%fused_computation.22 | custom fusion | bytes 131074 | tf_op jit(solution)/shard_map/scatter | solution.py:63
  67.5 0.2 copy.81
  67.7 20.9 %all_to_all.28 = bf16[8,256,32]{1,2,0:T(8,128)(2,1)} all-to-all(bf16[8,256,32]{1,2,0:T(8,128)(2,1)S(1)} %copy.81), channel_id=1, replica_groups=mesh['ey'=1,'ec'=8,'mx'=4,'mzh'=2,'mzl'=8] {'mx','mzh'}, dimensions={0} | all-to-all | bytes 262144 | tf_op jit(solution)/shard_map/all_to_all | solution.py:65
  88.7 0.0 all-gather.10.cloned.1.call-update
  88.7 0.0 all-gather.8.cloned.1.call-start
  88.8 1.2 pad_maximum_fusion
  90.0 0.0 all-gather.8.cloned.1.call-update
  90.0 62.6 %all-gather.10.cloned.1.call-done = bf16[64,256,32]{1,2,0:T(8,128)(2,1)} async-done(((bf16[8,256,32]{1,2,0:T(8,128)(2,1)}), bf16[64,256,32]{1,2,0:T(8,128)(2,1)}) %all-gather.10.cloned.1.call-update) | async-done | bytes 1048592 | tf_op jit(solution)/shard_map/all_gather | solution.py:73
  152.6 1.3 copy.82
  153.9 64.0 %all-gather.8.cloned.1.call-done = bf16[3,704,2048]{2,1,0:T(8,128)(2,1)} async-done(((bf16[3,704,256]{2,1,0:T(8,128)(2,1)}), bf16[3,704,2048]{2,1,0:T(8,128)(2,1)}) %all-gather.8.cloned.1.call-update) | async-done | bytes 8650768 | tf_op jit(solution)/shard_map/all_gather | solution.py:77
  217.9 2.7 fusion.2
  220.6 6.0 %fusion.3 = bf16[256,2048]{1,0:T(8,128)(2,1)S(1)} fusion(bf16[3,704,2048]{2,1,0:T(8,128)(2,1)} %all-gather.8.cloned.1.call-done, bf16[256,2048]{0,1:T(8,128)(2,1)S(1)} %bitcast.68, f32[256,704]{0,1:T(8,128)S(1)} %fusion.2), kind=kOutput, calls=%fused_computation.10 | convolution fusion | flops 1478000640 | bytes 8585216 | tf_op jit(solution)/shard_map/dot_general | solution.py:91
  226.6 1.3 copy.83
  227.9 15.5 %all-to-all-start.3 = ((bf16[256,64,32]{0,2,1:T(8,128)(2,1)}), bf16[256,64,32]{0,2,1:T(8,128)(2,1)S(1)}, u32[]{:S(2)}, u32[]{:S(2)}) async-start(bf16[256,64,32]{0,2,1:T(8,128)(2,1)} %bitcast.17), calls=%async_computation.3 | async-start | bytes 2097152 | tf_op jit(solution)/shard_map/all_to_all | solution.py:96
  243.5 0.1 rev.3
  243.6 0.1 copy.85
  243.8 50.3 %all-to-all-done.3 = bf16[256,64,32]{0,2,1:T(8,128)(2,1)S(1)} async-done(((bf16[256,64,32]{0,2,1:T(8,128)(2,1)}), bf16[256,64,32]{0,2,1:T(8,128)(2,1)S(1)}, u32[]{:S(2)}, u32[]{:S(2)}) %all-to-all-start.3) | async-done | bytes 1048608 | tf_op jit(solution)/shard_map/all_to_all | solution.py:96
  294.1 0.2 bitcast_reduce_fusion
  294.3 0.3 copy.84
  294.6 2.8 gather_fusion
  297.4 2.8 multiply_reduce_fusion
  300.3 0.1 copy.86
  300.4 22.4 %all-gather.3 = f32[16,1,512]{2,1,0:T(1,128)S(1)} all-gather(f32[1,1,512]{2,1,0:T(1,128)S(1)} %bitcast.79), channel_id=3, replica_groups=mesh['ey'=1,'ec'=8,'mx'=4,'mzh'=2,'mzl'=8] {'mzh','mzl'}, dimensions={0}, use_global_device_ids=true | all-gather | bytes 34816 | tf_op jit(solution)/shard_map/all_gather | solution.py:109
  322.8 9.5 %all-gather.4 = f32[4,1,512]{2,1,0:T(1,128)S(1)} all-gather(f32[1,1,512]{2,1,0:T(1,128)S(1)} %bitcast.78), channel_id=4, replica_groups=mesh['ey'=1,'ec'=8,'mx'=4,'mzh'=2,'mzl'=8] {'mx'}, dimensions={0}, use_global_device_ids=true | all-gather | bytes 10240 | tf_op jit(solution)/shard_map/all_gather | solution.py:111
  332.4 0.1 multiply_convert_fusion
  332.5 23.2 %all_gather.35 = bf16[4096,32]{0,1:T(8,128)(2,1)S(1)} all-gather(bf16[512,32]{0,1:T(8,128)(2,1)S(1)} %multiply_convert_fusion), channel_id=1, replica_groups=mesh['ey'=1,'ec'=8,'mx'=4,'mzh'=2,'mzl'=8] {'ey','ec'}, dimensions={0}, use_global_device_ids=true | all-gather | bytes 294912 | tf_op jit(solution)/shard_map/all_gather | solution.py:115
  355.8 0.5 copy.87
  356.2 1.3 gather_fusion.1
  357.6 0.7 copy.88
  (30 shorter events, 0.3 us)
Async XLA Ops:
  6.5 12.0 %copy-start.3 = (bf16[512,32]{0,1:T(8,128)(2,1)S(1)}, bf16[512,32]{0,1:T(8,128)(2,1)}, u32[]{:S(2)}) copy-start(bf16[512,32]{0,1:T(8,128)(2,1)} %param.9) | copy-start | bytes 98308
  8.3 42.2 %all-to-all-start = ((bf16[4,32,2048]{2,1,0:T(8,128)(2,1)}), bf16[4,32,2048]{2,1,0:T(8,128)(2,1)S(1)}, u32[]{:S(2)}, u32[]{:S(2)}) async-start(bf16[4,32,2048]{2,1,0:T(8,128)(2,1)} %broadcast_in_dim.8), calls=%async_computation | async-start | bytes 1048576 | tf_op jit(solution)/shard_map/all_to_all | solution.py:37
  14.1 74.6 %copy-start = (bf16[704,256]{1,0:T(8,128)(2,1)S(1)}, bf16[704,256]{1,0:T(8,128)(2,1)}, u32[]{:S(2)}) copy-start(bf16[704,256]{1,0:T(8,128)(2,1)} %param.15) | copy-start | bytes 1081348
  14.1 74.6 %copy-start.1 = (bf16[704,256]{1,0:T(8,128)(2,1)S(1)}, bf16[704,256]{1,0:T(8,128)(2,1)}, u32[]{:S(2)}) copy-start(bf16[704,256]{1,0:T(8,128)(2,1)} %param.14) | copy-start | bytes 1081348
  14.2 74.6 %copy-start.2 = (bf16[704,256]{1,0:T(8,128)(2,1)S(1)}, bf16[704,256]{1,0:T(8,128)(2,1)}, u32[]{:S(2)}) copy-start(bf16[704,256]{1,0:T(8,128)(2,1)} %param.13) | copy-start | bytes 1081348
  51.4 9.6 %all-to-all-start.1 = ((f32[512,4,32]{0,2,1:T(8,128)}), f32[512,4,32]{0,2,1:T(8,128)S(1)}, u32[]{:S(2)}, u32[]{:S(2)}) async-start(f32[512,4,32]{0,2,1:T(8,128)} %bitcast.2), calls=%async_computation.1 | async-start | bytes 524288 | tf_op jit(solution)/shard_map/all_to_all | solution.py:49
  55.4 97.1 %all-gather.10.cloned.1.call-start = ((), (), s32[]{:S(2)}) async-start(), calls=%async_computation.5 | async-start | bytes 1179648 | tf_op jit(solution)/shard_map/all_gather | solution.py:73
  88.7 129.2 %all-gather.8.cloned.1.call-start = ((), (), s32[]{:S(2)}) async-start(), calls=%async_computation.4 | async-start | bytes 9732096 | tf_op jit(solution)/shard_map/all_gather | solution.py:77
  226.6 16.9 %copy-start.4 = (f32[512,2]{0,1:T(2,128)S(1)}, f32[512,2]{0,1:T(2,128)}, u32[]{:S(2)}) copy-start(f32[512,2]{0,1:T(2,128)} %param.12) | copy-start | bytes 12292
  226.6 17.2 %copy-start.5 = (s32[512]{0:T(512)S(1)}, s32[512]{0:T(512)}, u32[]{:S(2)}) copy-start(s32[512]{0:T(512)} %param.17) | copy-start | bytes 6148
  227.9 66.2 %all-to-all-start.3 = ((bf16[256,64,32]{0,2,1:T(8,128)(2,1)}), bf16[256,64,32]{0,2,1:T(8,128)(2,1)S(1)}, u32[]{:S(2)}, u32[]{:S(2)}) async-start(bf16[256,64,32]{0,2,1:T(8,128)(2,1)} %bitcast.17), calls=%async_computation.3 | async-start | bytes 2097152 | tf_op jit(solution)/shard_map/all_to_all | solution.py:96
  294.6 37.8 %copy-start.6 = (f32[32]{0:T(128)S(1)}, f32[32]{0:T(128)}, u32[]{:S(2)}) copy-start(f32[32]{0:T(128)} %param.16) | copy-start | bytes 388
Sparse Core Ops, SparseCore 0:
  88.8 63.6 all-gather.9
  154.7 63.1 all-gather.7

commit v8 on v6

--- a/solution.py
+++ b/solution.py
@@ -56,11 +56,11 @@
         axis=1,
     ).astype(jnp.bfloat16)
     destination = slot_targets(routes, capacity, EXPERTS)
-    source_rows = jnp.repeat(jnp.arange(tok_rows, dtype=jnp.int32), top_k)
-    slotted = (
-        jnp.zeros((EXPERTS * capacity, feat_local), jnp.bfloat16)
-        .at[destination]
-        .set(attended[source_rows])
+    slot_ids = jnp.arange(EXPERTS * capacity, dtype=jnp.int32)
+    chosen = destination.reshape(tok_rows, top_k)[None, :, :] == slot_ids[:, None, None]
+    placing = jnp.any(chosen, axis=2).astype(jnp.bfloat16)
+    slotted = jnp.dot(placing, attended, preferred_element_type=jnp.float32).astype(
+        jnp.bfloat16
     )
     slotted = jnp.repeat(slotted.reshape(EXPERTS, capacity, feat_local), copies, axis=0)
     outgoing = slotted.transpose(1, 0, 2).reshape(capacity, mp_count * feat_local)
@@ -92,9 +92,13 @@
     ).reshape(
         EXPERTS * capacity, feat_local
     )
-    picked = expert_out[destination].reshape(tok_rows, top_k, feat_local)
     weights = 1.0 / (1.0 + jnp.exp(router_logits[:, ::-1] - router_logits))
-    branch = jnp.sum(picked * weights[:, :, None], axis=1)
+    picking = jnp.sum(
+        jnp.where(chosen, weights[None, :, :], 0.0), axis=2
+    ).T
+    branch = jnp.dot(
+        picking, expert_out, precision=lax.Precision.HIGHEST, preferred_element_type=jnp.float32
+    )
     combined = attended.astype(jnp.float32) + branch
     squares = jnp.sum(
         lax.all_gather(jnp.sum(combined * combined, axis=1), "mz", axis=0), axis=0

time: 263 us -> 256 us (0.973)
  local copies, waits for them, and re-layouts: 16.4 us -> 7.04 us
  waiting for transfers between devices: 48.6 us -> 41.6 us
  matrix products: 9.64 us -> 15.1 us
  other arithmetic: 8.18 us -> 12.5 us
    scatter x1 -> x0, local copies, waits for them, and re-layouts: 6.41 us -> none  [shards(): slotted = jnp.zeros((EXPERTS * capacity, feat_local), jnp.bfloat16).at[de...]
    dot_general x0 -> x2, matrix products: none -> 5.49 us  [the longest x1 4.76 us: shards(): jnp.dot(picking, expert_out, precision=lax.Precision.HIGHEST, preferred_e...]
    all_to_all x1, waiting for transfers between devices: 43 us -> 39.2 us  [shards(): lax.all_to_all(partial_value.astype(jnp.bfloat16), MP, split_axis=1, conc...]
    all_to_all x1, waiting for transfers between devices: 5.53 us -> 2.31 us  [shards(): lax.all_to_all(partial_attended.reshape(tok_rows, x_count, feat_local), '...]
    reduce_or x0 -> x1, other arithmetic: none -> 3.21 us  [shards(): placing = jnp.any(chosen, axis=2).astype(jnp.bfloat16)]
    gather x1 -> x0, local copies, waits for them, and re-layouts: 2.81 us -> none  [shards(): picked = expert_out[destination].reshape(tok_rows, top_k, feat_local)]
  transfers between devices with their start and end apart: 4 -> 4, of which waited for: 2 -> 2; matrix products, arithmetic and copies ran while one was open for 5% -> 6% of each run, Pallas kernels for 0% -> 0%
where the time goes in v8:
time: 256 us
  blocking collectives  146 us (57%)
  waiting for transfers between devices  41.6 us (16%)
  starting transfers between devices  19.7 us (8%)
  matrix products  15.1 us (6%)
  between operations  13.6 us (5%)
  other arithmetic  12.5 us (5%)
  local copies, waits for them, and re-layouts  7.04 us (3%)
    all_to_all x1, blocking collectives, shards(): lax.all_to_all(outgoing, MP, split_axis=1, concat_axis=1, tiled=True)  50 us
    all_to_all x1, waiting for transfers between devices, shards(): lax.all_to_all(partial_value.astype(jnp.bfloat16), MP, split_axis=1, conc...  39.2 us
    all_gather x1, blocking collectives, shards(): along_z = lax.all_gather(context, 'mz', axis=1, tiled=True)  33.2 us
    all_gather x1, blocking collectives, shards(): everyone = lax.all_gather(normed, EX, axis=0, tiled=True)  31.9 us
    all_gather x1, blocking collectives, shards(): lax.all_gather(jnp.sum(combined * combined, axis=1), 'mz', axis=0)  21.8 us
    all_to_all x1, starting transfers between devices, shards(): lax.all_to_all(partial_value.astype(jnp.bfloat16), MP, split_axis=1, conc...  10.7 us
    all_gather x1, blocking collectives, shards(): squares = jnp.sum(lax.all_gather(squares, 'mx', axis=0), axis=0)  8.99 us
    dot_general x1, matrix products, shards(): jnp.dot(activated, stacked[2], preferred_element_type=jnp.float32)  5.97 us
  transfers between devices with their start and end apart: 4, of which 2 were waited for; matrix products, arithmetic and copies ran while one was open for 6% of the time, Pallas kernels for 0%

profile of v8, /device:TPU:1, one launch (start us, length us, event | category | flops | bytes accessed | tf_op | source)
XLA Modules:
  0.0 255.5 jit_solution(4273797763994970304)
XLA Ops:
  6.5 0.0 copy-start.1
  6.5 0.0 copy-start
  6.5 0.0 all-gather.6.cloned.1.call-start
  6.5 2.4 pad_maximum_fusion
  8.9 0.0 all-gather.6.cloned.1.call-update
  9.0 1.8 broadcast_in_dim.18
  10.7 4.8 %all-to-all-start = ((bf16[4,32,2048]{2,1,0:T(8,128)(2,1)}), bf16[4,32,2048]{2,1,0:T(8,128)(2,1)S(1)}, u32[]{:S(2)}, u32[]{:S(2)}) async-start(bf16[4,32,2048]{2,1,0:T(8,128)(2,1)} %broadcast_in_dim.18), calls=%async_computation | async-start | bytes 1048576 | tf_op jit(solution)/shard_map/all_to_all | solution.py:37
  15.6 0.0 copy-done.1
  15.6 0.1 copy.53
  15.7 0.2 eq.42
  15.9 0.2 eq.38
  16.1 2.3 reduce-window.6
  18.4 0.3 slice_reduce_fusion
  18.6 0.2 reduce-window.9
  18.8 0.1 add_bitcast_fusion
  18.9 0.2 reduce_sum.67
  19.1 0.1 copy.55
  19.2 0.0 copy-done
  19.2 33.2 %all_gather.21 = bf16[512,512]{0,1:T(8,128)(2,1)S(1)} all-gather(bf16[512,32]{0,1:T(8,128)(2,1)S(1)} %copy-done), channel_id=1, replica_groups=mesh['ey'=1,'ec'=8,'mx'=4,'mz'=16] {'mz'}, dimensions={1}, use_global_device_ids=true | all-gather | bytes 557056 | tf_op jit(solution)/shard_map/all_gather | solution.py:35
  52.5 0.0 all-to-all-done
  52.5 0.9 fusion.13
  53.4 4.1 %all-to-all-start.1 = ((f32[512,4,32]{0,2,1:T(8,128)}), f32[512,4,32]{0,2,1:T(8,128)S(1)}, u32[]{:S(2)}, u32[]{:S(2)}) async-start(f32[512,4,32]{0,2,1:T(8,128)} %bitcast.2), calls=%async_computation.1 | async-start | bytes 524288 | tf_op jit(solution)/shard_map/all_to_all | solution.py:49
  57.6 3.2 %fusion = pred[2048,512]{1,0:T(8,128)(4,1)S(1)} fusion(s32[512,2]{0,1:T(2,128)S(1)} %multiply_add_fusion), kind=kLoop, calls=%fused_computation.3 | loop fusion | flops 3145728 | bytes 1052672 | tf_op jit(solution)/shard_map/reduce_or | solution.py:61
  60.8 2.3 all-to-all-done.1
  63.1 0.7 convolution_convert_fusion
  63.9 0.1 broadcast_in_dim.32
  64.0 50.0 %all_to_all.32 = bf16[256,64,32]{0,2,1:T(8,128)(2,1)S(1)} all-to-all(bf16[256,64,32]{0,2,1:T(8,128)(2,1)S(1)} %bitcast.67), channel_id=1, replica_groups=mesh['ey'=1,'ec'=8,'mx'=4,'mz'=16] {'mx','mz'}, dimensions={1} | all-to-all | bytes 2097152 | tf_op jit(solution)/shard_map/all_to_all | solution.py:67
  114.0 2.7 %fusion.3 = f32[256,704]{0,1:T(8,128)S(1)} fusion(bf16[256,2048]{0,1:T(8,128)(2,1)S(1)} %bitcast.70, bf16[3,704,2048]{2,1,0:T(8,128)(2,1)} %all-gather.6.cloned.1.call-done), kind=kOutput, calls=%fused_computation.9 | convolution fusion | flops 738197504 | bytes 4653056 | tf_op jit(solution)/shard_map/rd,hd->rh/dot_general | solution.py:69
  116.7 6.0 %fusion.4 = bf16[256,2048]{1,0:T(8,128)(2,1)S(1)} fusion(bf16[3,704,2048]{2,1,0:T(8,128)(2,1)} %all-gather.6.cloned.1.call-done, bf16[256,2048]{0,1:T(8,128)(2,1)S(1)} %bitcast.71, f32[256,704]{0,1:T(8,128)S(1)} %fusion.3), kind=kOutput, calls=%fused_computation.10 | convolution fusion | flops 1478000640 | bytes 8585216 | tf_op jit(solution)/shard_map/dot_general | solution.py:82
  122.7 0.0 copy-start.2
  122.7 0.0 copy-start.3
  122.7 1.3 copy.57
  124.1 10.7 %all-to-all-start.3 = ((bf16[256,64,32]{0,2,1:T(8,128)(2,1)}), bf16[256,64,32]{0,2,1:T(8,128)(2,1)S(1)}, u32[]{:S(2)}, u32[]{:S(2)}) async-start(bf16[256,64,32]{0,2,1:T(8,128)(2,1)} %bitcast.13), calls=%async_computation.3 | async-start | bytes 2097152 | tf_op jit(solution)/shard_map/all_to_all | solution.py:87
  134.8 0.0 copy-done.2
  134.8 0.1 rev.3
  135.0 0.0 copy-done.3
  135.0 4.0 %select_reduce_fusion = f32[2048,512]{1,0:T(8,128)} fusion(f32[512,2]{0,1:T(2,128)S(1)} %add_divide_fusion, s32[512,2]{0,1:T(2,128)S(1)} %multiply_add_fusion), kind=kLoop, calls=%fused_computation.1 | loop fusion | flops 5242880 | bytes 4202496 | tf_op jit(solution)/shard_map/reduce_sum | solution.py:96
  139.0 39.2 %all-to-all-done.3 = bf16[256,64,32]{0,2,1:T(8,128)(2,1)S(1)} async-done(((bf16[256,64,32]{0,2,1:T(8,128)(2,1)}), bf16[256,64,32]{0,2,1:T(8,128)(2,1)S(1)}, u32[]{:S(2)}, u32[]{:S(2)}) %all-to-all-start.3) | async-done | bytes 1048608 | tf_op jit(solution)/shard_map/all_to_all | solution.py:87
  178.2 0.2 bitcast_reduce_fusion
  178.4 4.8 %multiply_reduce_fusion = (f32[512]{0:T(512)S(1)}, f32[512,32]{0,1:T(8,128)S(1)}) fusion(f32[2048,512]{1,0:T(8,128)} %select_reduce_fusion, f32[2048,32]{0,1:T(8,128)S(1)} %bitcast.68, bf16[512,32]{0,1:T(8,128)(2,1)S(1)} %reduce_sum.65), kind=kOutput, calls=%fused_computation.27 | convolution fusion | flops 402718208 | bytes 4556800 | tf_op jit(solution)/shard_map/dot_general | solution.py:99
  183.2 21.8 %all-gather.2 = f32[16,1,512]{2,1,0:T(1,128)S(1)} all-gather(f32[1,1,512]{2,1,0:T(1,128)S(1)} %bitcast.79), channel_id=2, replica_groups=mesh['ey'=1,'ec'=8,'mx'=4,'mz'=16] {'mz'}, dimensions={0}, use_global_device_ids=true | all-gather | bytes 34816 | tf_op jit(solution)/shard_map/all_gather | solution.py:104
  205.1 9.0 %all-gather.3 = f32[4,1,512]{2,1,0:T(1,128)S(1)} all-gather(f32[1,1,512]{2,1,0:T(1,128)S(1)} %bitcast.80), channel_id=3, replica_groups=mesh['ey'=1,'ec'=8,'mx'=4,'mz'=16] {'mx'}, dimensions={0}, use_global_device_ids=true | all-gather | bytes 10240 | tf_op jit(solution)/shard_map/all_gather | solution.py:106
  214.1 0.0 copy-done.4
  214.1 0.1 multiply_convert_fusion
  214.2 31.9 %all_gather.27 = bf16[4096,32]{0,1:T(8,128)(2,1)S(1)} all-gather(bf16[512,32]{0,1:T(8,128)(2,1)S(1)} %multiply_convert_fusion), channel_id=1, replica_groups=mesh['ey'=1,'ec'=8,'mx'=4,'mz'=16] {'ey','ec'}, dimensions={0}, use_global_device_ids=true | all-gather | bytes 294912 | tf_op jit(solution)/shard_map/all_gather | solution.py:110
  246.1 0.5 copy.59
  246.6 1.3 gather_fusion
  248.0 0.7 copy.60
  (14 shorter events, 0.2 us)
Async XLA Ops:
  6.5 9.0 %copy-start.1 = (s32[512,2]{0,1:T(2,128)S(1)}, s32[512,2]{0,1:T(2,128)}, u32[]{:S(2)}) copy-start(s32[512,2]{0,1:T(2,128)} %param.11) | copy-start | bytes 12292
  6.5 12.7 %copy-start = (bf16[512,32]{0,1:T(8,128)(2,1)S(1)}, bf16[512,32]{0,1:T(8,128)(2,1)}, u32[]{:S(2)}) copy-start(bf16[512,32]{0,1:T(8,128)(2,1)} %param.9) | copy-start | bytes 98308
  6.5 107.5 %all-gather.6.cloned.1.call-start = ((), (), s32[]{:S(2)}) async-start(), calls=%async_computation.4 | async-start | bytes 9732096 | tf_op jit(solution)/shard_map/all_gather | solution.py:68
  10.7 41.7 %all-to-all-start = ((bf16[4,32,2048]{2,1,0:T(8,128)(2,1)}), bf16[4,32,2048]{2,1,0:T(8,128)(2,1)S(1)}, u32[]{:S(2)}, u32[]{:S(2)}) async-start(bf16[4,32,2048]{2,1,0:T(8,128)(2,1)} %broadcast_in_dim.18), calls=%async_computation | async-start | bytes 1048576 | tf_op jit(solution)/shard_map/all_to_all | solution.py:37
  53.4 9.7 %all-to-all-start.1 = ((f32[512,4,32]{0,2,1:T(8,128)}), f32[512,4,32]{0,2,1:T(8,128)S(1)}, u32[]{:S(2)}, u32[]{:S(2)}) async-start(f32[512,4,32]{0,2,1:T(8,128)} %bitcast.2), calls=%async_computation.1 | async-start | bytes 524288 | tf_op jit(solution)/shard_map/all_to_all | solution.py:49
  122.7 12.1 %copy-start.2 = (f32[512,2]{0,1:T(2,128)S(1)}, f32[512,2]{0,1:T(2,128)}, u32[]{:S(2)}) copy-start(f32[512,2]{0,1:T(2,128)} %param.12) | copy-start | bytes 12292
  122.7 12.2 %copy-start.3 = (s32[512]{0:T(512)S(1)}, s32[512]{0:T(512)}, u32[]{:S(2)}) copy-start(s32[512]{0:T(512)} %param.17) | copy-start | bytes 6148
  124.1 54.2 %all-to-all-start.3 = ((bf16[256,64,32]{0,2,1:T(8,128)(2,1)}), bf16[256,64,32]{0,2,1:T(8,128)(2,1)S(1)}, u32[]{:S(2)}, u32[]{:S(2)}) async-start(bf16[256,64,32]{0,2,1:T(8,128)(2,1)} %bitcast.13), calls=%async_computation.3 | async-start | bytes 2097152 | tf_op jit(solution)/shard_map/all_to_all | solution.py:87
  139.0 75.1 %copy-start.4 = (f32[32]{0:T(128)S(1)}, f32[32]{0:T(128)}, u32[]{:S(2)}) copy-start(f32[32]{0:T(128)} %param.16) | copy-start | bytes 388
Sparse Core Ops, SparseCore 0:
  9.5 68.4 all-gather.5

commit v9 on v8

--- a/solution.py
+++ b/solution.py
@@ -18,6 +18,12 @@
     earlier = jnp.cumsum(onehot, axis=0) - onehot
     slot_index = jnp.sum(earlier * onehot, axis=1)
     return flat_routes * capacity + slot_index
+
+
+def gather_sum(values, axis):
+    count = lax.axis_size(axis)
+    spread = jnp.broadcast_to(values[None], (count,) + values.shape)
+    return jnp.sum(lax.all_to_all(spread, axis, 0, 0, tiled=True), axis=0)
 
 
 def shards(
@@ -100,10 +106,9 @@
         picking, expert_out, precision=lax.Precision.HIGHEST, preferred_element_type=jnp.float32
     )
     combined = attended.astype(jnp.float32) + branch
-    squares = jnp.sum(
-        lax.all_gather(jnp.sum(combined * combined, axis=1), "mz", axis=0), axis=0
-    )
-    squares = jnp.sum(lax.all_gather(squares, "mx", axis=0), axis=0)
+    squares = jnp.sum(combined * combined, axis=1)
+    squares = gather_sum(squares, "mz")
+    squares = gather_sum(squares, "mx")
     normed = (
         combined * norm_gain[None, :] * lax.rsqrt(squares / model_width + epsilon)[:, None]
     ).astype(jnp.bfloat16)

time: 256 us -> 246 us (0.961)
  blocking collectives: 146 us -> 107 us
  waiting for transfers between devices: 41.6 us -> 57.5 us
  starting transfers between devices: 19.7 us -> 30.9 us
    all_gather x2 -> x0, blocking collectives: 30.8 us -> none  [the longest x1 21.8 us: shards(): lax.all_gather(jnp.sum(combined * combined, axis=1), 'mz', axis=0)]
    all_to_all x0 -> x2, waiting for transfers between devices: none -> 15.9 us  [gather_sum(): return jnp.sum(lax.all_to_all(spread, axis, 0, 0, tiled=True), axis=0)]
    all_to_all x0 -> x2, starting transfers between devices: none -> 11.1 us  [gather_sum(): return jnp.sum(lax.all_to_all(spread, axis, 0, 0, tiled=True), axis=0)]
    all_gather x1, blocking collectives: 31.9 us -> 24 us  [shards(): everyone = lax.all_gather(normed, EX, axis=0, tiled=True)]
  transfers between devices with their start and end apart: 4 -> 6, of which waited for: 2 -> 4; matrix products, arithmetic and copies ran while one was open for 6% -> 6% of each run, Pallas kernels for 0% -> 0%
where the time goes in v9:
time: 246 us; the launch traced here: 245 us
  blocking collectives  107 us (43%)
  waiting for transfers between devices  57.5 us (23%)
  starting transfers between devices  30.9 us (13%)
  matrix products  15.1 us (6%)
  between operations  13.6 us (6%)
  other arithmetic  12.5 us (5%)
  local copies, waits for them, and re-layouts  8.28 us (3%)
    all_to_all x1, blocking collectives, shards(): lax.all_to_all(outgoing, MP, split_axis=1, concat_axis=1, tiled=True)  50 us
    all_to_all x1, waiting for transfers between devices, shards(): lax.all_to_all(partial_value.astype(jnp.bfloat16), MP, split_axis=1, conc...  39.3 us
    all_gather x1, blocking collectives, shards(): along_z = lax.all_gather(context, 'mz', axis=1, tiled=True)  33.2 us
    all_gather x1, blocking collectives, shards(): everyone = lax.all_gather(normed, EX, axis=0, tiled=True)  24 us
    all_to_all x2, waiting for transfers between devices, gather_sum(): return jnp.sum(lax.all_to_all(spread, axis, 0, 0, tiled=True), axis=0)  15.9 us
    all_to_all x2, starting transfers between devices, gather_sum(): return jnp.sum(lax.all_to_all(spread, axis, 0, 0, tiled=True), axis=0)  11.1 us
    all_to_all x1, starting transfers between devices, shards(): lax.all_to_all(partial_value.astype(jnp.bfloat16), MP, split_axis=1, conc...  10.7 us
    dot_general x1, matrix products, shards(): jnp.dot(activated, stacked[2], preferred_element_type=jnp.float32)  5.97 us
  transfers between devices with their start and end apart: 6, of which 4 were waited for; matrix products, arithmetic and copies ran while one was open for 6% of the time, Pallas kernels for 0%

profile of v9, /device:TPU:1, one launch (start us, length us, event | category | flops | bytes accessed | tf_op | source)
XLA Modules:
  0.0 245.2 jit_solution(9263669151255068140)
XLA Ops:
  6.5 0.0 all-gather.2.cloned.1.call-start
  6.5 2.4 pad_maximum_fusion
  8.9 0.0 all-gather.2.cloned.1.call-update
  9.0 1.8 broadcast_in_dim.22
  10.7 4.8 %all-to-all-start = ((bf16[4,32,2048]{2,1,0:T(8,128)(2,1)}), bf16[4,32,2048]{2,1,0:T(8,128)(2,1)S(1)}, u32[]{:S(2)}, u32[]{:S(2)}) async-start(bf16[4,32,2048]{2,1,0:T(8,128)(2,1)} %broadcast_in_dim.22), calls=%async_computation | async-start | bytes 1048576 | tf_op jit(solution)/shard_map/all_to_all | solution.py:43
  15.6 0.0 copy-done.1
  15.6 0.1 copy.65
  15.7 0.2 eq.42
  15.9 0.2 eq.38
  16.1 2.3 reduce-window.6
  18.4 0.3 slice_reduce_fusion
  18.6 0.2 reduce-window.9
  18.8 0.1 add_bitcast_fusion
  18.9 0.2 reduce_sum.67
  19.1 0.1 copy.67
  19.2 0.0 copy-done
  19.2 33.2 %all_gather.9 = bf16[512,512]{0,1:T(8,128)(2,1)S(1)} all-gather(bf16[512,32]{0,1:T(8,128)(2,1)S(1)} %copy-done), channel_id=1, replica_groups=mesh['ey'=1,'ec'=8,'mx'=4,'mz'=16] {'mz'}, dimensions={1}, use_global_device_ids=true | all-gather | bytes 557056 | tf_op jit(solution)/shard_map/all_gather | solution.py:41
  52.5 0.0 all-to-all-done
  52.5 0.9 fusion.13
  53.4 4.1 %all-to-all-start.1 = ((f32[512,4,32]{0,2,1:T(8,128)}), f32[512,4,32]{0,2,1:T(8,128)S(1)}, u32[]{:S(2)}, u32[]{:S(2)}) async-start(f32[512,4,32]{0,2,1:T(8,128)} %bitcast.2), calls=%async_computation.1 | async-start | bytes 524288 | tf_op jit(solution)/shard_map/all_to_all | solution.py:55
  57.6 3.2 %fusion = pred[2048,512]{1,0:T(8,128)(4,1)S(1)} fusion(s32[512,2]{0,1:T(2,128)S(1)} %multiply_add_fusion), kind=kLoop, calls=%fused_computation.3 | loop fusion | flops 3145728 | bytes 1052672 | tf_op jit(solution)/shard_map/reduce_or | solution.py:67
  60.8 2.3 all-to-all-done.1
  63.1 0.7 convolution_convert_fusion
  63.9 0.1 broadcast_in_dim.25
  64.0 50.0 %all_to_all.44 = bf16[256,64,32]{0,2,1:T(8,128)(2,1)S(1)} all-to-all(bf16[256,64,32]{0,2,1:T(8,128)(2,1)S(1)} %bitcast.65), channel_id=1, replica_groups=mesh['ey'=1,'ec'=8,'mx'=4,'mz'=16] {'mx','mz'}, dimensions={1} | all-to-all | bytes 2097152 | tf_op jit(solution)/shard_map/all_to_all | solution.py:73
  114.0 2.7 %fusion.3 = f32[256,704]{0,1:T(8,128)S(1)} fusion(bf16[256,2048]{0,1:T(8,128)(2,1)S(1)} %bitcast.68, bf16[3,704,2048]{2,1,0:T(8,128)(2,1)} %all-gather.2.cloned.1.call-done), kind=kOutput, calls=%fused_computation.9 | convolution fusion | flops 738197504 | bytes 4653056 | tf_op jit(solution)/shard_map/rd,hd->rh/dot_general | solution.py:75
  116.7 6.0 %fusion.4 = bf16[256,2048]{1,0:T(8,128)(2,1)S(1)} fusion(bf16[3,704,2048]{2,1,0:T(8,128)(2,1)} %all-gather.2.cloned.1.call-done, bf16[256,2048]{0,1:T(8,128)(2,1)S(1)} %bitcast.69, f32[256,704]{0,1:T(8,128)S(1)} %fusion.3), kind=kOutput, calls=%fused_computation.10 | convolution fusion | flops 1478000640 | bytes 8585216 | tf_op jit(solution)/shard_map/dot_general | solution.py:88
  122.7 0.0 copy-start.2
  122.7 1.3 copy.69
  124.1 10.7 %all-to-all-start.3 = ((bf16[256,64,32]{0,2,1:T(8,128)(2,1)}), bf16[256,64,32]{0,2,1:T(8,128)(2,1)S(1)}, u32[]{:S(2)}, u32[]{:S(2)}) async-start(bf16[256,64,32]{0,2,1:T(8,128)(2,1)} %bitcast.13), calls=%async_computation.3 | async-start | bytes 2097152 | tf_op jit(solution)/shard_map/all_to_all | solution.py:93
  134.8 0.0 copy-done.2
  134.8 0.1 rev.3
  135.0 4.0 %select_reduce_fusion = f32[2048,512]{1,0:T(8,128)} fusion(f32[512,2]{0,1:T(2,128)S(1)} %add_divide_fusion, s32[512,2]{0,1:T(2,128)S(1)} %multiply_add_fusion), kind=kLoop, calls=%fused_computation.1 | loop fusion | flops 5242880 | bytes 4202496 | tf_op jit(solution)/shard_map/reduce_sum | solution.py:102
  139.0 39.3 %all-to-all-done.3 = bf16[256,64,32]{0,2,1:T(8,128)(2,1)S(1)} async-done(((bf16[256,64,32]{0,2,1:T(8,128)(2,1)}), bf16[256,64,32]{0,2,1:T(8,128)(2,1)S(1)}, u32[]{:S(2)}, u32[]{:S(2)}) %all-to-all-start.3) | async-done | bytes 1048608 | tf_op jit(solution)/shard_map/all_to_all | solution.py:93
  178.2 0.2 bitcast_reduce_fusion
  178.4 4.8 %multiply_reduce_fusion = (f32[512]{0:T(512)S(1)}, f32[512,32]{0,1:T(8,128)S(1)}) fusion(f32[2048,512]{1,0:T(8,128)} %select_reduce_fusion, f32[2048,32]{0,1:T(8,128)S(1)} %bitcast.66, bf16[512,32]{0,1:T(8,128)(2,1)S(1)} %reduce_sum.65), kind=kOutput, calls=%fused_computation.27 | convolution fusion | flops 402718208 | bytes 4556800 | tf_op jit(solution)/shard_map/dot_general | solution.py:105
  183.2 0.6 broadcast_in_dim.26
  183.8 7.5 %all-to-all-start.4 = ((f32[16,1,512]{2,1,0:T(1,128)}), f32[16,1,512]{2,1,0:T(1,128)S(1)}, u32[]{:S(2)}, u32[]{:S(2)}) async-start(f32[16,1,512]{2,1,0:T(1,128)} %broadcast_in_dim.26), calls=%async_computation.4 | async-start | bytes 65536 | tf_op jit(solution)/shard_map/all_to_all | solution.py:26
  191.3 0.0 copy-done.3
  191.3 11.5 %all-to-all-done.4 = f32[16,1,512]{2,1,0:T(1,128)S(1)} async-done(((f32[16,1,512]{2,1,0:T(1,128)}), f32[16,1,512]{2,1,0:T(1,128)S(1)}, u32[]{:S(2)}, u32[]{:S(2)}) %all-to-all-start.4) | async-done | bytes 32800 | tf_op jit(solution)/shard_map/all_to_all | solution.py:26
  202.8 0.6 broadcast_in_dim.46
  203.4 3.7 %all-to-all-start.5 = ((f32[4,1,512]{2,1,0:T(1,128)}), f32[4,1,512]{2,1,0:T(1,128)S(1)}, u32[]{:S(2)}, u32[]{:S(2)}) async-start(f32[4,1,512]{2,1,0:T(1,128)} %broadcast_in_dim.46), calls=%async_computation.5 | async-start | bytes 16384 | tf_op jit(solution)/shard_map/all_to_all | solution.py:26
  207.1 4.5 %all-to-all-done.5 = f32[4,1,512]{2,1,0:T(1,128)S(1)} async-done(((f32[4,1,512]{2,1,0:T(1,128)}), f32[4,1,512]{2,1,0:T(1,128)S(1)}, u32[]{:S(2)}, u32[]{:S(2)}) %all-to-all-start.5) | async-done | bytes 8224 | tf_op jit(solution)/shard_map/all_to_all | solution.py:26
  211.6 0.1 multiply_convert_fusion
  211.7 24.0 %all_gather.11 = bf16[4096,32]{0,1:T(8,128)(2,1)S(1)} all-gather(bf16[512,32]{0,1:T(8,128)(2,1)S(1)} %multiply_convert_fusion), channel_id=1, replica_groups=mesh['ey'=1,'ec'=8,'mx'=4,'mz'=16] {'ey','ec'}, dimensions={0}, use_global_device_ids=true | all-gather | bytes 294912 | tf_op jit(solution)/shard_map/all_gather | solution.py:115
  235.7 0.5 copy.73
  236.3 1.3 gather_fusion
  237.6 0.7 copy.74
  (18 shorter events, 0.2 us)
Async XLA Ops:
  6.5 9.0 %copy-start.1 = (s32[512,2]{0,1:T(2,128)S(1)}, s32[512,2]{0,1:T(2,128)}, u32[]{:S(2)}) copy-start(s32[512,2]{0,1:T(2,128)} %param.11) | copy-start | bytes 12292
  6.5 12.7 %copy-start = (bf16[512,32]{0,1:T(8,128)(2,1)S(1)}, bf16[512,32]{0,1:T(8,128)(2,1)}, u32[]{:S(2)}) copy-start(bf16[512,32]{0,1:T(8,128)(2,1)} %param.9) | copy-start | bytes 98308
  6.5 107.5 %all-gather.2.cloned.1.call-start = ((), (), s32[]{:S(2)}) async-start(), calls=%async_computation.6 | async-start | bytes 9732096 | tf_op jit(solution)/shard_map/all_gather | solution.py:74
  10.7 41.7 %all-to-all-start = ((bf16[4,32,2048]{2,1,0:T(8,128)(2,1)}), bf16[4,32,2048]{2,1,0:T(8,128)(2,1)S(1)}, u32[]{:S(2)}, u32[]{:S(2)}) async-start(bf16[4,32,2048]{2,1,0:T(8,128)(2,1)} %broadcast_in_dim.22), calls=%async_computation | async-start | bytes 1048576 | tf_op jit(solution)/shard_map/all_to_all | solution.py:43
  53.4 9.7 %all-to-all-start.1 = ((f32[512,4,32]{0,2,1:T(8,128)}), f32[512,4,32]{0,2,1:T(8,128)S(1)}, u32[]{:S(2)}, u32[]{:S(2)}) async-start(f32[512,4,32]{0,2,1:T(8,128)} %bitcast.2), calls=%async_computation.1 | async-start | bytes 524288 | tf_op jit(solution)/shard_map/all_to_all | solution.py:55
  122.7 12.1 %copy-start.2 = (f32[512,2]{0,1:T(2,128)S(1)}, f32[512,2]{0,1:T(2,128)}, u32[]{:S(2)}) copy-start(f32[512,2]{0,1:T(2,128)} %param.12) | copy-start | bytes 12292
  124.1 54.2 %all-to-all-start.3 = ((bf16[256,64,32]{0,2,1:T(8,128)(2,1)}), bf16[256,64,32]{0,2,1:T(8,128)(2,1)S(1)}, u32[]{:S(2)}, u32[]{:S(2)}) async-start(bf16[256,64,32]{0,2,1:T(8,128)(2,1)} %bitcast.13), calls=%async_computation.3 | async-start | bytes 2097152 | tf_op jit(solution)/shard_map/all_to_all | solution.py:93
  139.0 52.3 %copy-start.3 = (s32[512]{0:T(512)S(1)}, s32[512]{0:T(512)}, u32[]{:S(2)}) copy-start(s32[512]{0:T(512)} %param.17) | copy-start | bytes 6148
  139.0 72.6 %copy-start.4 = (f32[32]{0:T(128)S(1)}, f32[32]{0:T(128)}, u32[]{:S(2)}) copy-start(f32[32]{0:T(128)} %param.16) | copy-start | bytes 388
  183.8 18.9 %all-to-all-start.4 = ((f32[16,1,512]{2,1,0:T(1,128)}), f32[16,1,512]{2,1,0:T(1,128)S(1)}, u32[]{:S(2)}, u32[]{:S(2)}) async-start(f32[16,1,512]{2,1,0:T(1,128)} %broadcast_in_dim.26), calls=%async_computation.4 | async-start | bytes 65536 | tf_op jit(solution)/shard_map/all_to_all | solution.py:26
  203.4 8.2 %all-to-all-start.5 = ((f32[4,1,512]{2,1,0:T(1,128)}), f32[4,1,512]{2,1,0:T(1,128)S(1)}, u32[]{:S(2)}, u32[]{:S(2)}) async-start(f32[4,1,512]{2,1,0:T(1,128)} %broadcast_in_dim.46), calls=%async_computation.5 | async-start | bytes 16384 | tf_op jit(solution)/shard_map/all_to_all | solution.py:26
Sparse Core Ops, SparseCore 0:
  9.5 68.4 all-gather.1

commit v10 on v9

--- a/solution.py
+++ b/solution.py
@@ -38,7 +38,15 @@
     top_k = routes.shape[1]
     x_count = lax.axis_size("mx")
     x_at = lax.axis_index("mx")
-    along_z = lax.all_gather(context, "mz", axis=1, tiled=True)
+    z_count = lax.axis_size("mz")
+    along_z = lax.all_to_all(
+        jnp.broadcast_to(context[None], (z_count,) + context.shape),
+        "mz",
+        split_axis=0,
+        concat_axis=0,
+        tiled=True,
+    )
+    along_z = along_z.transpose(1, 0, 2).reshape(tok_rows, z_count * feat_local)
     z_width = along_z.shape[1]
     rows_x = lax.all_to_all(
         jnp.broadcast_to(out_proj[None], (x_count,) + out_proj.shape),
@@ -112,7 +120,14 @@
     normed = (
         combined * norm_gain[None, :] * lax.rsqrt(squares / model_width + epsilon)[:, None]
     ).astype(jnp.bfloat16)
-    everyone = lax.all_gather(normed, EX, axis=0, tiled=True)
+    ex_count = lax.axis_size(EX)
+    everyone = lax.all_to_all(
+        jnp.broadcast_to(normed[None], (ex_count,) + normed.shape),
+        EX,
+        split_axis=0,
+        concat_axis=0,
+        tiled=True,
+    ).reshape(ex_count * tok_rows, feat_local)
     return everyone[request_order]
 
 

time: 246 us -> 264 us (1.073)
  waiting for transfers between devices: 57.5 us -> 73.3 us
  starting transfers between devices: 30.9 us -> 40 us
  blocking collectives: 107 us -> 101 us
    all_gather x2 -> x0, blocking collectives: 57.3 us -> none  [the longest x1 33.2 us: shards(): along_z = lax.all_gather(context, 'mz', axis=1, tiled=True)]
    all_to_all x0 -> x3, blocking collectives: none -> 38 us  [the longest x2 26.4 us: gather_sum(): return jnp.sum(lax.all_to_all(spread, axis, 0, 0, tiled=True), axis=0)]
    all_to_all x1, blocking collectives: 50 us -> 62.9 us  [shards(): lax.all_to_all(outgoing, MP, split_axis=1, concat_axis=1, tiled=True)]
    all_to_all x3 -> x2, waiting for transfers between devices: 15.9 us -> 24.8 us  [the longest x1 18.4 us: shards(): lax.all_to_all(jnp.broadcast_to(context[None], (z_count,) + context.shape...]
    all_to_all x3 -> x2, starting transfers between devices: 16 us -> 24.7 us  [the longest x1 16.5 us: shards(): lax.all_to_all(jnp.broadcast_to(context[None], (z_count,) + context.shape...]
    all_to_all x1, waiting for transfers between devices: 39.3 us -> 46.1 us  [shards(): lax.all_to_all(partial_value.astype(jnp.bfloat16), MP, split_axis=1, conc...]
  transfers between devices with their start and end apart: 6 -> 5, of which waited for: 4 -> 4; matrix products, arithmetic and copies ran while one was open for 6% -> 6% of each run, Pallas kernels for 0% -> 0%
where the time goes in v10:
time: 264 us; the launch traced here: 263 us
  blocking collectives  101 us (38%)
  waiting for transfers between devices  73.3 us (28%)
  starting transfers between devices  40 us (15%)
  matrix products  15.1 us (6%)
  between operations  13.6 us (5%)
  other arithmetic  12.5 us (5%)
  local copies, waits for them, and re-layouts  7.83 us (3%)
    all_to_all x1, blocking collectives, shards(): lax.all_to_all(outgoing, MP, split_axis=1, concat_axis=1, tiled=True)  62.9 us
    all_to_all x1, waiting for transfers between devices, shards(): lax.all_to_all(partial_value.astype(jnp.bfloat16), MP, split_axis=1, conc...  46.1 us
    all_to_all x2, blocking collectives, gather_sum(): return jnp.sum(lax.all_to_all(spread, axis, 0, 0, tiled=True), axis=0)  26.4 us
    all_to_all x1, waiting for transfers between devices, shards(): lax.all_to_all(jnp.broadcast_to(context[None], (z_count,) + context.shape...  18.4 us
    all_to_all x1, starting transfers between devices, shards(): lax.all_to_all(jnp.broadcast_to(context[None], (z_count,) + context.shape...  16.5 us
    all_to_all x1, starting transfers between devices, shards(): lax.all_to_all(partial_value.astype(jnp.bfloat16), MP, split_axis=1, conc...  11.9 us
    all_to_all x1, blocking collectives, shards(): lax.all_to_all(jnp.broadcast_to(out_proj[None], (x_count,) + out_proj.sha...  11.6 us
    all_to_all x1, starting transfers between devices, shards(): lax.all_to_all(jnp.broadcast_to(normed[None], (ex_count,) + normed.shape)...  8.13 us
  transfers between devices with their start and end apart: 5, of which 4 were waited for; matrix products, arithmetic and copies ran while one was open for 6% of the time, Pallas kernels for 0%

profile of v10, /device:TPU:1, one launch (start us, length us, event | category | flops | bytes accessed | tf_op | source)
XLA Modules:
  0.0 263.2 jit_solution(15559189454654920151)
XLA Ops:
  6.5 0.0 all-gather.2.cloned.1.call-start
  6.5 2.4 pad_maximum_fusion
  8.9 0.0 all-gather.2.cloned.1.call-update
  9.0 1.0 broadcast_in_dim.26
  9.9 11.6 %all_to_all.54 = bf16[4,32,2048]{2,1,0:T(8,128)(2,1)S(1)} all-to-all(bf16[4,32,2048]{2,1,0:T(8,128)(2,1)S(1)} %broadcast_in_dim.26), channel_id=1, replica_groups=mesh['ey'=1,'ec'=8,'mx'=4,'mz'=16] {'mx'}, dimensions={0} | all-to-all | bytes 1048576 | tf_op jit(solution)/shard_map/all_to_all | solution.py:51
  21.5 0.0 copy-done
  21.5 0.9 broadcast_in_dim.27
  22.4 16.5 %all-to-all-start.1 = ((bf16[16,512,32]{1,2,0:T(8,128)(2,1)}), bf16[16,512,32]{1,2,0:T(8,128)(2,1)S(1)}, u32[]{:S(2)}, u32[]{:S(2)}) async-start(bf16[16,512,32]{1,2,0:T(8,128)(2,1)} %broadcast_in_dim.27), calls=%async_computation.1 | async-start | bytes 1048576 | tf_op jit(solution)/shard_map/all_to_all | solution.py:42
  38.9 0.0 copy-done.1
  38.9 0.1 copy.66
  39.1 0.2 eq.42
  39.3 0.2 eq.38
  39.5 2.3 reduce-window.6
  41.7 0.3 slice_reduce_fusion
  42.0 0.2 reduce-window.9
  42.2 0.1 add_bitcast_fusion
  42.3 0.2 reduce_sum.67
  42.5 0.1 copy.68
  42.6 18.4 %all-to-all-done.1 = bf16[16,512,32]{1,2,0:T(8,128)(2,1)S(1)} async-done(((bf16[16,512,32]{1,2,0:T(8,128)(2,1)}), bf16[16,512,32]{1,2,0:T(8,128)(2,1)S(1)}, u32[]{:S(2)}, u32[]{:S(2)}) %all-to-all-start.1) | async-done | bytes 524320 | tf_op jit(solution)/shard_map/all_to_all | solution.py:42
  61.0 0.9 fusion.13
  61.9 3.4 %all-to-all-start.2 = ((f32[512,4,32]{0,2,1:T(8,128)}), f32[512,4,32]{0,2,1:T(8,128)S(1)}, u32[]{:S(2)}, u32[]{:S(2)}) async-start(f32[512,4,32]{0,2,1:T(8,128)} %bitcast.4), calls=%async_computation.2 | async-start | bytes 524288 | tf_op jit(solution)/shard_map/all_to_all | solution.py:63
  65.3 3.2 %fusion = pred[2048,512]{1,0:T(8,128)(4,1)S(1)} fusion(s32[512,2]{0,1:T(2,128)S(1)} %multiply_add_fusion), kind=kLoop, calls=%fused_computation.3 | loop fusion | flops 3145728 | bytes 1052672 | tf_op jit(solution)/shard_map/reduce_or | solution.py:75
  68.5 2.3 all-to-all-done.2
  70.8 0.7 convolution_convert_fusion
  71.6 0.1 broadcast_in_dim.30
  71.7 62.9 %all_to_all.55 = bf16[256,64,32]{0,2,1:T(8,128)(2,1)S(1)} all-to-all(bf16[256,64,32]{0,2,1:T(8,128)(2,1)S(1)} %bitcast.70), channel_id=1, replica_groups=mesh['ey'=1,'ec'=8,'mx'=4,'mz'=16] {'mx','mz'}, dimensions={1} | all-to-all | bytes 2097152 | tf_op jit(solution)/shard_map/all_to_all | solution.py:81
  134.6 2.7 %fusion.3 = f32[256,704]{0,1:T(8,128)S(1)} fusion(bf16[256,2048]{0,1:T(8,128)(2,1)S(1)} %bitcast.74, bf16[3,704,2048]{2,1,0:T(8,128)(2,1)} %all-gather.2.cloned.1.call-done), kind=kOutput, calls=%fused_computation.9 | convolution fusion | flops 738197504 | bytes 4653056 | tf_op jit(solution)/shard_map/rd,hd->rh/dot_general | solution.py:83
  137.4 6.0 %fusion.4 = bf16[256,2048]{1,0:T(8,128)(2,1)S(1)} fusion(bf16[3,704,2048]{2,1,0:T(8,128)(2,1)} %all-gather.2.cloned.1.call-done, bf16[256,2048]{0,1:T(8,128)(2,1)S(1)} %bitcast.75, f32[256,704]{0,1:T(8,128)S(1)} %fusion.3), kind=kOutput, calls=%fused_computation.10 | convolution fusion | flops 1478000640 | bytes 8585216 | tf_op jit(solution)/shard_map/dot_general | solution.py:96
  143.4 0.0 copy-start.2
  143.4 1.3 copy.70
  144.7 11.9 %all-to-all-start.4 = ((bf16[256,64,32]{0,2,1:T(8,128)(2,1)}), bf16[256,64,32]{0,2,1:T(8,128)(2,1)S(1)}, u32[]{:S(2)}, u32[]{:S(2)}) async-start(bf16[256,64,32]{0,2,1:T(8,128)(2,1)} %bitcast.15), calls=%async_computation.4 | async-start | bytes 2097152 | tf_op jit(solution)/shard_map/all_to_all | solution.py:101
  156.6 0.0 copy-done.2
  156.6 0.1 rev.3
  156.8 4.0 %select_reduce_fusion = f32[2048,512]{1,0:T(8,128)} fusion(f32[512,2]{0,1:T(2,128)S(1)} %add_divide_fusion, s32[512,2]{0,1:T(2,128)S(1)} %multiply_add_fusion), kind=kLoop, calls=%fused_computation.1 | loop fusion | flops 5242880 | bytes 4202496 | tf_op jit(solution)/shard_map/reduce_sum | solution.py:110
  160.8 46.1 %all-to-all-done.4 = bf16[256,64,32]{0,2,1:T(8,128)(2,1)S(1)} async-done(((bf16[256,64,32]{0,2,1:T(8,128)(2,1)}), bf16[256,64,32]{0,2,1:T(8,128)(2,1)S(1)}, u32[]{:S(2)}, u32[]{:S(2)}) %all-to-all-start.4) | async-done | bytes 1048608 | tf_op jit(solution)/shard_map/all_to_all | solution.py:101
  206.9 0.2 bitcast_reduce_fusion
  207.1 4.8 %multiply_reduce_fusion = (f32[512]{0:T(512)S(1)}, f32[512,32]{0,1:T(8,128)S(1)}) fusion(f32[2048,512]{1,0:T(8,128)} %select_reduce_fusion, f32[2048,32]{0,1:T(8,128)S(1)} %bitcast.72, bf16[512,32]{0,1:T(8,128)(2,1)S(1)} %reduce_sum.65), kind=kOutput, calls=%fused_computation.27 | convolution fusion | flops 402718208 | bytes 4556800 | tf_op jit(solution)/shard_map/dot_general | solution.py:113
  211.9 19.9 %all_to_all.56 = f32[16,1,512]{2,1,0:T(1,128)S(1)} all-to-all(f32[16,1,512]{2,1,0:T(1,128)S(1)} %broadcast_in_dim.31), channel_id=1, replica_groups=mesh['ey'=1,'ec'=8,'mx'=4,'mz'=16] {'mz'}, dimensions={0} | all-to-all | bytes 65536 | tf_op jit(solution)/shard_map/all_to_all | solution.py:26
  231.8 6.5 %all_to_all.57 = f32[4,1,512]{2,1,0:T(1,128)S(1)} all-to-all(f32[4,1,512]{2,1,0:T(1,128)S(1)} %broadcast_in_dim.32), channel_id=1, replica_groups=mesh['ey'=1,'ec'=8,'mx'=4,'mz'=16] {'mx'}, dimensions={0} | all-to-all | bytes 16384 | tf_op jit(solution)/shard_map/all_to_all | solution.py:26
  238.4 0.0 copy-done.4
  238.4 0.1 multiply_convert_fusion
  238.5 0.7 broadcast_in_dim.33
  239.2 8.1 %all-to-all-start.7 = ((bf16[8,512,32]{1,2,0:T(8,128)(2,1)}), bf16[8,512,32]{1,2,0:T(8,128)(2,1)S(1)}, u32[]{:S(2)}, u32[]{:S(2)}) async-start(bf16[8,512,32]{1,2,0:T(8,128)(2,1)} %broadcast_in_dim.33), calls=%async_computation.7 | async-start | bytes 524288 | tf_op jit(solution)/shard_map/all_to_all | solution.py:124
  247.3 0.0 copy-done.3
  247.3 6.5 %all-to-all-done.7 = bf16[8,512,32]{1,2,0:T(8,128)(2,1)S(1)} async-done(((bf16[8,512,32]{1,2,0:T(8,128)(2,1)}), bf16[8,512,32]{1,2,0:T(8,128)(2,1)S(1)}, u32[]{:S(2)}, u32[]{:S(2)}) %all-to-all-start.7) | async-done | bytes 262176 | tf_op jit(solution)/shard_map/all_to_all | solution.py:124
  253.8 0.5 copy.74
  254.3 1.3 gather_fusion
  255.7 0.7 copy.75
  (19 shorter events, 0.2 us)
Async XLA Ops:
  6.5 15.0 %copy-start = (bf16[512,32]{0,1:T(8,128)(2,1)S(1)}, bf16[512,32]{0,1:T(8,128)(2,1)}, u32[]{:S(2)}) copy-start(bf16[512,32]{0,1:T(8,128)(2,1)} %param.9) | copy-start | bytes 98308
  6.5 32.4 %copy-start.1 = (s32[512,2]{0,1:T(2,128)S(1)}, s32[512,2]{0,1:T(2,128)}, u32[]{:S(2)}) copy-start(s32[512,2]{0,1:T(2,128)} %param.11) | copy-start | bytes 12292
  6.5 128.1 %all-gather.2.cloned.1.call-start = ((), (), s32[]{:S(2)}) async-start(), calls=%async_computation.8 | async-start | bytes 9732096 | tf_op jit(solution)/shard_map/all_gather | solution.py:82
  22.4 38.6 %all-to-all-start.1 = ((bf16[16,512,32]{1,2,0:T(8,128)(2,1)}), bf16[16,512,32]{1,2,0:T(8,128)(2,1)S(1)}, u32[]{:S(2)}, u32[]{:S(2)}) async-start(bf16[16,512,32]{1,2,0:T(8,128)(2,1)} %broadcast_in_dim.27), calls=%async_computation.1 | async-start | bytes 1048576 | tf_op jit(solution)/shard_map/all_to_all | solution.py:42
  61.9 8.9 %all-to-all-start.2 = ((f32[512,4,32]{0,2,1:T(8,128)}), f32[512,4,32]{0,2,1:T(8,128)S(1)}, u32[]{:S(2)}, u32[]{:S(2)}) async-start(f32[512,4,32]{0,2,1:T(8,128)} %bitcast.4), calls=%async_computation.2 | async-start | bytes 524288 | tf_op jit(solution)/shard_map/all_to_all | solution.py:63
  143.4 13.2 %copy-start.2 = (f32[512,2]{0,1:T(2,128)S(1)}, f32[512,2]{0,1:T(2,128)}, u32[]{:S(2)}) copy-start(f32[512,2]{0,1:T(2,128)} %param.12) | copy-start | bytes 12292
  144.7 62.2 %all-to-all-start.4 = ((bf16[256,64,32]{0,2,1:T(8,128)(2,1)}), bf16[256,64,32]{0,2,1:T(8,128)(2,1)S(1)}, u32[]{:S(2)}, u32[]{:S(2)}) async-start(bf16[256,64,32]{0,2,1:T(8,128)(2,1)} %bitcast.15), calls=%async_computation.4 | async-start | bytes 2097152 | tf_op jit(solution)/shard_map/all_to_all | solution.py:101
  160.8 77.6 %copy-start.4 = (f32[32]{0:T(128)S(1)}, f32[32]{0:T(128)}, u32[]{:S(2)}) copy-start(f32[32]{0:T(128)} %param.16) | copy-start | bytes 388
  160.8 86.6 %copy-start.3 = (s32[512]{0:T(512)S(1)}, s32[512]{0:T(512)}, u32[]{:S(2)}) copy-start(s32[512]{0:T(512)} %param.17) | copy-start | bytes 6148
  239.2 14.6 %all-to-all-start.7 = ((bf16[8,512,32]{1,2,0:T(8,128)(2,1)}), bf16[8,512,32]{1,2,0:T(8,128)(2,1)S(1)}, u32[]{:S(2)}, u32[]{:S(2)}) async-start(bf16[8,512,32]{1,2,0:T(8,128)(2,1)} %broadcast_in_dim.33), calls=%async_computation.7 | async-start | bytes 524288 | tf_op jit(solution)/shard_map/all_to_all | solution.py:124
Sparse Core Ops, SparseCore 0:
  9.5 68.4 all-gather.1

commit v11 on v9

--- a/solution.py
+++ b/solution.py
@@ -112,7 +112,14 @@
     normed = (
         combined * norm_gain[None, :] * lax.rsqrt(squares / model_width + epsilon)[:, None]
     ).astype(jnp.bfloat16)
-    everyone = lax.all_gather(normed, EX, axis=0, tiled=True)
+    ex_count = lax.axis_size(EX)
+    everyone = lax.all_to_all(
+        jnp.broadcast_to(normed[None], (ex_count,) + normed.shape),
+        EX,
+        split_axis=0,
+        concat_axis=0,
+        tiled=True,
+    ).reshape(ex_count * tok_rows, feat_local)
     return everyone[request_order]
 
 

time: 246 us -> 243 us (0.988)
  waiting for transfers between devices: 57.5 us -> 48.1 us
  starting transfers between devices: 30.9 us -> 34.9 us
  blocking collectives: 107 us -> 110 us
    all_to_all x0 -> x2, blocking collectives: none -> 26.7 us  [gather_sum(): return jnp.sum(lax.all_to_all(spread, axis, 0, 0, tiled=True), axis=0)]
    all_gather x1 -> x0, blocking collectives: 24 us -> none  [shards(): everyone = lax.all_gather(normed, EX, axis=0, tiled=True)]
    all_to_all x2 -> x1, waiting for transfers between devices: 15.9 us -> 6.48 us  [shards(): lax.all_to_all(jnp.broadcast_to(normed[None], (ex_count,) + normed.shape)...]
    all_to_all x2 -> x1, starting transfers between devices: 11.1 us -> 15.1 us  [shards(): lax.all_to_all(jnp.broadcast_to(normed[None], (ex_count,) + normed.shape)...]
  transfers between devices with their start and end apart: 6 -> 5, of which waited for: 4 -> 3; matrix products, arithmetic and copies ran while one was open for 6% -> 6% of each run, Pallas kernels for 0% -> 0%
where the time goes in v11:
time: 243 us; the launch traced here: 242 us
  blocking collectives  110 us (45%)
  waiting for transfers between devices  48.1 us (20%)
  starting transfers between devices  34.9 us (14%)
  matrix products  15.1 us (6%)
  between operations  13.6 us (6%)
  other arithmetic  12.5 us (5%)
  local copies, waits for them, and re-layouts  7.78 us (3%)
    all_to_all x1, blocking collectives, shards(): lax.all_to_all(outgoing, MP, split_axis=1, concat_axis=1, tiled=True)  50 us
    all_to_all x1, waiting for transfers between devices, shards(): lax.all_to_all(partial_value.astype(jnp.bfloat16), MP, split_axis=1, conc...  39.3 us
    all_gather x1, blocking collectives, shards(): along_z = lax.all_gather(context, 'mz', axis=1, tiled=True)  33.2 us
    all_to_all x2, blocking collectives, gather_sum(): return jnp.sum(lax.all_to_all(spread, axis, 0, 0, tiled=True), axis=0)  26.7 us
    all_to_all x1, starting transfers between devices, shards(): lax.all_to_all(jnp.broadcast_to(normed[None], (ex_count,) + normed.shape)...  15.1 us
    all_to_all x1, starting transfers between devices, shards(): lax.all_to_all(partial_value.astype(jnp.bfloat16), MP, split_axis=1, conc...  10.7 us
    all_to_all x1, waiting for transfers between devices, shards(): lax.all_to_all(jnp.broadcast_to(normed[None], (ex_count,) + normed.shape)...  6.48 us
    dot_general x1, matrix products, shards(): jnp.dot(activated, stacked[2], preferred_element_type=jnp.float32)  5.97 us
  transfers between devices with their start and end apart: 5, of which 3 were waited for; matrix products, arithmetic and copies ran while one was open for 6% of the time, Pallas kernels for 0%

profile of v11, /device:TPU:1, one launch (start us, length us, event | category | flops | bytes accessed | tf_op | source)
XLA Modules:
  0.0 241.9 jit_solution(13506717572950970329)
XLA Ops:
  6.5 0.0 copy-start.1
  6.5 0.0 all-gather.2.cloned.1.call-start
  6.5 2.4 pad_maximum_fusion
  8.9 0.0 all-gather.2.cloned.1.call-update
  9.0 1.8 broadcast_in_dim.24
  10.7 4.8 %all-to-all-start = ((bf16[4,32,2048]{2,1,0:T(8,128)(2,1)}), bf16[4,32,2048]{2,1,0:T(8,128)(2,1)S(1)}, u32[]{:S(2)}, u32[]{:S(2)}) async-start(bf16[4,32,2048]{2,1,0:T(8,128)(2,1)} %broadcast_in_dim.24), calls=%async_computation | async-start | bytes 1048576 | tf_op jit(solution)/shard_map/all_to_all | solution.py:43
  15.6 0.0 copy-done.1
  15.6 0.1 copy.65
  15.7 0.2 eq.42
  15.9 0.2 eq.38
  16.1 2.3 reduce-window.6
  18.4 0.3 slice_reduce_fusion
  18.6 0.2 reduce-window.9
  18.8 0.1 add_bitcast_fusion
  18.9 0.2 reduce_sum.67
  19.1 0.1 copy.67
  19.2 0.0 copy-done
  19.2 33.2 %all_gather.6 = bf16[512,512]{0,1:T(8,128)(2,1)S(1)} all-gather(bf16[512,32]{0,1:T(8,128)(2,1)S(1)} %copy-done), channel_id=1, replica_groups=mesh['ey'=1,'ec'=8,'mx'=4,'mz'=16] {'mz'}, dimensions={1}, use_global_device_ids=true | all-gather | bytes 557056 | tf_op jit(solution)/shard_map/all_gather | solution.py:41
  52.5 0.0 all-to-all-done
  52.5 0.9 fusion.13
  53.4 4.1 %all-to-all-start.1 = ((f32[512,4,32]{0,2,1:T(8,128)}), f32[512,4,32]{0,2,1:T(8,128)S(1)}, u32[]{:S(2)}, u32[]{:S(2)}) async-start(f32[512,4,32]{0,2,1:T(8,128)} %bitcast.2), calls=%async_computation.1 | async-start | bytes 524288 | tf_op jit(solution)/shard_map/all_to_all | solution.py:55
  57.6 3.2 %fusion = pred[2048,512]{1,0:T(8,128)(4,1)S(1)} fusion(s32[512,2]{0,1:T(2,128)S(1)} %multiply_add_fusion), kind=kLoop, calls=%fused_computation.3 | loop fusion | flops 3145728 | bytes 1052672 | tf_op jit(solution)/shard_map/reduce_or | solution.py:67
  60.8 2.3 all-to-all-done.1
  63.1 0.7 convolution_convert_fusion
  63.9 0.1 broadcast_in_dim.27
  64.0 50.0 %all_to_all.49 = bf16[256,64,32]{0,2,1:T(8,128)(2,1)S(1)} all-to-all(bf16[256,64,32]{0,2,1:T(8,128)(2,1)S(1)} %bitcast.67), channel_id=1, replica_groups=mesh['ey'=1,'ec'=8,'mx'=4,'mz'=16] {'mx','mz'}, dimensions={1} | all-to-all | bytes 2097152 | tf_op jit(solution)/shard_map/all_to_all | solution.py:73
  114.0 2.7 %fusion.3 = f32[256,704]{0,1:T(8,128)S(1)} fusion(bf16[256,2048]{0,1:T(8,128)(2,1)S(1)} %bitcast.70, bf16[3,704,2048]{2,1,0:T(8,128)(2,1)} %all-gather.2.cloned.1.call-done), kind=kOutput, calls=%fused_computation.9 | convolution fusion | flops 738197504 | bytes 4653056 | tf_op jit(solution)/shard_map/rd,hd->rh/dot_general | solution.py:75
  116.7 6.0 %fusion.4 = bf16[256,2048]{1,0:T(8,128)(2,1)S(1)} fusion(bf16[3,704,2048]{2,1,0:T(8,128)(2,1)} %all-gather.2.cloned.1.call-done, bf16[256,2048]{0,1:T(8,128)(2,1)S(1)} %bitcast.71, f32[256,704]{0,1:T(8,128)S(1)} %fusion.3), kind=kOutput, calls=%fused_computation.10 | convolution fusion | flops 1478000640 | bytes 8585216 | tf_op jit(solution)/shard_map/dot_general | solution.py:88
  122.7 0.0 copy-start.2
  122.7 1.3 copy.69
  124.1 10.7 %all-to-all-start.3 = ((bf16[256,64,32]{0,2,1:T(8,128)(2,1)}), bf16[256,64,32]{0,2,1:T(8,128)(2,1)S(1)}, u32[]{:S(2)}, u32[]{:S(2)}) async-start(bf16[256,64,32]{0,2,1:T(8,128)(2,1)} %bitcast.13), calls=%async_computation.3 | async-start | bytes 2097152 | tf_op jit(solution)/shard_map/all_to_all | solution.py:93
  134.8 0.0 copy-done.2
  134.8 0.1 rev.3
  135.0 4.0 %select_reduce_fusion = f32[2048,512]{1,0:T(8,128)} fusion(f32[512,2]{0,1:T(2,128)S(1)} %add_divide_fusion, s32[512,2]{0,1:T(2,128)S(1)} %multiply_add_fusion), kind=kLoop, calls=%fused_computation.1 | loop fusion | flops 5242880 | bytes 4202496 | tf_op jit(solution)/shard_map/reduce_sum | solution.py:102
  139.0 39.3 %all-to-all-done.3 = bf16[256,64,32]{0,2,1:T(8,128)(2,1)S(1)} async-done(((bf16[256,64,32]{0,2,1:T(8,128)(2,1)}), bf16[256,64,32]{0,2,1:T(8,128)(2,1)S(1)}, u32[]{:S(2)}, u32[]{:S(2)}) %all-to-all-start.3) | async-done | bytes 1048608 | tf_op jit(solution)/shard_map/all_to_all | solution.py:93
  178.2 0.2 bitcast_reduce_fusion
  178.4 4.8 %multiply_reduce_fusion = (f32[512]{0:T(512)S(1)}, f32[512,32]{0,1:T(8,128)S(1)}) fusion(f32[2048,512]{1,0:T(8,128)} %select_reduce_fusion, f32[2048,32]{0,1:T(8,128)S(1)} %bitcast.68, bf16[512,32]{0,1:T(8,128)(2,1)S(1)} %reduce_sum.65), kind=kOutput, calls=%fused_computation.27 | convolution fusion | flops 402718208 | bytes 4556800 | tf_op jit(solution)/shard_map/dot_general | solution.py:105
  183.2 18.7 %all_to_all.50 = f32[16,1,512]{2,1,0:T(1,128)S(1)} all-to-all(f32[16,1,512]{2,1,0:T(1,128)S(1)} %broadcast_in_dim.28), channel_id=1, replica_groups=mesh['ey'=1,'ec'=8,'mx'=4,'mz'=16] {'mz'}, dimensions={0} | all-to-all | bytes 65536 | tf_op jit(solution)/shard_map/all_to_all | solution.py:26
  202.0 8.0 %all_to_all.51 = f32[4,1,512]{2,1,0:T(1,128)S(1)} all-to-all(f32[4,1,512]{2,1,0:T(1,128)S(1)} %broadcast_in_dim.29), channel_id=1, replica_groups=mesh['ey'=1,'ec'=8,'mx'=4,'mz'=16] {'mx'}, dimensions={0} | all-to-all | bytes 16384 | tf_op jit(solution)/shard_map/all_to_all | solution.py:26
  210.0 0.0 copy-done.4
  210.0 0.1 multiply_convert_fusion
  210.1 0.7 broadcast_in_dim.30
  210.8 15.1 %all-to-all-start.6 = ((bf16[8,512,32]{1,2,0:T(8,128)(2,1)}), bf16[8,512,32]{1,2,0:T(8,128)(2,1)S(1)}, u32[]{:S(2)}, u32[]{:S(2)}) async-start(bf16[8,512,32]{1,2,0:T(8,128)(2,1)} %broadcast_in_dim.30), calls=%async_computation.6 | async-start | bytes 524288 | tf_op jit(solution)/shard_map/all_to_all | solution.py:116
  225.9 0.0 copy-done.3
  226.0 6.5 %all-to-all-done.6 = bf16[8,512,32]{1,2,0:T(8,128)(2,1)S(1)} async-done(((bf16[8,512,32]{1,2,0:T(8,128)(2,1)}), bf16[8,512,32]{1,2,0:T(8,128)(2,1)S(1)}, u32[]{:S(2)}, u32[]{:S(2)}) %all-to-all-start.6) | async-done | bytes 262176 | tf_op jit(solution)/shard_map/all_to_all | solution.py:116
  232.5 0.5 copy.73
  233.0 1.3 gather_fusion
  234.3 0.7 copy.74
  (18 shorter events, 0.2 us)
Async XLA Ops:
  6.5 9.0 %copy-start.1 = (s32[512,2]{0,1:T(2,128)S(1)}, s32[512,2]{0,1:T(2,128)}, u32[]{:S(2)}) copy-start(s32[512,2]{0,1:T(2,128)} %param.11) | copy-start | bytes 12292
  6.5 12.7 %copy-start = (bf16[512,32]{0,1:T(8,128)(2,1)S(1)}, bf16[512,32]{0,1:T(8,128)(2,1)}, u32[]{:S(2)}) copy-start(bf16[512,32]{0,1:T(8,128)(2,1)} %param.9) | copy-start | bytes 98308
  6.5 107.5 %all-gather.2.cloned.1.call-start = ((), (), s32[]{:S(2)}) async-start(), calls=%async_computation.7 | async-start | bytes 9732096 | tf_op jit(solution)/shard_map/all_gather | solution.py:74
  10.7 41.7 %all-to-all-start = ((bf16[4,32,2048]{2,1,0:T(8,128)(2,1)}), bf16[4,32,2048]{2,1,0:T(8,128)(2,1)S(1)}, u32[]{:S(2)}, u32[]{:S(2)}) async-start(bf16[4,32,2048]{2,1,0:T(8,128)(2,1)} %broadcast_in_dim.24), calls=%async_computation | async-start | bytes 1048576 | tf_op jit(solution)/shard_map/all_to_all | solution.py:43
  53.4 9.7 %all-to-all-start.1 = ((f32[512,4,32]{0,2,1:T(8,128)}), f32[512,4,32]{0,2,1:T(8,128)S(1)}, u32[]{:S(2)}, u32[]{:S(2)}) async-start(f32[512,4,32]{0,2,1:T(8,128)} %bitcast.2), calls=%async_computation.1 | async-start | bytes 524288 | tf_op jit(solution)/shard_map/all_to_all | solution.py:55
  122.7 12.1 %copy-start.2 = (f32[512,2]{0,1:T(2,128)S(1)}, f32[512,2]{0,1:T(2,128)}, u32[]{:S(2)}) copy-start(f32[512,2]{0,1:T(2,128)} %param.12) | copy-start | bytes 12292
  124.1 54.2 %all-to-all-start.3 = ((bf16[256,64,32]{0,2,1:T(8,128)(2,1)}), bf16[256,64,32]{0,2,1:T(8,128)(2,1)S(1)}, u32[]{:S(2)}, u32[]{:S(2)}) async-start(bf16[256,64,32]{0,2,1:T(8,128)(2,1)} %bitcast.13), calls=%async_computation.3 | async-start | bytes 2097152 | tf_op jit(solution)/shard_map/all_to_all | solution.py:93
  139.0 71.0 %copy-start.4 = (f32[32]{0:T(128)S(1)}, f32[32]{0:T(128)}, u32[]{:S(2)}) copy-start(f32[32]{0:T(128)} %param.16) | copy-start | bytes 388
  139.0 87.0 %copy-start.3 = (s32[512]{0:T(512)S(1)}, s32[512]{0:T(512)}, u32[]{:S(2)}) copy-start(s32[512]{0:T(512)} %param.17) | copy-start | bytes 6148
  210.8 21.6 %all-to-all-start.6 = ((bf16[8,512,32]{1,2,0:T(8,128)(2,1)}), bf16[8,512,32]{1,2,0:T(8,128)(2,1)S(1)}, u32[]{:S(2)}, u32[]{:S(2)}) async-start(bf16[8,512,32]{1,2,0:T(8,128)(2,1)} %broadcast_in_dim.30), calls=%async_computation.6 | async-start | bytes 524288 | tf_op jit(solution)/shard_map/all_to_all | solution.py:116
Sparse Core Ops, SparseCore 0:
  9.5 68.4 all-gather.1

commit v12 on v11

--- a/solution.py
+++ b/solution.py
@@ -107,8 +107,7 @@
     )
     combined = attended.astype(jnp.float32) + branch
     squares = jnp.sum(combined * combined, axis=1)
-    squares = gather_sum(squares, "mz")
-    squares = gather_sum(squares, "mx")
+    squares = gather_sum(squares, MP)
     normed = (
         combined * norm_gain[None, :] * lax.rsqrt(squares / model_width + epsilon)[:, None]
     ).astype(jnp.bfloat16)

time: 243 us -> 238 us (0.979)
    all_to_all x2 -> x1, blocking collectives: 26.7 us -> 24.4 us  [gather_sum(): return jnp.sum(lax.all_to_all(spread, axis, 0, 0, tiled=True), axis=0)]
where the time goes in v12:
time: 238 us
  blocking collectives  108 us (45%)
  waiting for transfers between devices  48.1 us (20%)
  starting transfers between devices  33.1 us (14%)
  matrix products  15.1 us (6%)
  between operations  13.6 us (6%)
  other arithmetic  12.6 us (5%)
  local copies, waits for them, and re-layouts  7.82 us (3%)
    all_to_all x1, blocking collectives, shards(): lax.all_to_all(outgoing, MP, split_axis=1, concat_axis=1, tiled=True)  50 us
    all_to_all x1, waiting for transfers between devices, shards(): lax.all_to_all(partial_value.astype(jnp.bfloat16), MP, split_axis=1, conc...  39.3 us
    all_gather x1, blocking collectives, shards(): along_z = lax.all_gather(context, 'mz', axis=1, tiled=True)  33.2 us
    all_to_all x1, blocking collectives, gather_sum(): return jnp.sum(lax.all_to_all(spread, axis, 0, 0, tiled=True), axis=0)  24.4 us
    all_to_all x1, starting transfers between devices, shards(): lax.all_to_all(jnp.broadcast_to(normed[None], (ex_count,) + normed.shape)...  13.3 us
    all_to_all x1, starting transfers between devices, shards(): lax.all_to_all(partial_value.astype(jnp.bfloat16), MP, split_axis=1, conc...  10.7 us
    all_to_all x1, waiting for transfers between devices, shards(): lax.all_to_all(jnp.broadcast_to(normed[None], (ex_count,) + normed.shape)...  6.48 us
    dot_general x1, matrix products, shards(): jnp.dot(activated, stacked[2], preferred_element_type=jnp.float32)  5.97 us
  transfers between devices with their start and end apart: 5, of which 3 were waited for; matrix products, arithmetic and copies ran while one was open for 6% of the time, Pallas kernels for 0%

profile of v12, /device:TPU:1, one launch (start us, length us, event | category | flops | bytes accessed | tf_op | source)
XLA Modules:
  0.0 237.8 jit_solution(9829036731700674526)
XLA Ops:
  6.5 0.0 all-gather.2.cloned.1.call-start
  6.5 2.4 %pad_maximum_fusion = bf16[3,704,256]{2,1,0:T(8,128)(2,1)} fusion(bf16[1,704,256]{2,1,0:T(8,128)(2,1)} %bitcast.74, bf16[1,704,256]{2,1,0:T(8,128)(2,1)} %bitcast.75, bf16[1,704,256]{2,1,0:T(8,128)(2,1)} %bitcast.76), kind=kLoop, calls=%fused_computation.16 | loop fusion | flops 1081344 | bytes 2162688 | tf_op jit(solution)/shard_map/stack | solution.py:74
  8.9 0.0 all-gather.2.cloned.1.call-update
  9.0 1.8 broadcast_in_dim.22
  10.7 4.8 %all-to-all-start = ((bf16[4,32,2048]{2,1,0:T(8,128)(2,1)}), bf16[4,32,2048]{2,1,0:T(8,128)(2,1)S(1)}, u32[]{:S(2)}, u32[]{:S(2)}) async-start(bf16[4,32,2048]{2,1,0:T(8,128)(2,1)} %broadcast_in_dim.22), calls=%async_computation | async-start | bytes 1048576 | tf_op jit(solution)/shard_map/all_to_all | solution.py:43
  15.6 0.0 copy-done.1
  15.6 0.1 copy.64
  15.7 0.2 eq.42
  15.9 0.2 eq.38
  16.1 2.3 reduce-window.6
  18.4 0.3 slice_reduce_fusion
  18.6 0.2 reduce-window.9
  18.8 0.1 add_bitcast_fusion
  18.9 0.2 reduce_sum.58
  19.1 0.1 copy.66
  19.2 0.0 copy-done
  19.2 33.2 %all_gather.6 = bf16[512,512]{0,1:T(8,128)(2,1)S(1)} all-gather(bf16[512,32]{0,1:T(8,128)(2,1)S(1)} %copy-done), channel_id=1, replica_groups=mesh['ey'=1,'ec'=8,'mx'=4,'mz'=16] {'mz'}, dimensions={1}, use_global_device_ids=true | all-gather | bytes 557056 | tf_op jit(solution)/shard_map/all_gather | solution.py:41
  52.5 0.0 all-to-all-done
  52.5 0.9 fusion.13
  53.4 4.1 %all-to-all-start.1 = ((f32[512,4,32]{0,2,1:T(8,128)}), f32[512,4,32]{0,2,1:T(8,128)S(1)}, u32[]{:S(2)}, u32[]{:S(2)}) async-start(f32[512,4,32]{0,2,1:T(8,128)} %bitcast.2), calls=%async_computation.1 | async-start | bytes 524288 | tf_op jit(solution)/shard_map/all_to_all | solution.py:55
  57.6 3.2 %fusion = pred[2048,512]{1,0:T(8,128)(4,1)S(1)} fusion(s32[512,2]{0,1:T(2,128)S(1)} %multiply_add_fusion), kind=kLoop, calls=%fused_computation.3 | loop fusion | flops 3145728 | bytes 1052672 | tf_op jit(solution)/shard_map/reduce_or | solution.py:67
  60.8 2.3 all-to-all-done.1
  63.1 0.7 convolution_convert_fusion
  63.9 0.1 broadcast_in_dim.25
  64.0 50.0 %all_to_all.43 = bf16[256,64,32]{0,2,1:T(8,128)(2,1)S(1)} all-to-all(bf16[256,64,32]{0,2,1:T(8,128)(2,1)S(1)} %bitcast.67), channel_id=1, replica_groups=mesh['ey'=1,'ec'=8,'mx'=4,'mz'=16] {'mx','mz'}, dimensions={1} | all-to-all | bytes 2097152 | tf_op jit(solution)/shard_map/all_to_all | solution.py:73
  114.0 2.7 %fusion.3 = f32[256,704]{0,1:T(8,128)S(1)} fusion(bf16[256,2048]{0,1:T(8,128)(2,1)S(1)} %bitcast.70, bf16[3,704,2048]{2,1,0:T(8,128)(2,1)} %all-gather.2.cloned.1.call-done), kind=kOutput, calls=%fused_computation.9 | convolution fusion | flops 738197504 | bytes 4653056 | tf_op jit(solution)/shard_map/rd,hd->rh/dot_general | solution.py:75
  116.7 6.0 %fusion.4 = bf16[256,2048]{1,0:T(8,128)(2,1)S(1)} fusion(bf16[3,704,2048]{2,1,0:T(8,128)(2,1)} %all-gather.2.cloned.1.call-done, bf16[256,2048]{0,1:T(8,128)(2,1)S(1)} %bitcast.71, f32[256,704]{0,1:T(8,128)S(1)} %fusion.3), kind=kOutput, calls=%fused_computation.10 | convolution fusion | flops 1478000640 | bytes 8585216 | tf_op jit(solution)/shard_map/dot_general | solution.py:88
  122.7 0.0 copy-start.2
  122.7 1.3 copy.68
  124.1 10.7 %all-to-all-start.3 = ((bf16[256,64,32]{0,2,1:T(8,128)(2,1)}), bf16[256,64,32]{0,2,1:T(8,128)(2,1)S(1)}, u32[]{:S(2)}, u32[]{:S(2)}) async-start(bf16[256,64,32]{0,2,1:T(8,128)(2,1)} %bitcast.13), calls=%async_computation.3 | async-start | bytes 2097152 | tf_op jit(solution)/shard_map/all_to_all | solution.py:93
  134.8 0.0 copy-done.2
  134.8 0.1 rev.3
  135.0 4.0 %select_reduce_fusion = f32[2048,512]{1,0:T(8,128)} fusion(f32[512,2]{0,1:T(2,128)S(1)} %add_divide_fusion, s32[512,2]{0,1:T(2,128)S(1)} %multiply_add_fusion), kind=kLoop, calls=%fused_computation.1 | loop fusion | flops 5242880 | bytes 4202496 | tf_op jit(solution)/shard_map/reduce_sum | solution.py:102
  139.0 39.3 %all-to-all-done.3 = bf16[256,64,32]{0,2,1:T(8,128)(2,1)S(1)} async-done(((bf16[256,64,32]{0,2,1:T(8,128)(2,1)}), bf16[256,64,32]{0,2,1:T(8,128)(2,1)S(1)}, u32[]{:S(2)}, u32[]{:S(2)}) %all-to-all-start.3) | async-done | bytes 1048608 | tf_op jit(solution)/shard_map/all_to_all | solution.py:93
  178.2 0.2 bitcast_reduce_fusion
  178.4 4.8 %multiply_reduce_fusion = (f32[512]{0:T(512)S(1)}, f32[512,32]{0,1:T(8,128)S(1)}) fusion(f32[2048,512]{1,0:T(8,128)} %select_reduce_fusion, f32[2048,32]{0,1:T(8,128)S(1)} %bitcast.68, bf16[512,32]{0,1:T(8,128)(2,1)S(1)} %reduce_sum.56), kind=kOutput, calls=%fused_computation.27 | convolution fusion | flops 402718208 | bytes 4556800 | tf_op jit(solution)/shard_map/dot_general | solution.py:105
  183.2 0.1 broadcast_in_dim.26
  183.3 24.4 %all_to_all.44 = f32[64,1,512]{2,1,0:T(1,128)S(1)} all-to-all(f32[64,1,512]{2,1,0:T(1,128)S(1)} %broadcast_in_dim.26), channel_id=1, replica_groups=mesh['ey'=1,'ec'=8,'mx'=4,'mz'=16] {'mx','mz'}, dimensions={0} | all-to-all | bytes 262144 | tf_op jit(solution)/shard_map/all_to_all | solution.py:26
  207.6 0.1 reduce_sum.62
  207.8 0.0 copy-done.4
  207.8 0.1 multiply_convert_fusion
  207.8 0.7 broadcast_in_dim.46
  208.6 13.3 %all-to-all-start.5 = ((bf16[8,512,32]{1,2,0:T(8,128)(2,1)}), bf16[8,512,32]{1,2,0:T(8,128)(2,1)S(1)}, u32[]{:S(2)}, u32[]{:S(2)}) async-start(bf16[8,512,32]{1,2,0:T(8,128)(2,1)} %broadcast_in_dim.46), calls=%async_computation.5 | async-start | bytes 524288 | tf_op jit(solution)/shard_map/all_to_all | solution.py:115
  221.9 0.0 copy-done.3
  221.9 6.5 %all-to-all-done.5 = bf16[8,512,32]{1,2,0:T(8,128)(2,1)S(1)} async-done(((bf16[8,512,32]{1,2,0:T(8,128)(2,1)}), bf16[8,512,32]{1,2,0:T(8,128)(2,1)S(1)}, u32[]{:S(2)}, u32[]{:S(2)}) %all-to-all-start.5) | async-done | bytes 262176 | tf_op jit(solution)/shard_map/all_to_all | solution.py:115
  228.4 0.5 copy.71
  228.9 1.3 gather_fusion
  230.3 0.7 copy.72
  (15 shorter events, 0.1 us)
Async XLA Ops:
  6.5 9.0 %copy-start.1 = (s32[512,2]{0,1:T(2,128)S(1)}, s32[512,2]{0,1:T(2,128)}, u32[]{:S(2)}) copy-start(s32[512,2]{0,1:T(2,128)} %param.11) | copy-start | bytes 12292
  6.5 12.7 %copy-start = (bf16[512,32]{0,1:T(8,128)(2,1)S(1)}, bf16[512,32]{0,1:T(8,128)(2,1)}, u32[]{:S(2)}) copy-start(bf16[512,32]{0,1:T(8,128)(2,1)} %param.9) | copy-start | bytes 98308
  6.5 107.5 %all-gather.2.cloned.1.call-start = ((), (), s32[]{:S(2)}) async-start(), calls=%async_computation.6 | async-start | bytes 9732096 | tf_op jit(solution)/shard_map/all_gather | solution.py:74
  10.7 41.7 %all-to-all-start = ((bf16[4,32,2048]{2,1,0:T(8,128)(2,1)}), bf16[4,32,2048]{2,1,0:T(8,128)(2,1)S(1)}, u32[]{:S(2)}, u32[]{:S(2)}) async-start(bf16[4,32,2048]{2,1,0:T(8,128)(2,1)} %broadcast_in_dim.22), calls=%async_computation | async-start | bytes 1048576 | tf_op jit(solution)/shard_map/all_to_all | solution.py:43
  53.4 9.7 %all-to-all-start.1 = ((f32[512,4,32]{0,2,1:T(8,128)}), f32[512,4,32]{0,2,1:T(8,128)S(1)}, u32[]{:S(2)}, u32[]{:S(2)}) async-start(f32[512,4,32]{0,2,1:T(8,128)} %bitcast.2), calls=%async_computation.1 | async-start | bytes 524288 | tf_op jit(solution)/shard_map/all_to_all | solution.py:55
  122.7 12.1 %copy-start.2 = (f32[512,2]{0,1:T(2,128)S(1)}, f32[512,2]{0,1:T(2,128)}, u32[]{:S(2)}) copy-start(f32[512,2]{0,1:T(2,128)} %param.12) | copy-start | bytes 12292
  124.1 54.2 %all-to-all-start.3 = ((bf16[256,64,32]{0,2,1:T(8,128)(2,1)}), bf16[256,64,32]{0,2,1:T(8,128)(2,1)S(1)}, u32[]{:S(2)}, u32[]{:S(2)}) async-start(bf16[256,64,32]{0,2,1:T(8,128)(2,1)} %bitcast.13), calls=%async_computation.3 | async-start | bytes 2097152 | tf_op jit(solution)/shard_map/all_to_all | solution.py:93
  139.0 68.8 %copy-start.4 = (f32[32]{0:T(128)S(1)}, f32[32]{0:T(128)}, u32[]{:S(2)}) copy-start(f32[32]{0:T(128)} %param.16) | copy-start | bytes 388
  139.0 82.9 %copy-start.3 = (s32[512]{0:T(512)S(1)}, s32[512]{0:T(512)}, u32[]{:S(2)}) copy-start(s32[512]{0:T(512)} %param.17) | copy-start | bytes 6148
  208.6 19.8 %all-to-all-start.5 = ((bf16[8,512,32]{1,2,0:T(8,128)(2,1)}), bf16[8,512,32]{1,2,0:T(8,128)(2,1)S(1)}, u32[]{:S(2)}, u32[]{:S(2)}) async-start(bf16[8,512,32]{1,2,0:T(8,128)(2,1)} %broadcast_in_dim.46), calls=%async_computation.5 | async-start | bytes 524288 | tf_op jit(solution)/shard_map/all_to_all | solution.py:115
Sparse Core Ops, SparseCore 0:
  9.5 68.4 all-gather.1

commit v13 on v12

--- a/solution.py
+++ b/solution.py
@@ -12,11 +12,14 @@
 
 def slot_targets(routes, capacity, experts):
     flat_routes = routes.reshape(-1)
+    pairs = flat_routes.shape[0]
     onehot = (flat_routes[:, None] == jnp.arange(experts, dtype=jnp.int32)[None, :]).astype(
-        jnp.int32
+        jnp.bfloat16
     )
-    earlier = jnp.cumsum(onehot, axis=0) - onehot
-    slot_index = jnp.sum(earlier * onehot, axis=1)
+    order = jnp.arange(pairs, dtype=jnp.int32)
+    before = (order[None, :] < order[:, None]).astype(jnp.bfloat16)
+    earlier = jnp.dot(before, onehot, preferred_element_type=jnp.float32)
+    slot_index = jnp.sum(earlier * onehot.astype(jnp.float32), axis=1).astype(jnp.int32)
     return flat_routes * capacity + slot_index
 
 

time: 238 us -> 237 us (level)
  other arithmetic: 12.6 us -> 10 us
    another operation x2 -> x0, other arithmetic: 2.43 us -> none
  transfers between devices with their start and end apart: 5 -> 5, of which waited for: 3 -> 3; matrix products, arithmetic and copies ran while one was open for 6% -> 5% of each run, Pallas kernels for 0% -> 0%
where the time goes in v13:
time: 237 us; the launch traced here: 236 us
  blocking collectives  108 us (46%)
  waiting for transfers between devices  48.1 us (20%)
  starting transfers between devices  33.8 us (14%)
  matrix products  15.6 us (7%)
  between operations  13.6 us (6%)
  other arithmetic  10 us (4%)
  local copies, waits for them, and re-layouts  7.38 us (3%)
    all_to_all x1, blocking collectives, shards(): lax.all_to_all(outgoing, MP, split_axis=1, concat_axis=1, tiled=True)  50.3 us
    all_to_all x1, waiting for transfers between devices, shards(): lax.all_to_all(partial_value.astype(jnp.bfloat16), MP, split_axis=1, conc...  39.3 us
    all_gather x1, blocking collectives, shards(): along_z = lax.all_gather(context, 'mz', axis=1, tiled=True)  33.1 us
    all_to_all x1, blocking collectives, gather_sum(): return jnp.sum(lax.all_to_all(spread, axis, 0, 0, tiled=True), axis=0)  24.4 us
    all_to_all x1, starting transfers between devices, shards(): lax.all_to_all(jnp.broadcast_to(normed[None], (ex_count,) + normed.shape)...  14.1 us
    all_to_all x1, starting transfers between devices, shards(): lax.all_to_all(partial_value.astype(jnp.bfloat16), MP, split_axis=1, conc...  10.7 us
    all_to_all x1, waiting for transfers between devices, shards(): lax.all_to_all(jnp.broadcast_to(normed[None], (ex_count,) + normed.shape)...  6.48 us
    dot_general x1, matrix products, shards(): jnp.dot(activated, stacked[2], preferred_element_type=jnp.float32)  5.97 us
  transfers between devices with their start and end apart: 5, of which 3 were waited for; matrix products, arithmetic and copies ran while one was open for 5% of the time, Pallas kernels for 0%

profile of v13, /device:TPU:1, one launch (start us, length us, event | category | flops | bytes accessed | tf_op | source)
XLA Modules:
  0.0 236.3 jit_solution(14099953695503055893)
XLA Ops:
  6.5 0.0 copy-start.1
  6.5 0.0 copy-start
  6.5 0.0 all-gather.2.cloned.1.call-start
  6.5 2.4 %pad_maximum_fusion = bf16[3,704,256]{2,1,0:T(8,128)(2,1)} fusion(bf16[1,704,256]{2,1,0:T(8,128)(2,1)} %bitcast.55, bf16[1,704,256]{2,1,0:T(8,128)(2,1)} %bitcast.56, bf16[1,704,256]{2,1,0:T(8,128)(2,1)} %bitcast.57), kind=kLoop, calls=%fused_computation.20 | loop fusion | flops 1081344 | bytes 2162688 | tf_op jit(solution)/shard_map/stack | solution.py:77
  8.9 0.0 all-gather.2.cloned.1.call-update
  9.0 1.8 broadcast_in_dim.22
  10.7 4.8 %all-to-all-start = ((bf16[4,32,2048]{2,1,0:T(8,128)(2,1)}), bf16[4,32,2048]{2,1,0:T(8,128)(2,1)S(1)}, u32[]{:S(2)}, u32[]{:S(2)}) async-start(bf16[4,32,2048]{2,1,0:T(8,128)(2,1)} %broadcast_in_dim.22), calls=%async_computation | async-start | bytes 1048576 | tf_op jit(solution)/shard_map/all_to_all | solution.py:46
  15.6 0.0 copy-done.1
  15.6 0.1 copy.59
  15.7 0.2 eq.28
  15.9 0.5 fusion.9
  16.4 0.2 convert_element_type.48
  16.6 0.1 copy.60
  16.7 0.0 copy-done
  16.7 33.1 %all_gather.6 = bf16[512,512]{0,1:T(8,128)(2,1)S(1)} all-gather(bf16[512,32]{0,1:T(8,128)(2,1)S(1)} %copy-done), channel_id=1, replica_groups=mesh['ey'=1,'ec'=8,'mx'=4,'mz'=16] {'mz'}, dimensions={1}, use_global_device_ids=true | all-gather | bytes 557056 | tf_op jit(solution)/shard_map/all_gather | solution.py:44
  49.9 0.0 all-to-all-done
  49.9 0.9 fusion.16
  50.8 4.1 %all-to-all-start.1 = ((f32[512,4,32]{0,2,1:T(8,128)}), f32[512,4,32]{0,2,1:T(8,128)S(1)}, u32[]{:S(2)}, u32[]{:S(2)}) async-start(f32[512,4,32]{0,2,1:T(8,128)} %bitcast.2), calls=%async_computation.1 | async-start | bytes 524288 | tf_op jit(solution)/shard_map/all_to_all | solution.py:58
  54.9 3.2 %fusion = pred[2048,512]{1,0:T(8,128)(4,1)S(1)} fusion(s32[512,2]{0,1:T(2,128)S(1)} %multiply_add_fusion), kind=kLoop, calls=%fused_computation.3 | loop fusion | flops 3145728 | bytes 1052672 | tf_op jit(solution)/shard_map/reduce_or | solution.py:70
  58.1 2.3 all-to-all-done.1
  60.5 0.7 convolution_convert_fusion
  61.2 0.1 broadcast_in_dim.25
  61.4 50.3 %all_to_all.43 = bf16[256,64,32]{0,2,1:T(8,128)(2,1)S(1)} all-to-all(bf16[256,64,32]{0,2,1:T(8,128)(2,1)S(1)} %bitcast.48), channel_id=1, replica_groups=mesh['ey'=1,'ec'=8,'mx'=4,'mz'=16] {'mx','mz'}, dimensions={1} | all-to-all | bytes 2097152 | tf_op jit(solution)/shard_map/all_to_all | solution.py:76
  111.7 0.0 all-gather.2.cloned.1.call-done
  111.7 2.7 %fusion.4 = f32[256,704]{0,1:T(8,128)S(1)} fusion(bf16[256,2048]{0,1:T(8,128)(2,1)S(1)} %bitcast.51, bf16[3,704,2048]{2,1,0:T(8,128)(2,1)} %all-gather.2.cloned.1.call-done), kind=kOutput, calls=%fused_computation.11 | convolution fusion | flops 738197504 | bytes 4653056 | tf_op jit(solution)/shard_map/rd,hd->rh/dot_general | solution.py:78
  114.4 6.0 %fusion.5 = bf16[256,2048]{1,0:T(8,128)(2,1)S(1)} fusion(bf16[3,704,2048]{2,1,0:T(8,128)(2,1)} %all-gather.2.cloned.1.call-done, bf16[256,2048]{0,1:T(8,128)(2,1)S(1)} %bitcast.52, f32[256,704]{0,1:T(8,128)S(1)} %fusion.4), kind=kOutput, calls=%fused_computation.12 | convolution fusion | flops 1478000640 | bytes 8585216 | tf_op jit(solution)/shard_map/dot_general | solution.py:91
  120.4 0.0 copy-start.2
  120.4 1.3 copy.62
  121.7 10.7 %all-to-all-start.3 = ((bf16[256,64,32]{0,2,1:T(8,128)(2,1)}), bf16[256,64,32]{0,2,1:T(8,128)(2,1)S(1)}, u32[]{:S(2)}, u32[]{:S(2)}) async-start(bf16[256,64,32]{0,2,1:T(8,128)(2,1)} %bitcast.12), calls=%async_computation.3 | async-start | bytes 2097152 | tf_op jit(solution)/shard_map/all_to_all | solution.py:96
  132.5 0.0 copy-done.2
  132.5 0.1 rev.3
  132.7 4.0 %select_reduce_fusion = f32[2048,512]{1,0:T(8,128)} fusion(f32[512,2]{0,1:T(2,128)S(1)} %add_divide_fusion, s32[512,2]{0,1:T(2,128)S(1)} %multiply_add_fusion), kind=kLoop, calls=%fused_computation.1 | loop fusion | flops 5242880 | bytes 4202496 | tf_op jit(solution)/shard_map/reduce_sum | solution.py:105
  136.6 0.0 copy-start.4
  136.6 39.3 %all-to-all-done.3 = bf16[256,64,32]{0,2,1:T(8,128)(2,1)S(1)} async-done(((bf16[256,64,32]{0,2,1:T(8,128)(2,1)}), bf16[256,64,32]{0,2,1:T(8,128)(2,1)S(1)}, u32[]{:S(2)}, u32[]{:S(2)}) %all-to-all-start.3) | async-done | bytes 1048608 | tf_op jit(solution)/shard_map/all_to_all | solution.py:96
  175.9 0.2 bitcast_reduce_fusion
  176.1 4.8 %multiply_reduce_fusion = (f32[512]{0:T(512)S(1)}, f32[512,32]{0,1:T(8,128)S(1)}) fusion(f32[2048,512]{1,0:T(8,128)} %select_reduce_fusion, f32[2048,32]{0,1:T(8,128)S(1)} %bitcast.49, bf16[512,32]{0,1:T(8,128)(2,1)S(1)} %reduce_sum.54), kind=kOutput, calls=%fused_computation.31 | convolution fusion | flops 402718208 | bytes 4556800 | tf_op jit(solution)/shard_map/dot_general | solution.py:108
  180.9 0.1 broadcast_in_dim.26
  181.0 24.4 %all_to_all.44 = f32[64,1,512]{2,1,0:T(1,128)S(1)} all-to-all(f32[64,1,512]{2,1,0:T(1,128)S(1)} %broadcast_in_dim.26), channel_id=1, replica_groups=mesh['ey'=1,'ec'=8,'mx'=4,'mz'=16] {'mx','mz'}, dimensions={0} | all-to-all | bytes 262144 | tf_op jit(solution)/shard_map/all_to_all | solution.py:29
  205.4 0.1 reduce_sum.59
  205.5 0.0 copy-done.4
  205.5 0.1 multiply_convert_fusion
  205.6 0.7 broadcast_in_dim.27
  206.3 14.1 %all-to-all-start.5 = ((bf16[8,512,32]{1,2,0:T(8,128)(2,1)}), bf16[8,512,32]{1,2,0:T(8,128)(2,1)S(1)}, u32[]{:S(2)}, u32[]{:S(2)}) async-start(bf16[8,512,32]{1,2,0:T(8,128)(2,1)} %broadcast_in_dim.27), calls=%async_computation.5 | async-start | bytes 524288 | tf_op jit(solution)/shard_map/all_to_all | solution.py:118
  220.4 0.0 copy-done.3
  220.4 6.5 %all-to-all-done.5 = bf16[8,512,32]{1,2,0:T(8,128)(2,1)S(1)} async-done(((bf16[8,512,32]{1,2,0:T(8,128)(2,1)}), bf16[8,512,32]{1,2,0:T(8,128)(2,1)S(1)}, u32[]{:S(2)}, u32[]{:S(2)}) %all-to-all-start.5) | async-done | bytes 262176 | tf_op jit(solution)/shard_map/all_to_all | solution.py:118
  226.9 0.5 copy.65
  227.4 1.3 gather_fusion
  228.8 0.7 copy.66
  (10 shorter events, 0.1 us)
Async XLA Ops:
  6.5 9.0 %copy-start.1 = (s32[512,2]{0,1:T(2,128)S(1)}, s32[512,2]{0,1:T(2,128)}, u32[]{:S(2)}) copy-start(s32[512,2]{0,1:T(2,128)} %param.11) | copy-start | bytes 12292
  6.5 10.2 %copy-start = (bf16[512,32]{0,1:T(8,128)(2,1)S(1)}, bf16[512,32]{0,1:T(8,128)(2,1)}, u32[]{:S(2)}) copy-start(bf16[512,32]{0,1:T(8,128)(2,1)} %param.9) | copy-start | bytes 98308
  6.5 105.1 %all-gather.2.cloned.1.call-start = ((), (), s32[]{:S(2)}) async-start(), calls=%async_computation.6 | async-start | bytes 9732096 | tf_op jit(solution)/shard_map/all_gather | solution.py:77
  10.7 39.1 %all-to-all-start = ((bf16[4,32,2048]{2,1,0:T(8,128)(2,1)}), bf16[4,32,2048]{2,1,0:T(8,128)(2,1)S(1)}, u32[]{:S(2)}, u32[]{:S(2)}) async-start(bf16[4,32,2048]{2,1,0:T(8,128)(2,1)} %broadcast_in_dim.22), calls=%async_computation | async-start | bytes 1048576 | tf_op jit(solution)/shard_map/all_to_all | solution.py:46
  50.8 9.6 %all-to-all-start.1 = ((f32[512,4,32]{0,2,1:T(8,128)}), f32[512,4,32]{0,2,1:T(8,128)S(1)}, u32[]{:S(2)}, u32[]{:S(2)}) async-start(f32[512,4,32]{0,2,1:T(8,128)} %bitcast.2), calls=%async_computation.1 | async-start | bytes 524288 | tf_op jit(solution)/shard_map/all_to_all | solution.py:58
  120.4 12.1 %copy-start.2 = (f32[512,2]{0,1:T(2,128)S(1)}, f32[512,2]{0,1:T(2,128)}, u32[]{:S(2)}) copy-start(f32[512,2]{0,1:T(2,128)} %param.12) | copy-start | bytes 12292
  121.7 54.2 %all-to-all-start.3 = ((bf16[256,64,32]{0,2,1:T(8,128)(2,1)}), bf16[256,64,32]{0,2,1:T(8,128)(2,1)S(1)}, u32[]{:S(2)}, u32[]{:S(2)}) async-start(bf16[256,64,32]{0,2,1:T(8,128)(2,1)} %bitcast.12), calls=%async_computation.3 | async-start | bytes 2097152 | tf_op jit(solution)/shard_map/all_to_all | solution.py:96
  136.6 68.8 %copy-start.4 = (f32[32]{0:T(128)S(1)}, f32[32]{0:T(128)}, u32[]{:S(2)}) copy-start(f32[32]{0:T(128)} %param.16) | copy-start | bytes 388
  136.6 83.8 %copy-start.3 = (s32[512]{0:T(512)S(1)}, s32[512]{0:T(512)}, u32[]{:S(2)}) copy-start(s32[512]{0:T(512)} %param.17) | copy-start | bytes 6148
  206.3 20.6 %all-to-all-start.5 = ((bf16[8,512,32]{1,2,0:T(8,128)(2,1)}), bf16[8,512,32]{1,2,0:T(8,128)(2,1)S(1)}, u32[]{:S(2)}, u32[]{:S(2)}) async-start(bf16[8,512,32]{1,2,0:T(8,128)(2,1)} %broadcast_in_dim.27), calls=%async_computation.5 | async-start | bytes 524288 | tf_op jit(solution)/shard_map/all_to_all | solution.py:118
Sparse Core Ops, SparseCore 0:
  9.5 68.4 all-gather.1

commit v14 on v13

--- a/solution.py
+++ b/solution.py
@@ -106,7 +106,7 @@
         jnp.where(chosen, weights[None, :, :], 0.0), axis=2
     ).T
     branch = jnp.dot(
-        picking, expert_out, precision=lax.Precision.HIGHEST, preferred_element_type=jnp.float32
+        picking, expert_out, precision=lax.Precision.HIGH, preferred_element_type=jnp.float32
     )
     combined = attended.astype(jnp.float32) + branch
     squares = jnp.sum(combined * combined, axis=1)

time: 237 us -> 236 us (level)
  no operation moved by 1% of the time
where the time goes in v14:
time: 236 us; the launch traced here: 235 us
  blocking collectives  108 us (46%)
  waiting for transfers between devices  48.1 us (20%)
  starting transfers between devices  33.8 us (14%)
  matrix products  14.3 us (6%)
  between operations  13.6 us (6%)
  other arithmetic  10 us (4%)
  local copies, waits for them, and re-layouts  7.38 us (3%)
    all_to_all x1, blocking collectives, shards(): lax.all_to_all(outgoing, MP, split_axis=1, concat_axis=1, tiled=True)  50.3 us
    all_to_all x1, waiting for transfers between devices, shards(): lax.all_to_all(partial_value.astype(jnp.bfloat16), MP, split_axis=1, conc...  39.3 us
    all_gather x1, blocking collectives, shards(): along_z = lax.all_gather(context, 'mz', axis=1, tiled=True)  33.1 us
    all_to_all x1, blocking collectives, gather_sum(): return jnp.sum(lax.all_to_all(spread, axis, 0, 0, tiled=True), axis=0)  24.4 us
    all_to_all x1, starting transfers between devices, shards(): lax.all_to_all(jnp.broadcast_to(normed[None], (ex_count,) + normed.shape)...  14.1 us
    all_to_all x1, starting transfers between devices, shards(): lax.all_to_all(partial_value.astype(jnp.bfloat16), MP, split_axis=1, conc...  10.7 us
    all_to_all x1, waiting for transfers between devices, shards(): lax.all_to_all(jnp.broadcast_to(normed[None], (ex_count,) + normed.shape)...  6.48 us
    dot_general x1, matrix products, shards(): jnp.dot(activated, stacked[2], preferred_element_type=jnp.float32)  5.97 us
  transfers between devices with their start and end apart: 5, of which 3 were waited for; matrix products, arithmetic and copies ran while one was open for 5% of the time, Pallas kernels for 0%

profile of v14, /device:TPU:1, one launch (start us, length us, event | category | flops | bytes accessed | tf_op | source)
XLA Modules:
  0.0 235.0 jit_solution(7683322067185880641)
XLA Ops:
  6.5 0.0 copy-start.1
  6.5 0.0 copy-start
  6.5 0.0 all-gather.2.cloned.1.call-start
  6.5 2.4 %pad_maximum_fusion = bf16[3,704,256]{2,1,0:T(8,128)(2,1)} fusion(bf16[1,704,256]{2,1,0:T(8,128)(2,1)} %bitcast.55, bf16[1,704,256]{2,1,0:T(8,128)(2,1)} %bitcast.56, bf16[1,704,256]{2,1,0:T(8,128)(2,1)} %bitcast.57), kind=kLoop, calls=%fused_computation.20 | loop fusion | flops 1081344 | bytes 2162688 | tf_op jit(solution)/shard_map/stack | solution.py:77
  8.9 0.0 all-gather.2.cloned.1.call-update
  9.0 1.8 broadcast_in_dim.22
  10.7 4.8 %all-to-all-start = ((bf16[4,32,2048]{2,1,0:T(8,128)(2,1)}), bf16[4,32,2048]{2,1,0:T(8,128)(2,1)S(1)}, u32[]{:S(2)}, u32[]{:S(2)}) async-start(bf16[4,32,2048]{2,1,0:T(8,128)(2,1)} %broadcast_in_dim.22), calls=%async_computation | async-start | bytes 1048576 | tf_op jit(solution)/shard_map/all_to_all | solution.py:46
  15.6 0.0 copy-done.1
  15.6 0.1 copy.59
  15.7 0.2 eq.28
  15.9 0.5 fusion.9
  16.4 0.2 convert_element_type.48
  16.6 0.1 copy.60
  16.7 0.0 copy-done
  16.7 33.1 %all_gather.6 = bf16[512,512]{0,1:T(8,128)(2,1)S(1)} all-gather(bf16[512,32]{0,1:T(8,128)(2,1)S(1)} %copy-done), channel_id=1, replica_groups=mesh['ey'=1,'ec'=8,'mx'=4,'mz'=16] {'mz'}, dimensions={1}, use_global_device_ids=true | all-gather | bytes 557056 | tf_op jit(solution)/shard_map/all_gather | solution.py:44
  49.9 0.0 all-to-all-done
  49.9 0.9 fusion.16
  50.8 4.1 %all-to-all-start.1 = ((f32[512,4,32]{0,2,1:T(8,128)}), f32[512,4,32]{0,2,1:T(8,128)S(1)}, u32[]{:S(2)}, u32[]{:S(2)}) async-start(f32[512,4,32]{0,2,1:T(8,128)} %bitcast.2), calls=%async_computation.1 | async-start | bytes 524288 | tf_op jit(solution)/shard_map/all_to_all | solution.py:58
  54.9 3.2 %fusion = pred[2048,512]{1,0:T(8,128)(4,1)S(1)} fusion(s32[512,2]{0,1:T(2,128)S(1)} %multiply_add_fusion), kind=kLoop, calls=%fused_computation.3 | loop fusion | flops 3145728 | bytes 1052672 | tf_op jit(solution)/shard_map/reduce_or | solution.py:70
  58.1 2.3 all-to-all-done.1
  60.5 0.7 convolution_convert_fusion
  61.2 0.1 broadcast_in_dim.25
  61.4 50.3 %all_to_all.43 = bf16[256,64,32]{0,2,1:T(8,128)(2,1)S(1)} all-to-all(bf16[256,64,32]{0,2,1:T(8,128)(2,1)S(1)} %bitcast.48), channel_id=1, replica_groups=mesh['ey'=1,'ec'=8,'mx'=4,'mz'=16] {'mx','mz'}, dimensions={1} | all-to-all | bytes 2097152 | tf_op jit(solution)/shard_map/all_to_all | solution.py:76
  111.7 0.0 all-gather.2.cloned.1.call-done
  111.7 2.7 %fusion.4 = f32[256,704]{0,1:T(8,128)S(1)} fusion(bf16[256,2048]{0,1:T(8,128)(2,1)S(1)} %bitcast.51, bf16[3,704,2048]{2,1,0:T(8,128)(2,1)} %all-gather.2.cloned.1.call-done), kind=kOutput, calls=%fused_computation.11 | convolution fusion | flops 738197504 | bytes 4653056 | tf_op jit(solution)/shard_map/rd,hd->rh/dot_general | solution.py:78
  114.4 6.0 %fusion.5 = bf16[256,2048]{1,0:T(8,128)(2,1)S(1)} fusion(bf16[3,704,2048]{2,1,0:T(8,128)(2,1)} %all-gather.2.cloned.1.call-done, bf16[256,2048]{0,1:T(8,128)(2,1)S(1)} %bitcast.52, f32[256,704]{0,1:T(8,128)S(1)} %fusion.4), kind=kOutput, calls=%fused_computation.12 | convolution fusion | flops 1478000640 | bytes 8585216 | tf_op jit(solution)/shard_map/dot_general | solution.py:91
  120.4 0.0 copy-start.2
  120.4 1.3 copy.62
  121.7 10.7 %all-to-all-start.3 = ((bf16[256,64,32]{0,2,1:T(8,128)(2,1)}), bf16[256,64,32]{0,2,1:T(8,128)(2,1)S(1)}, u32[]{:S(2)}, u32[]{:S(2)}) async-start(bf16[256,64,32]{0,2,1:T(8,128)(2,1)} %bitcast.12), calls=%async_computation.3 | async-start | bytes 2097152 | tf_op jit(solution)/shard_map/all_to_all | solution.py:96
  132.5 0.0 copy-done.2
  132.5 0.1 rev.3
  132.7 4.0 %select_reduce_fusion = f32[2048,512]{1,0:T(8,128)} fusion(f32[512,2]{0,1:T(2,128)S(1)} %add_divide_fusion, s32[512,2]{0,1:T(2,128)S(1)} %multiply_add_fusion), kind=kLoop, calls=%fused_computation.1 | loop fusion | flops 5242880 | bytes 4202496 | tf_op jit(solution)/shard_map/reduce_sum | solution.py:105
  136.6 0.0 copy-start.4
  136.6 39.3 %all-to-all-done.3 = bf16[256,64,32]{0,2,1:T(8,128)(2,1)S(1)} async-done(((bf16[256,64,32]{0,2,1:T(8,128)(2,1)}), bf16[256,64,32]{0,2,1:T(8,128)(2,1)S(1)}, u32[]{:S(2)}, u32[]{:S(2)}) %all-to-all-start.3) | async-done | bytes 1048608 | tf_op jit(solution)/shard_map/all_to_all | solution.py:96
  175.9 0.2 bitcast_reduce_fusion
  176.1 3.4 %multiply_reduce_fusion = (f32[512]{0:T(512)S(1)}, f32[512,32]{0,1:T(8,128)S(1)}) fusion(f32[2048,512]{1,0:T(8,128)} %select_reduce_fusion, f32[2048,32]{0,1:T(8,128)S(1)} %bitcast.49, bf16[512,32]{0,1:T(8,128)(2,1)S(1)} %reduce_sum.54), kind=kOutput, calls=%fused_computation.31 | convolution fusion | flops 201391616 | bytes 4556800 | tf_op jit(solution)/shard_map/dot_general | solution.py:108
  179.5 0.1 broadcast_in_dim.26
  179.6 24.4 %all_to_all.44 = f32[64,1,512]{2,1,0:T(1,128)S(1)} all-to-all(f32[64,1,512]{2,1,0:T(1,128)S(1)} %broadcast_in_dim.26), channel_id=1, replica_groups=mesh['ey'=1,'ec'=8,'mx'=4,'mz'=16] {'mx','mz'}, dimensions={0} | all-to-all | bytes 262144 | tf_op jit(solution)/shard_map/all_to_all | solution.py:29
  204.0 0.1 reduce_sum.59
  204.1 0.0 copy-done.4
  204.1 0.1 multiply_convert_fusion
  204.2 0.7 broadcast_in_dim.27
  204.9 14.1 %all-to-all-start.5 = ((bf16[8,512,32]{1,2,0:T(8,128)(2,1)}), bf16[8,512,32]{1,2,0:T(8,128)(2,1)S(1)}, u32[]{:S(2)}, u32[]{:S(2)}) async-start(bf16[8,512,32]{1,2,0:T(8,128)(2,1)} %broadcast_in_dim.27), calls=%async_computation.5 | async-start | bytes 524288 | tf_op jit(solution)/shard_map/all_to_all | solution.py:118
  219.1 0.0 copy-done.3
  219.1 6.5 %all-to-all-done.5 = bf16[8,512,32]{1,2,0:T(8,128)(2,1)S(1)} async-done(((bf16[8,512,32]{1,2,0:T(8,128)(2,1)}), bf16[8,512,32]{1,2,0:T(8,128)(2,1)S(1)}, u32[]{:S(2)}, u32[]{:S(2)}) %all-to-all-start.5) | async-done | bytes 262176 | tf_op jit(solution)/shard_map/all_to_all | solution.py:118
  225.6 0.5 copy.65
  226.1 1.3 gather_fusion
  227.4 0.7 copy.66
  (10 shorter events, 0.1 us)
Async XLA Ops:
  6.5 9.0 %copy-start.1 = (s32[512,2]{0,1:T(2,128)S(1)}, s32[512,2]{0,1:T(2,128)}, u32[]{:S(2)}) copy-start(s32[512,2]{0,1:T(2,128)} %param.11) | copy-start | bytes 12292
  6.5 10.2 %copy-start = (bf16[512,32]{0,1:T(8,128)(2,1)S(1)}, bf16[512,32]{0,1:T(8,128)(2,1)}, u32[]{:S(2)}) copy-start(bf16[512,32]{0,1:T(8,128)(2,1)} %param.9) | copy-start | bytes 98308
  6.5 105.1 %all-gather.2.cloned.1.call-start = ((), (), s32[]{:S(2)}) async-start(), calls=%async_computation.6 | async-start | bytes 9732096 | tf_op jit(solution)/shard_map/all_gather | solution.py:77
  10.7 39.1 %all-to-all-start = ((bf16[4,32,2048]{2,1,0:T(8,128)(2,1)}), bf16[4,32,2048]{2,1,0:T(8,128)(2,1)S(1)}, u32[]{:S(2)}, u32[]{:S(2)}) async-start(bf16[4,32,2048]{2,1,0:T(8,128)(2,1)} %broadcast_in_dim.22), calls=%async_computation | async-start | bytes 1048576 | tf_op jit(solution)/shard_map/all_to_all | solution.py:46
  50.8 9.6 %all-to-all-start.1 = ((f32[512,4,32]{0,2,1:T(8,128)}), f32[512,4,32]{0,2,1:T(8,128)S(1)}, u32[]{:S(2)}, u32[]{:S(2)}) async-start(f32[512,4,32]{0,2,1:T(8,128)} %bitcast.2), calls=%async_computation.1 | async-start | bytes 524288 | tf_op jit(solution)/shard_map/all_to_all | solution.py:58
  120.4 12.1 %copy-start.2 = (f32[512,2]{0,1:T(2,128)S(1)}, f32[512,2]{0,1:T(2,128)}, u32[]{:S(2)}) copy-start(f32[512,2]{0,1:T(2,128)} %param.12) | copy-start | bytes 12292
  121.7 54.2 %all-to-all-start.3 = ((bf16[256,64,32]{0,2,1:T(8,128)(2,1)}), bf16[256,64,32]{0,2,1:T(8,128)(2,1)S(1)}, u32[]{:S(2)}, u32[]{:S(2)}) async-start(bf16[256,64,32]{0,2,1:T(8,128)(2,1)} %bitcast.12), calls=%async_computation.3 | async-start | bytes 2097152 | tf_op jit(solution)/shard_map/all_to_all | solution.py:96
  136.6 67.5 %copy-start.4 = (f32[32]{0:T(128)S(1)}, f32[32]{0:T(128)}, u32[]{:S(2)}) copy-start(f32[32]{0:T(128)} %param.16) | copy-start | bytes 388
  136.6 82.4 %copy-start.3 = (s32[512]{0:T(512)S(1)}, s32[512]{0:T(512)}, u32[]{:S(2)}) copy-start(s32[512]{0:T(512)} %param.17) | copy-start | bytes 6148
  204.9 20.6 %all-to-all-start.5 = ((bf16[8,512,32]{1,2,0:T(8,128)(2,1)}), bf16[8,512,32]{1,2,0:T(8,128)(2,1)S(1)}, u32[]{:S(2)}, u32[]{:S(2)}) async-start(bf16[8,512,32]{1,2,0:T(8,128)(2,1)} %broadcast_in_dim.27), calls=%async_computation.5 | async-start | bytes 524288 | tf_op jit(solution)/shard_map/all_to_all | solution.py:118
Sparse Core Ops, SparseCore 0:
  9.5 68.4 all-gather.1

commit v15 on v14

--- a/solution.py
+++ b/solution.py
@@ -75,18 +75,14 @@
     outgoing = slotted.transpose(1, 0, 2).reshape(capacity, mp_count * feat_local)
     inbox_rows = lax.all_to_all(outgoing, MP, split_axis=1, concat_axis=1, tiled=True)
     stacked = lax.all_gather(jnp.stack([w_gate, w_up, w_down]), EX, axis=2, tiled=True)
-    gate_next = jnp.einsum(
-        "rd,hd->rh",
+    both = jnp.einsum(
+        "rd,ghd->rgh",
         inbox_rows,
-        stacked[0],
+        stacked[:2],
         preferred_element_type=jnp.float32,
     )
-    up_next = jnp.einsum(
-        "rd,hd->rh",
-        inbox_rows,
-        stacked[1],
-        preferred_element_type=jnp.float32,
-    )
+    gate_next = both[:, 0]
+    up_next = both[:, 1]
     activated = (jax.nn.silu(gate_next) * up_next).astype(jnp.bfloat16)
     partial_value = jnp.dot(
         activated,

time: 236 us -> 234 us (level)
    dot_general x1, matrix products: 5.97 us -> 2.9 us  [shards(): jnp.dot(activated, stacked[2], preferred_element_type=jnp.float32)]
where the time goes in v15:
time: 234 us
  blocking collectives  108 us (46%)
  waiting for transfers between devices  48.1 us (21%)
  starting transfers between devices  33.8 us (14%)
  between operations  13.6 us (6%)
  matrix products  12.8 us (5%)
  other arithmetic  10 us (4%)
  local copies, waits for them, and re-layouts  7.38 us (3%)
    all_to_all x1, blocking collectives, shards(): lax.all_to_all(outgoing, MP, split_axis=1, concat_axis=1, tiled=True)  50.3 us
    all_to_all x1, waiting for transfers between devices, shards(): lax.all_to_all(partial_value.astype(jnp.bfloat16), MP, split_axis=1, conc...  39.3 us
    all_gather x1, blocking collectives, shards(): along_z = lax.all_gather(context, 'mz', axis=1, tiled=True)  33.1 us
    all_to_all x1, blocking collectives, gather_sum(): return jnp.sum(lax.all_to_all(spread, axis, 0, 0, tiled=True), axis=0)  24.4 us
    all_to_all x1, starting transfers between devices, shards(): lax.all_to_all(jnp.broadcast_to(normed[None], (ex_count,) + normed.shape)...  14.1 us
    all_to_all x1, starting transfers between devices, shards(): lax.all_to_all(partial_value.astype(jnp.bfloat16), MP, split_axis=1, conc...  10.7 us
    all_to_all x1, waiting for transfers between devices, shards(): lax.all_to_all(jnp.broadcast_to(normed[None], (ex_count,) + normed.shape)...  6.48 us
    all_to_all x1, starting transfers between devices, shards(): lax.all_to_all(jnp.broadcast_to(out_proj[None], (x_count,) + out_proj.sha...  4.84 us
  transfers between devices with their start and end apart: 5, of which 3 were waited for; matrix products, arithmetic and copies ran while one was open for 5% of the time, Pallas kernels for 0%

profile of v15, /device:TPU:1, one launch (start us, length us, event | category | flops | bytes accessed | tf_op | source)
XLA Modules:
  0.0 233.5 jit_solution(15177697204085938144)
XLA Ops:
  6.5 0.0 copy-start.1
  6.5 0.0 copy-start
  6.5 0.0 all-gather.2.cloned.1.call-start
  6.5 2.4 %pad_maximum_fusion = bf16[3,704,256]{2,1,0:T(8,128)(2,1)} fusion(bf16[1,704,256]{2,1,0:T(8,128)(2,1)} %bitcast.46, bf16[1,704,256]{2,1,0:T(8,128)(2,1)} %bitcast.47, bf16[1,704,256]{2,1,0:T(8,128)(2,1)} %bitcast.48), kind=kLoop, calls=%fused_computation.16 | loop fusion | flops 1081344 | bytes 2162688 | tf_op jit(solution)/shard_map/stack | solution.py:77
  8.9 0.0 all-gather.2.cloned.1.call-update
  9.0 1.8 broadcast_in_dim.22
  10.7 4.8 %all-to-all-start = ((bf16[4,32,2048]{2,1,0:T(8,128)(2,1)}), bf16[4,32,2048]{2,1,0:T(8,128)(2,1)S(1)}, u32[]{:S(2)}, u32[]{:S(2)}) async-start(bf16[4,32,2048]{2,1,0:T(8,128)(2,1)} %broadcast_in_dim.22), calls=%async_computation | async-start | bytes 1048576 | tf_op jit(solution)/shard_map/all_to_all | solution.py:46
  15.6 0.0 copy-done.1
  15.6 0.1 copy.64
  15.7 0.2 eq.28
  15.9 0.5 fusion.7
  16.4 0.2 convert_element_type.51
  16.6 0.1 copy.65
  16.7 0.0 copy-done
  16.7 33.1 %all_gather.6 = bf16[512,512]{0,1:T(8,128)(2,1)S(1)} all-gather(bf16[512,32]{0,1:T(8,128)(2,1)S(1)} %copy-done), channel_id=1, replica_groups=mesh['ey'=1,'ec'=8,'mx'=4,'mz'=16] {'mz'}, dimensions={1}, use_global_device_ids=true | all-gather | bytes 557056 | tf_op jit(solution)/shard_map/all_gather | solution.py:44
  49.9 0.0 all-to-all-done
  49.9 0.9 fusion.11
  50.8 4.1 %all-to-all-start.1 = ((f32[512,4,32]{0,2,1:T(8,128)}), f32[512,4,32]{0,2,1:T(8,128)S(1)}, u32[]{:S(2)}, u32[]{:S(2)}) async-start(f32[512,4,32]{0,2,1:T(8,128)} %bitcast.2), calls=%async_computation.1 | async-start | bytes 524288 | tf_op jit(solution)/shard_map/all_to_all | solution.py:58
  54.9 3.2 %fusion = pred[2048,512]{1,0:T(8,128)(4,1)S(1)} fusion(s32[512,2]{0,1:T(2,128)S(1)} %multiply_add_fusion), kind=kLoop, calls=%fused_computation.3 | loop fusion | flops 3145728 | bytes 1052672 | tf_op jit(solution)/shard_map/reduce_or | solution.py:70
  58.1 2.3 all-to-all-done.1
  60.5 0.7 convolution_convert_fusion
  61.2 0.1 broadcast_in_dim.25
  61.4 50.3 %all_to_all.43 = bf16[256,64,32]{0,2,1:T(8,128)(2,1)S(1)} all-to-all(bf16[256,64,32]{0,2,1:T(8,128)(2,1)S(1)} %bitcast.40), channel_id=1, replica_groups=mesh['ey'=1,'ec'=8,'mx'=4,'mz'=16] {'mx','mz'}, dimensions={1} | all-to-all | bytes 2097152 | tf_op jit(solution)/shard_map/all_to_all | solution.py:76
  111.7 0.0 all-gather.2.cloned.1.call-done
  111.7 4.3 %fusion.1 = f32[256,2,704]{0,2,1:T(8,128)S(1)} fusion(bf16[256,2048,1]{0,1,2:T(8,128)(2,1)S(1)} %bitcast.43, bf16[3,704,2048]{2,1,0:T(8,128)(2,1)} %all-gather.2.cloned.1.call-done), kind=kOutput, calls=%fused_computation.4 | convolution fusion | flops 1476395008 | bytes 8257536 | tf_op jit(solution)/shard_map/rd,ghd->rgh/dot_general | solution.py:78
  116.0 0.0 copy-start.2
  116.0 2.9 %fusion.5 = bf16[256,2048]{1,0:T(8,128)(2,1)S(1)} fusion(bf16[3,704,2048]{2,1,0:T(8,128)(2,1)} %all-gather.2.cloned.1.call-done, f32[256,2,704]{0,2,1:T(8,128)S(1)} %fusion.1), kind=kOutput, calls=%fused_computation.10 | convolution fusion | flops 739803136 | bytes 5373952 | tf_op jit(solution)/shard_map/dot_general | solution.py:87
  118.9 1.3 copy.68
  120.3 10.7 %all-to-all-start.3 = ((bf16[256,64,32]{0,2,1:T(8,128)(2,1)}), bf16[256,64,32]{0,2,1:T(8,128)(2,1)S(1)}, u32[]{:S(2)}, u32[]{:S(2)}) async-start(bf16[256,64,32]{0,2,1:T(8,128)(2,1)} %bitcast.12), calls=%async_computation.3 | async-start | bytes 2097152 | tf_op jit(solution)/shard_map/all_to_all | solution.py:92
  131.0 0.0 copy-done.2
  131.0 0.1 rev.3
  131.2 4.0 %select_reduce_fusion = f32[2048,512]{1,0:T(8,128)} fusion(f32[512,2]{0,1:T(2,128)S(1)} %add_divide_fusion, s32[512,2]{0,1:T(2,128)S(1)} %multiply_add_fusion), kind=kLoop, calls=%fused_computation.1 | loop fusion | flops 5242880 | bytes 4202496 | tf_op jit(solution)/shard_map/reduce_sum | solution.py:101
  135.2 0.0 copy-start.4
  135.2 39.3 %all-to-all-done.3 = bf16[256,64,32]{0,2,1:T(8,128)(2,1)S(1)} async-done(((bf16[256,64,32]{0,2,1:T(8,128)(2,1)}), bf16[256,64,32]{0,2,1:T(8,128)(2,1)S(1)}, u32[]{:S(2)}, u32[]{:S(2)}) %all-to-all-start.3) | async-done | bytes 1048608 | tf_op jit(solution)/shard_map/all_to_all | solution.py:92
  174.4 0.2 bitcast_reduce_fusion
  174.6 3.4 %multiply_reduce_fusion = (f32[512]{0:T(512)S(1)}, f32[512,32]{0,1:T(8,128)S(1)}) fusion(f32[2048,512]{1,0:T(8,128)} %select_reduce_fusion, f32[2048,32]{0,1:T(8,128)S(1)} %bitcast.41, bf16[512,32]{0,1:T(8,128)(2,1)S(1)} %reduce_sum.54), kind=kOutput, calls=%fused_computation.24 | convolution fusion | flops 201391616 | bytes 4556800 | tf_op jit(solution)/shard_map/dot_general | solution.py:104
  178.0 0.1 broadcast_in_dim.26
  178.1 24.4 %all_to_all.44 = f32[64,1,512]{2,1,0:T(1,128)S(1)} all-to-all(f32[64,1,512]{2,1,0:T(1,128)S(1)} %broadcast_in_dim.26), channel_id=1, replica_groups=mesh['ey'=1,'ec'=8,'mx'=4,'mz'=16] {'mx','mz'}, dimensions={0} | all-to-all | bytes 262144 | tf_op jit(solution)/shard_map/all_to_all | solution.py:29
  202.5 0.1 reduce_sum.59
  202.6 0.0 copy-done.4
  202.6 0.1 multiply_convert_fusion
  202.7 0.7 broadcast_in_dim.27
  203.4 14.1 %all-to-all-start.5 = ((bf16[8,512,32]{1,2,0:T(8,128)(2,1)}), bf16[8,512,32]{1,2,0:T(8,128)(2,1)S(1)}, u32[]{:S(2)}, u32[]{:S(2)}) async-start(bf16[8,512,32]{1,2,0:T(8,128)(2,1)} %broadcast_in_dim.27), calls=%async_computation.5 | async-start | bytes 524288 | tf_op jit(solution)/shard_map/all_to_all | solution.py:114
  217.6 0.0 copy-done.3
  217.6 6.5 %all-to-all-done.5 = bf16[8,512,32]{1,2,0:T(8,128)(2,1)S(1)} async-done(((bf16[8,512,32]{1,2,0:T(8,128)(2,1)}), bf16[8,512,32]{1,2,0:T(8,128)(2,1)S(1)}, u32[]{:S(2)}, u32[]{:S(2)}) %all-to-all-start.5) | async-done | bytes 262176 | tf_op jit(solution)/shard_map/all_to_all | solution.py:114
  224.1 0.5 copy.71
  224.6 1.3 gather_fusion
  226.0 0.7 copy.72
  (10 shorter events, 0.1 us)
Async XLA Ops:
  6.5 9.0 %copy-start.1 = (s32[512,2]{0,1:T(2,128)S(1)}, s32[512,2]{0,1:T(2,128)}, u32[]{:S(2)}) copy-start(s32[512,2]{0,1:T(2,128)} %param.11) | copy-start | bytes 12292
  6.5 10.2 %copy-start = (bf16[512,32]{0,1:T(8,128)(2,1)S(1)}, bf16[512,32]{0,1:T(8,128)(2,1)}, u32[]{:S(2)}) copy-start(bf16[512,32]{0,1:T(8,128)(2,1)} %param.9) | copy-start | bytes 98308
  6.5 105.1 %all-gather.2.cloned.1.call-start = ((), (), s32[]{:S(2)}) async-start(), calls=%async_computation.6 | async-start | bytes 9732096 | tf_op jit(solution)/shard_map/all_gather | solution.py:77
  10.7 39.1 %all-to-all-start = ((bf16[4,32,2048]{2,1,0:T(8,128)(2,1)}), bf16[4,32,2048]{2,1,0:T(8,128)(2,1)S(1)}, u32[]{:S(2)}, u32[]{:S(2)}) async-start(bf16[4,32,2048]{2,1,0:T(8,128)(2,1)} %broadcast_in_dim.22), calls=%async_computation | async-start | bytes 1048576 | tf_op jit(solution)/shard_map/all_to_all | solution.py:46
  50.8 9.6 %all-to-all-start.1 = ((f32[512,4,32]{0,2,1:T(8,128)}), f32[512,4,32]{0,2,1:T(8,128)S(1)}, u32[]{:S(2)}, u32[]{:S(2)}) async-start(f32[512,4,32]{0,2,1:T(8,128)} %bitcast.2), calls=%async_computation.1 | async-start | bytes 524288 | tf_op jit(solution)/shard_map/all_to_all | solution.py:58
  116.0 15.0 %copy-start.2 = (f32[512,2]{0,1:T(2,128)S(1)}, f32[512,2]{0,1:T(2,128)}, u32[]{:S(2)}) copy-start(f32[512,2]{0,1:T(2,128)} %param.12) | copy-start | bytes 12292
  120.3 54.2 %all-to-all-start.3 = ((bf16[256,64,32]{0,2,1:T(8,128)(2,1)}), bf16[256,64,32]{0,2,1:T(8,128)(2,1)S(1)}, u32[]{:S(2)}, u32[]{:S(2)}) async-start(bf16[256,64,32]{0,2,1:T(8,128)(2,1)} %bitcast.12), calls=%async_computation.3 | async-start | bytes 2097152 | tf_op jit(solution)/shard_map/all_to_all | solution.py:92
  135.2 67.5 %copy-start.4 = (f32[32]{0:T(128)S(1)}, f32[32]{0:T(128)}, u32[]{:S(2)}) copy-start(f32[32]{0:T(128)} %param.16) | copy-start | bytes 388
  135.2 82.4 %copy-start.3 = (s32[512]{0:T(512)S(1)}, s32[512]{0:T(512)}, u32[]{:S(2)}) copy-start(s32[512]{0:T(512)} %param.17) | copy-start | bytes 6148
  203.4 20.6 %all-to-all-start.5 = ((bf16[8,512,32]{1,2,0:T(8,128)(2,1)}), bf16[8,512,32]{1,2,0:T(8,128)(2,1)S(1)}, u32[]{:S(2)}, u32[]{:S(2)}) async-start(bf16[8,512,32]{1,2,0:T(8,128)(2,1)} %broadcast_in_dim.27), calls=%async_computation.5 | async-start | bytes 524288 | tf_op jit(solution)/shard_map/all_to_all | solution.py:114
Sparse Core Ops, SparseCore 0:
  9.5 68.4 all-gather.1
